TPU v7x, 128 devices: a whole 4x4x4 slice. The times are simulated.
128 devices in a mesh: row: 8 (over z_lo, y), col: 16 (over x, z_hi, core).
Axes of the slice: x: 4, y: 4, z: 4 (z_hi: 2, z_lo: 2; z = z_hi * 2 + z_lo), core: 2. Of those that a mesh axis runs over, the one named last changes fastest.
Arguments:
- tokens: bfloat16 [2048, 2304], P('row', 'col'), may hold values from -6 to 6
- gate_weight: bfloat16 [8, 2304, 5760], P(None, 'col', 'row'), may hold values from -0.125 to 0.125
- up_weight: bfloat16 [8, 2304, 5760], P(None, 'col', 'row'), may hold values from -0.125 to 0.125
- down_weight: bfloat16 [8, 5760, 2304], P(None, 'row', 'col'), may hold values from -0.078125 to 0.078125
- route_ids: int32 [2048, 2], replicated, may hold values from 0 to 7, all different within a row; in each aligned block of 2048 rows (0 to 2047, 2048 to 4095, ...) at most 1024 rows name the same one
- route_weight: float32 [2048, 2], replicated, may hold values from 0.2 to 1
- prefill_cache: bfloat16 [2, 2048, 16, 2304], P(None, ('row', 'col')), may hold values from -6 to 6
- dest_col: int32 [8, 16, 16], P('row'), may hold values from 0 to 15, as said below
- dest_slot: int32 [8, 16, 16], P('row'), may hold values from 0 to 15, as said below
- pages_used: int32 [8, 16], P('row'), may hold values from 4 to 16, as said below
Outputs:
- mixed: bfloat16 [2048, 2304], P('row', 'col')
- decode_cache: bfloat16 [2, 2048, 16, 2304], P(None, ('row', 'col'))
Inputs may be any that keep to these rules, and one draw needn't show every extreme that they name: `route_ids`: each token names two different experts; no expert is named by more than 1024 tokens, a bound that some block reaches. For every device (r, c), dest_col[r, c, :] names each col index exactly 1 times. For every r and col index c2, the page slots of row r with dest_col = c2 carry distinct dest_slot values, so they fill all 16 slots of device (r, c2). The live slots of a device are its first pages_used slots; some device has all 16 live.
All inputs are finite; a program needn't handle non-finite values.
Results may differ from a plain program's by a relative error of at most 0.03.
Values may be sent and summed in bfloat16 or wider, within the bound.
No kernel may reach another device: no remote copies, remote signals or barrier semaphores. Data moves between devices by JAX's collectives and lax.ppermute only.
A program may use at most 192 MiB of HBM per device.

v0:
```python
import jax
import jax.numpy as jnp
from jax import lax
from jax.sharding import PartitionSpec as P


def aligned_apply(slot_rows, weights):
    experts = weights.shape[0]
    shaped = slot_rows.reshape(experts, -1, slot_rows.shape[1])
    product = jnp.einsum("ecd,edf->ecf", shaped, weights, preferred_element_type=jnp.float32)
    return product.reshape(-1, weights.shape[2])


def move_pages(prefill_cache, dest_col, dest_slot, pages_used):
    col_devices = lax.axis_size("col")
    own_index = lax.axis_index("col")
    slot_count = prefill_cache.shape[1]
    per_peer = slot_count // col_devices
    dest_table = dest_col[0]
    targets = dest_slot[0]
    page_index = jnp.arange(slot_count, dtype=jnp.int32)
    same_dest = dest_table[:, :, None] == dest_table[:, None, :]
    earlier = page_index[None, :] < page_index[:, None]
    dest_rank = jnp.sum((same_dest & earlier[None]).astype(jnp.int32), axis=2)
    send_order = lax.dynamic_index_in_dim(
        dest_table * per_peer + dest_rank, own_index, 0, keepdims=False
    )
    inverse = jnp.zeros((slot_count,), jnp.int32).at[send_order].set(page_index)
    own_used = lax.dynamic_index_in_dim(pages_used[0], own_index, 0, keepdims=False)
    is_live = page_index < own_used
    masked_pages = jnp.where(
        is_live[None, :, None, None], prefill_cache, jnp.zeros((), prefill_cache.dtype)
    )
    received = lax.all_to_all(
        masked_pages[:, inverse], "col", split_axis=1, concat_axis=1, tiled=True
    )
    senders = jnp.arange(col_devices, dtype=jnp.int32)[:, None]
    arrival = jnp.where(dest_table == own_index, senders * per_peer + dest_rank, slot_count)
    slot_of_arrival = (
        jnp.zeros((slot_count + 1,), jnp.int32)
        .at[arrival.reshape(-1)]
        .set(targets.reshape(-1))[:slot_count]
    )
    source_of_slot = jnp.zeros((slot_count,), jnp.int32).at[slot_of_arrival].set(page_index)
    return received[:, source_of_slot]


def shards(
    tokens,
    gate_weight,
    up_weight,
    down_weight,
    route_ids,
    route_weight,
    prefill_cache,
    dest_col,
    dest_slot,
    pages_used,
):
    decode_cache = move_pages(prefill_cache, dest_col, dest_slot, pages_used)
    gathered = lax.all_gather(tokens, "row", axis=0, tiled=True)
    token_count = route_ids.shape[0]
    assignments = token_count * 2
    capacity = token_count // 2
    experts = gate_weight.shape[0]
    flat_expert = route_ids.reshape(-1)
    labels = jnp.arange(experts, dtype=jnp.int32)
    assign_index = jnp.arange(assignments, dtype=jnp.int32)
    paired = jnp.concatenate([gate_weight, up_weight], axis=2)
    onehot = (flat_expert[:, None] == labels[None, :]).astype(jnp.int32)
    position = jnp.sum(jnp.cumsum(onehot, axis=0) * onehot, axis=1) - 1
    slot_of_assign = flat_expert * capacity + position
    row_assign = (
        jnp.full((experts * capacity,), assignments, jnp.int32).at[slot_of_assign].set(assign_index)
    )
    row_token = row_assign // 2
    padded_tokens = jnp.concatenate(
        [gathered, jnp.zeros((1, gathered.shape[1]), gathered.dtype)], axis=0
    )
    slot_rows = padded_tokens[row_token]
    weights_flat = jnp.concatenate([route_weight.reshape(-1), jnp.zeros((1,), jnp.float32)])
    row_weight = weights_flat[row_assign]
    partial_sums = aligned_apply(slot_rows, paired)
    summed = lax.psum_scatter(
        partial_sums.astype(jnp.bfloat16), "col", scatter_dimension=0, tiled=True
    ).astype(jnp.float32)
    share_rows = summed.shape[0]
    hidden_width = gate_weight.shape[2]
    own_weight = lax.dynamic_slice_in_dim(
        row_weight, lax.axis_index("col") * share_rows, share_rows, 0
    )
    hidden = (
        own_weight[:, None] * jax.nn.silu(summed[:, :hidden_width]) * summed[:, hidden_width:]
    ).astype(jnp.bfloat16)
    hidden_all = lax.all_gather(hidden, "col", axis=0, tiled=True)
    down_rows = aligned_apply(hidden_all, down_weight)
    pair_slots = slot_of_assign.reshape(token_count, 2)
    per_token = down_rows[pair_slots[:, 0]] + down_rows[pair_slots[:, 1]]
    mixed = lax.psum_scatter(per_token.astype(jnp.bfloat16), "row", scatter_dimension=0, tiled=True)
    return (mixed, decode_cache)


def solution(mesh):
    in_specs = (
        P("row", "col"),
        P(None, "col", "row"),
        P(None, "col", "row"),
        P(None, "row", "col"),
        P(),
        P(),
        P(None, ("row", "col"), None, None),
        P("row", None, None),
        P("row", None, None),
        P("row", None),
    )
    out_specs = (P("row", "col"), P(None, ("row", "col"), None, None))
    return jax.shard_map(shards, mesh=mesh, in_specs=in_specs, out_specs=out_specs, check_vma=False)
```

profile of v0, /device:TPU:1, one launch (start us, length us, event | category | flops | bytes accessed | tf_op | source)
XLA Modules:
  0.0 514.9 jit_solution(9502357657079924522)
XLA Ops:
  7.2 1.2 copy.43
  9.4 2.3 reduce-window.6
  12.4 2.0 sub.17
  14.4 2.8 fusion.28
  17.2 1.8 mul.40
  19.1 15.5 %scatter_custom_fusion = s32[8192]{0:T(1024)S(1)} fusion(s32[4096]{0:T(1024)S(1)} %bitcast.51, s32[4096]{0:T(1024)S(1)} %iota.35, s32[]{:T(128)} %constant.20.clone.1), kind=kCustom, calls=%fused_computation.48 | custom fusion | bytes 32772 | tf_op jit(solution)/shard_map/scatter | solution.py:74
  34.8 27.4 %all_gather.6 = bf16[2048,144]{1,0:T(8,128)(2,1)S(1)} all-gather(bf16[256,144]{1,0:T(8,128)(2,1)S(1)} %copy.46), channel_id=1, replica_groups=mesh['row'=8,'col'=16] {'row'}, dimensions={0}, use_global_device_ids=true | all-gather | bytes 663552 | tf_op jit(solution)/shard_map/all_gather | solution.py:61
  62.4 32.9 %gather_fusion.1 = bf16[8192,144]{1,0:T(8,128)(2,1)} fusion(bf16[2049,144]{1,0:T(8,128)(2,1)S(1)} %concatenate.10, s32[8192]{0:T(1024)S(1)} %get-tuple-element.15), kind=kCustom, calls=%fused_computation.1 | custom fusion | bytes 4751360 | tf_op jit(solution)/shard_map/gather | solution.py:80
  95.3 15.6 %convert_bitcast_fusion = bf16[8,180,8,1024]{3,2,1,0:T(8,128)(2,1)} fusion(bf16[8,1024,144]{2,1,0:T(8,128)(2,1)} %bitcast.44, bf16[8,144,720]{2,1,0:T(8,128)(2,1)} %param.12, bf16[8,144,720]{2,1,0:T(8,128)(2,1)} %param.11), kind=kOutput, calls=%fused_computation.10 | convolution fusion | flops 3415818240 | bytes 29270016 | tf_op jit(solution)/shard_map/ecd,edf->ecf/dot_general | solution.py:10
  110.9 20.1 %copy.60 = bf16[8,180,8,1024]{3,2,0,1:T(8,128)(2,1)} copy(bf16[8,180,8,1024]{3,2,1,0:T(8,128)(2,1)} %convert_bitcast_fusion) | data formatting | bytes 47185920 | tf_op jit(solution)/shard_map/convert_element_type | solution.py:85
  131.0 0.6 copy-done.4
  132.5 45.5 %gather_fusion = f32[8192]{0:T(1024)S(1)} fusion(f32[4097]{0:T(1024)S(1)} %pad_maximum_fusion, s32[8192]{0:T(1024)S(1)} %get-tuple-element.14), kind=kCustom, calls=%fused_computation | custom fusion | bytes 98304 | tf_op jit(solution)/shard_map/gather | solution.py:82
  178.2 139.8 %reduce-scatter.3.cloned.1.call-done = bf16[512,1440]{0,1:T(8,128)(2,1)} async-done(((bf16[8192,1440]{0,1:T(8,128)(2,1)}), bf16[512,1440]{0,1:T(8,128)(2,1)}) %reduce-scatter.3.cloned.1.call-update) | async-done | bytes 1474576 | tf_op jit(solution)/shard_map/reduce_scatter | solution.py:84
  318.0 1.8 convert_element_type.26
  319.8 1.4 fusion.6
  322.5 0.6 scatter_custom_fusion.1
  323.2 1.6 scatter_custom_fusion.2
  324.8 0.7 iota_compare_fusion.3
  325.5 3.3 broadcast_select_fusion
  328.7 4.0 gather_fusion.4
  332.7 5.7 %all-to-all-start = ((bf16[2,16,16,2304]{3,2,0,1:T(8,128)(2,1)}), bf16[2,16,16,2304]{3,2,0,1:T(8,128)(2,1)}, u32[]{:S(2)}, u32[]{:S(2)}) async-start(bf16[2,16,16,2304]{3,2,0,1:T(8,128)(2,1)} %bitcast.45), calls=%async_computation.2 | async-start | bytes 4718592 | tf_op jit(solution)/shard_map/all_to_all | solution.py:34
  338.5 0.9 fusion.8
  339.4 96.2 %all-gather.2.cloned.1.call-done = bf16[8192,720]{0,1:T(8,128)(2,1)} async-done(((bf16[512,720]{0,1:T(8,128)(2,1)}), bf16[8192,720]{0,1:T(8,128)(2,1)}) %all-gather.2.cloned.1.call-update) | async-done | bytes 11796496 | tf_op jit(solution)/shard_map/all_gather | solution.py:95
  435.6 11.5 %fusion = f32[8,1024,144]{2,1,0:T(8,128)} fusion(bf16[8,720,144]{1,2,0:T(8,128)(2,1)S(1)} %copy-done, bf16[90,8,8,1024]{3,2,1,0:T(8,128)(2,1)} %bitcast.53), kind=kOutput, calls=%fused_computation.11 | convolution fusion | flops 1698693120 | bytes 18173952 | tf_op jit(solution)/shard_map/reshape | solution.py:11
  447.1 11.9 %gather_fusion.3 = f32[2048,144]{1,0:T(8,128)} fusion(f32[8192,144]{1,0:T(8,128)} %bitcast.41, s32[2048]{0:T(1024)S(1)} %get-tuple-element.18), kind=kCustom, calls=%fused_computation.3 | custom fusion | bytes 2367488 | tf_op jit(solution)/shard_map/gather | solution.py:98
  459.1 12.0 %gather_fusion.2 = f32[2048,144]{1,0:T(8,128)} fusion(f32[8192,144]{1,0:T(8,128)} %bitcast.42, s32[2048]{0:T(1024)S(1)} %get-tuple-element.19), kind=kCustom, calls=%fused_computation.2 | custom fusion | bytes 2367488 | tf_op jit(solution)/shard_map/gather | solution.py:98
  471.1 3.4 add_convert_fusion
  475.2 3.2 copy.53
  478.4 3.8 gather_fusion.5
  482.2 3.2 copy.55
  485.4 21.3 %reduce-scatter.5.cloned.1.call-done = bf16[256,144]{1,0:T(8,128)(2,1)} async-done(((bf16[2048,144]{1,0:T(8,128)(2,1)}), bf16[256,144]{1,0:T(8,128)(2,1)}) %reduce-scatter.5.cloned.1.call-update) | async-done | bytes 73744 | tf_op jit(solution)/shard_map/reduce_scatter | solution.py:99
  506.7 1.6 copy.54
  (55 shorter events, 5.1 us)
Async XLA Ops:
  7.2 428.5 %copy-start = (bf16[8,720,144]{1,2,0:T(8,128)(2,1)S(1)}, bf16[8,720,144]{1,2,0:T(8,128)(2,1)}, u32[]{:S(2)}) copy-start(bf16[8,720,144]{1,2,0:T(8,128)(2,1)} %param.13) | copy-start | bytes 4976644
  7.2 310.8 %reduce-scatter.3.cloned.1.call-start = ((), (), s32[]{:S(2)}) async-start(), calls=%async_computation.3 | async-start | bytes 25067520 | tf_op jit(solution)/shard_map/reduce_scatter | solution.py:84
  14.4 20.3 %copy-start.3 = (bf16[256,144]{0,1:T(8,128)(2,1)S(1)}, bf16[256,144]{0,1:T(8,128)(2,1)}, u32[]{:S(2)}) copy-start(bf16[256,144]{0,1:T(8,128)(2,1)} %param.10) | copy-start | bytes 221188
  131.0 0.7 copy-start.4
  131.0 304.6 %all-gather.2.cloned.1.call-start = ((), (), s32[]{:S(2)}) async-start(), calls=%async_computation.4 | async-start | bytes 12533760 | tf_op jit(solution)/shard_map/all_gather | solution.py:95
  319.8 1.4 copy-start.2
  319.8 2.1 copy-start.5
  319.8 2.1 copy-start.6
  332.7 5.7 %copy-start.1 = (s32[2048,2]{1,0:T(8,128)S(1)}, s32[2048,2]{1,0:T(8,128)}, u32[]{:S(2)}) copy-start(s32[2048,2]{1,0:T(8,128)} %get-tuple-element.12) | copy-start | bytes 49156
  332.7 142.4 %all-to-all-start = ((bf16[2,16,16,2304]{3,2,0,1:T(8,128)(2,1)}), bf16[2,16,16,2304]{3,2,0,1:T(8,128)(2,1)}, u32[]{:S(2)}, u32[]{:S(2)}) async-start(bf16[2,16,16,2304]{3,2,0,1:T(8,128)(2,1)} %bitcast.45), calls=%async_computation.2 | async-start | bytes 4718592 | tf_op jit(solution)/shard_map/all_to_all | solution.py:34
  338.4 168.3 %reduce-scatter.5.cloned.1.call-start = ((), (), s32[]{:S(2)}) async-start(), calls=%async_computation.5 | async-start | bytes 1179648 | tf_op jit(solution)/shard_map/reduce_scatter | solution.py:99
Sparse Core Ops, SparseCore 0:
  131.1 186.8 reduce-scatter.2
  321.3 114.2 all-gather.1
  474.6 32.0 reduce-scatter.4
where the time goes:
time: 520 us; the launch traced here: 515 us
  waiting for transfers between devices  257 us (49%)
  local copies, waits for them, and re-layouts  166 us (32%)
  blocking collectives  27.4 us (5%)
  matrix products  27.1 us (5%)
  other arithmetic  17.4 us (3%)
  between operations  14.1 us (3%)
  starting transfers between devices  5.8 us (1%)
    reduce_scatter x1, waiting for transfers between devices, shards(): lax.psum_scatter(partial_sums.astype(jnp.bfloat16), 'col', scatter_dimens...  140 us
    all_gather x1, waiting for transfers between devices, shards(): hidden_all = lax.all_gather(hidden, 'col', axis=0, tiled=True)  96.2 us
    gather x1, local copies, waits for them, and re-layouts, shards(): row_weight = weights_flat[row_assign]  45.5 us
    gather x1, local copies, waits for them, and re-layouts, shards(): slot_rows = padded_tokens[row_token]  32.9 us
    all_gather x1, blocking collectives, shards(): gathered = lax.all_gather(tokens, 'row', axis=0, tiled=True)  27.4 us
    gather x2, local copies, waits for them, and re-layouts, shards(): per_token = down_rows[pair_slots[:, 0]] + down_rows[pair_slots[:, 1]]  23.9 us
    reduce_scatter x1, waiting for transfers between devices, shards(): lax.psum_scatter(per_token.astype(jnp.bfloat16), 'row', scatter_dimension...  21.3 us
    convert_element_type x1, local copies, waits for them, and re-layouts, shards(): partial_sums.astype(jnp.bfloat16)  20.1 us
  transfers between devices with their start and end apart: 4, of which 3 were waited for; matrix products, arithmetic and copies ran while one was open for 21% of the time, Pallas kernels for 0%

commit v1 on v0

--- a/solution.py
+++ b/solution.py
@@ -2,13 +2,6 @@
 import jax.numpy as jnp
 from jax import lax
 from jax.sharding import PartitionSpec as P
-
-
-def aligned_apply(slot_rows, weights):
-    experts = weights.shape[0]
-    shaped = slot_rows.reshape(experts, -1, slot_rows.shape[1])
-    product = jnp.einsum("ecd,edf->ecf", shaped, weights, preferred_element_type=jnp.float32)
-    return product.reshape(-1, weights.shape[2])
 
 
 def move_pages(prefill_cache, dest_col, dest_slot, pages_used):
@@ -59,43 +52,35 @@
 ):
     decode_cache = move_pages(prefill_cache, dest_col, dest_slot, pages_used)
     gathered = lax.all_gather(tokens, "row", axis=0, tiled=True)
-    token_count = route_ids.shape[0]
-    assignments = token_count * 2
-    capacity = token_count // 2
+    token_count, width = gathered.shape
     experts = gate_weight.shape[0]
-    flat_expert = route_ids.reshape(-1)
+    hidden_width = gate_weight.shape[2]
     labels = jnp.arange(experts, dtype=jnp.int32)
-    assign_index = jnp.arange(assignments, dtype=jnp.int32)
-    paired = jnp.concatenate([gate_weight, up_weight], axis=2)
-    onehot = (flat_expert[:, None] == labels[None, :]).astype(jnp.int32)
-    position = jnp.sum(jnp.cumsum(onehot, axis=0) * onehot, axis=1) - 1
-    slot_of_assign = flat_expert * capacity + position
-    row_assign = (
-        jnp.full((experts * capacity,), assignments, jnp.int32).at[slot_of_assign].set(assign_index)
+    onehot = route_ids[:, :, None] == labels[None, None, :]
+    expanded = jnp.where(
+        onehot[:, :, :, None], gathered[:, None, None, :], jnp.zeros((), gathered.dtype)
+    ).reshape(token_count * 2, experts * width)
+    paired = jnp.concatenate([gate_weight, up_weight], axis=2).reshape(
+        experts * width, 2 * hidden_width
     )
-    row_token = row_assign // 2
-    padded_tokens = jnp.concatenate(
-        [gathered, jnp.zeros((1, gathered.shape[1]), gathered.dtype)], axis=0
-    )
-    slot_rows = padded_tokens[row_token]
-    weights_flat = jnp.concatenate([route_weight.reshape(-1), jnp.zeros((1,), jnp.float32)])
-    row_weight = weights_flat[row_assign]
-    partial_sums = aligned_apply(slot_rows, paired)
+    partial_sums = jnp.dot(expanded, paired, preferred_element_type=jnp.float32)
     summed = lax.psum_scatter(
         partial_sums.astype(jnp.bfloat16), "col", scatter_dimension=0, tiled=True
     ).astype(jnp.float32)
     share_rows = summed.shape[0]
-    hidden_width = gate_weight.shape[2]
     own_weight = lax.dynamic_slice_in_dim(
-        row_weight, lax.axis_index("col") * share_rows, share_rows, 0
+        route_weight.reshape(-1), lax.axis_index("col") * share_rows, share_rows, 0
     )
     hidden = (
         own_weight[:, None] * jax.nn.silu(summed[:, :hidden_width]) * summed[:, hidden_width:]
     ).astype(jnp.bfloat16)
-    hidden_all = lax.all_gather(hidden, "col", axis=0, tiled=True)
-    down_rows = aligned_apply(hidden_all, down_weight)
-    pair_slots = slot_of_assign.reshape(token_count, 2)
-    per_token = down_rows[pair_slots[:, 0]] + down_rows[pair_slots[:, 1]]
+    hidden_all = lax.all_gather(hidden, "col", axis=0, tiled=True).reshape(
+        token_count, 2, 1, hidden_width
+    )
+    picked = jnp.where(onehot[:, :, :, None], hidden_all, jnp.zeros((), hidden_all.dtype))
+    by_expert = jnp.sum(picked, axis=1).reshape(token_count, experts * hidden_width)
+    down_flat = down_weight.reshape(experts * hidden_width, down_weight.shape[2])
+    per_token = jnp.dot(by_expert, down_flat, preferred_element_type=jnp.float32)
     mixed = lax.psum_scatter(per_token.astype(jnp.bfloat16), "row", scatter_dimension=0, tiled=True)
     return (mixed, decode_cache)
 

time: 520 us -> 434 us (0.83)
  local copies, waits for them, and re-layouts: 166 us -> 85.9 us
  waiting for transfers between devices: 257 us -> 208 us
  other arithmetic: 17.4 us -> 54.6 us
  matrix products: 27.1 us -> 33.9 us
    gather x4 -> x0, local copies, waits for them, and re-layouts: 102 us -> none  [the longest x1 45.5 us: shards(): row_weight = weights_flat[row_assign]]
    all_gather x1, waiting for transfers between devices: 96.2 us -> 62.9 us  [shards(): lax.all_gather(hidden, 'col', axis=0, tiled=True)]
    reduce_sum x1, other arithmetic: 0.11 us -> 32.7 us  [shards(): jnp.sum(picked, axis=1).reshape(token_count, experts * hidden_width)]
    broadcast_in_dim x0 -> x2, local copies, waits for them, and re-layouts: none -> 29.4 us  [shards(): jnp.where(onehot[:, :, :, None], hidden_all, jnp.zeros((), hidden_all.dty...]
    select_n x0 -> x1, local copies, waits for them, and re-layouts: none -> 25.4 us  [shards(): jnp.where(onehot[:, :, :, None], gathered[:, None, None, :], jnp.zeros(()...]
    convert_element_type x1 -> x0, local copies, waits for them, and re-layouts: 20.1 us -> none  [shards(): partial_sums.astype(jnp.bfloat16)]
    dot_general x1 -> x2, matrix products: 15.6 us -> 33.9 us  [the longest x1 21.7 us: shards(): partial_sums = jnp.dot(expanded, paired, preferred_element_type=jnp.float32)]
    reduce_scatter x1, waiting for transfers between devices: 140 us -> 123 us  [shards(): lax.psum_scatter(partial_sums.astype(jnp.bfloat16), 'col', scatter_dimens...]
  transfers between devices with their start and end apart: 4 -> 4, of which waited for: 3 -> 3; matrix products, arithmetic and copies ran while one was open for 21% -> 25% of each run, Pallas kernels for 0% -> 0%
where the time goes in v1:
time: 434 us; the launch traced here: 428 us
  waiting for transfers between devices  208 us (48%)
  local copies, waits for them, and re-layouts  85.9 us (20%)
  other arithmetic  54.6 us (13%)
  matrix products  33.9 us (8%)
  blocking collectives  25.2 us (6%)
  between operations  14 us (3%)
  starting transfers between devices  6.27 us (1%)
    reduce_scatter x1, waiting for transfers between devices, shards(): lax.psum_scatter(partial_sums.astype(jnp.bfloat16), 'col', scatter_dimens...  123 us
    all_gather x1, waiting for transfers between devices, shards(): lax.all_gather(hidden, 'col', axis=0, tiled=True)  62.9 us
    reduce_sum x1, other arithmetic, shards(): jnp.sum(picked, axis=1).reshape(token_count, experts * hidden_width)  32.7 us
    broadcast_in_dim x2, local copies, waits for them, and re-layouts, shards(): jnp.where(onehot[:, :, :, None], hidden_all, jnp.zeros((), hidden_all.dty...  29.4 us
    select_n x1, local copies, waits for them, and re-layouts, shards(): jnp.where(onehot[:, :, :, None], gathered[:, None, None, :], jnp.zeros(()...  25.4 us
    all_gather x1, blocking collectives, shards(): gathered = lax.all_gather(tokens, 'row', axis=0, tiled=True)  25.2 us
    reduce_scatter x1, waiting for transfers between devices, shards(): lax.psum_scatter(per_token.astype(jnp.bfloat16), 'row', scatter_dimension...  22.2 us
    dot_general x1, matrix products, shards(): partial_sums = jnp.dot(expanded, paired, preferred_element_type=jnp.float32)  21.7 us
  transfers between devices with their start and end apart: 4, of which 3 were waited for; matrix products, arithmetic and copies ran while one was open for 25% of the time, Pallas kernels for 0%

profile of v1, /device:TPU:1, one launch (start us, length us, event | category | flops | bytes accessed | tf_op | source)
XLA Modules:
  0.0 427.6 jit_solution(1592344005975928051)
XLA Ops:
  7.2 0.9 iota_compare_fusion
  8.1 0.6 copy-done.2
  8.7 1.8 copy.27
  10.5 25.2 %all_gather.6 = bf16[2048,144]{0,1:T(8,128)(2,1)S(1)} all-gather(bf16[256,144]{0,1:T(8,128)(2,1)} %param.10), channel_id=1, replica_groups=mesh['row'=8,'col'=16] {'row'}, dimensions={0}, use_global_device_ids=true | all-gather | bytes 663552 | tf_op jit(solution)/shard_map/all_gather | solution.py:54
  35.7 1.3 copy.28
  37.0 9.9 %broadcast_select_fusion = bf16[2048,2,8,144]{3,2,1,0:T(8,128)(2,1)} fusion(pred[2048,2,8]{2,1,0:T(4,128)(4,1)S(1)} %copy.27, bf16[2048,144]{1,0:T(8,128)(2,1)} %copy.28), kind=kLoop, calls=%fused_computation.6 | loop fusion | flops 4718592 | bytes 10059776 | tf_op jit(solution)/shard_map/jit(_where)/select_n | solution.py:60
  46.9 25.4 %select_n.74 = bf16[4096,1152]{1,0:T(8,128)(2,1)} reshape(bf16[2048,2,8,144]{3,2,1,0:T(8,128)(2,1)} %broadcast_select_fusion) | data formatting | bytes 18874368 | tf_op jit(solution)/shard_map/jit(_where)/select_n | solution.py:60
  72.3 4.5 %pad_maximum_fusion = bf16[8,144,1440]{2,1,0:T(8,128)(2,1)} fusion(bf16[8,144,720]{2,1,0:T(8,128)(2,1)S(1)} %copy-done.1, bf16[8,144,720]{2,1,0:T(8,128)(2,1)} %param.11), kind=kLoop, calls=%fused_computation.8 | loop fusion | flops 6635520 | bytes 6635520 | tf_op jit(solution)/shard_map/concatenate | solution.py:63
  76.8 21.7 %convolution_convert_fusion = bf16[4096,1440]{0,1:T(8,128)(2,1)} fusion(bf16[4096,1152]{1,0:T(8,128)(2,1)} %select_n.74, bf16[1152,1440]{1,0:T(8,128)(2,1)} %bitcast.26), kind=kOutput, calls=%fused_computation.7 | convolution fusion | flops 13595443200 | bytes 24551424 | tf_op jit(solution)/shard_map/dot_general | solution.py:66
  99.6 0.5 reshape.127
  100.1 122.6 %reduce-scatter.3.cloned.1.call-done = bf16[256,1440]{0,1:T(8,128)(2,1)} async-done(((bf16[4096,1440]{0,1:T(8,128)(2,1)}), bf16[256,1440]{0,1:T(8,128)(2,1)}) %reduce-scatter.3.cloned.1.call-update) | async-done | bytes 737296 | tf_op jit(solution)/shard_map/reduce_scatter | solution.py:67
  222.8 1.2 convert_element_type.18
  224.0 1.0 fusion.1
  225.1 0.4 convert_reduce_fusion
  225.7 0.6 constant_dynamic-slice_fusion.2
  226.3 1.4 scatter_custom_fusion.1
  227.8 0.6 scatter_custom_fusion
  228.4 0.7 iota_compare_fusion.2
  229.1 3.3 broadcast_select_fusion.1
  232.4 3.8 gather_fusion
  236.1 6.0 %all-to-all-start = ((bf16[2,16,16,2304]{3,2,0,1:T(8,128)(2,1)}), bf16[2,16,16,2304]{3,2,0,1:T(8,128)(2,1)}, u32[]{:S(2)}, u32[]{:S(2)}) async-start(bf16[2,16,16,2304]{3,2,0,1:T(8,128)(2,1)} %bitcast.24), calls=%async_computation.2 | async-start | bytes 4718592 | tf_op jit(solution)/shard_map/all_to_all | solution.py:27
  242.2 62.9 %all-gather.2.cloned.1.call-done = bf16[4096,720]{0,1:T(8,128)(2,1)} async-done(((bf16[256,720]{0,1:T(8,128)(2,1)}), bf16[4096,720]{0,1:T(8,128)(2,1)}) %all-gather.2.cloned.1.call-update) | async-done | bytes 5898256 | tf_op jit(solution)/shard_map/all_gather | solution.py:77
  305.1 8.5 %copy.29 = bf16[4096,720]{1,0:T(8,128)(2,1)} copy(bf16[4096,720]{0,1:T(8,128)(2,1)} %all-gather.2.cloned.1.call-done) | data formatting | bytes 11796480 | tf_op jit(solution)/shard_map/all_gather | solution.py:77
  313.6 13.2 %broadcast_in_dim.84 = bf16[2048,2,720]{2,1,0:T(2,128)(2,1)} reshape(bf16[4096,720]{1,0:T(8,128)(2,1)} %copy.29) | data formatting | bytes 11796480 | tf_op jit(solution)/shard_map/jit(_where)/broadcast_in_dim | solution.py:80
  326.9 16.1 %copy.30 = bf16[2048,2,720]{0,2,1:T(8,128)(2,1)} copy(bf16[2048,2,720]{2,1,0:T(2,128)(2,1)} %broadcast_in_dim.84) | data formatting | bytes 11796480 | tf_op jit(solution)/shard_map/jit(_where)/broadcast_in_dim | solution.py:80
  343.0 32.7 %select_reduce_fusion = bf16[2048,8,720]{0,2,1:T(8,128)(2,1)} fusion(pred[2048,2,8]{0,2,1:T(8,128)(4,1)S(1)} %copy-done.3, bf16[2048,2,720]{0,2,1:T(8,128)(2,1)} %copy.30), kind=kLoop, calls=%fused_computation.5 | loop fusion | flops 35389440 | bytes 29523968 | tf_op jit(solution)/shard_map/reduce_sum | solution.py:81
  375.7 12.2 %fusion = bf16[2048,144]{0,1:T(8,128)(2,1)} fusion(bf16[8,720,144]{1,2,0:T(8,128)(2,1)S(1)} %copy-done, bf16[2048,8,720]{0,2,1:T(8,128)(2,1)} %select_reduce_fusion), kind=kOutput, calls=%fused_computation.10 | convolution fusion | flops 3397681152 | bytes 25841664 | tf_op jit(solution)/shard_map/dot_general | solution.py:83
  387.9 0.6 scatter_custom_fusion.2
  388.6 3.2 copy.31
  391.8 3.8 gather_fusion.1
  395.6 3.3 copy.32
  398.9 22.2 %reduce-scatter.5.cloned.1.call-done = bf16[256,144]{0,1:T(8,128)(2,1)} async-done(((bf16[2048,144]{0,1:T(8,128)(2,1)}), bf16[256,144]{0,1:T(8,128)(2,1)}) %reduce-scatter.5.cloned.1.call-update) | async-done | bytes 73744 | tf_op jit(solution)/shard_map/reduce_scatter | solution.py:84
  (38 shorter events, 1.6 us)
Async XLA Ops:
  7.2 368.5 %copy-start = (bf16[8,720,144]{1,2,0:T(8,128)(2,1)S(1)}, bf16[8,720,144]{1,2,0:T(8,128)(2,1)}, u32[]{:S(2)}) copy-start(bf16[8,720,144]{1,2,0:T(8,128)(2,1)} %param.13) | copy-start | bytes 4976644
  7.2 215.6 %reduce-scatter.3.cloned.1.call-start = ((), (), s32[]{:S(2)}) async-start(), calls=%async_computation.3 | async-start | bytes 12533760 | tf_op jit(solution)/shard_map/reduce_scatter | solution.py:67
  8.1 0.6 copy-start.2
  46.9 25.4 %copy-start.1 = (bf16[8,144,720]{2,1,0:T(8,128)(2,1)S(1)}, bf16[8,144,720]{2,1,0:T(8,128)(2,1)}, u32[]{:S(2)}) copy-start(bf16[8,144,720]{2,1,0:T(8,128)(2,1)} %param.12) | copy-start | bytes 4976644
  98.5 0.7 copy-start.5
  98.5 126.5 %copy-start.4 = (s32[1,16,16]{2,1,0:T(8,128)S(1)}, s32[1,16,16]{2,1,0:T(8,128)}, u32[]{:S(2)}) copy-start(s32[1,16,16]{2,1,0:T(8,128)} %param.17) | copy-start | bytes 3076
  98.5 127.1 %copy-start.6 = (s32[1,16,16]{2,1,0:T(8,128)S(1)}, s32[1,16,16]{2,1,0:T(8,128)}, u32[]{:S(2)}) copy-start(s32[1,16,16]{2,1,0:T(8,128)} %param.18) | copy-start | bytes 3076
  98.6 127.2 %copy-start.7 = (s32[1,16]{1,0:T(1,128)S(1)}, s32[1,16]{1,0:T(1,128)}, u32[]{:S(2)}) copy-start(s32[1,16]{1,0:T(1,128)} %param.19) | copy-start | bytes 196
  98.6 206.5 %all-gather.2.cloned.1.call-start = ((), (), s32[]{:S(2)}) async-start(), calls=%async_computation.4 | async-start | bytes 6266880 | tf_op jit(solution)/shard_map/all_gather | solution.py:77
  236.1 152.4 %all-to-all-start = ((bf16[2,16,16,2304]{3,2,0,1:T(8,128)(2,1)}), bf16[2,16,16,2304]{3,2,0,1:T(8,128)(2,1)}, u32[]{:S(2)}, u32[]{:S(2)}) async-start(bf16[2,16,16,2304]{3,2,0,1:T(8,128)(2,1)} %bitcast.24), calls=%async_computation.2 | async-start | bytes 4718592 | tf_op jit(solution)/shard_map/all_to_all | solution.py:27
  242.1 179.0 %reduce-scatter.5.cloned.1.call-start = ((), (), s32[]{:S(2)}) async-start(), calls=%async_computation.5 | async-start | bytes 663552 | tf_op jit(solution)/shard_map/reduce_scatter | solution.py:84
  326.9 16.1 %copy-start.3 = (pred[2048,2,8]{0,2,1:T(8,128)(4,1)S(1)}, pred[2048,2,8]{0,2,1:T(8,128)(4,1)}, u32[]{:S(2)}) copy-start(pred[2048,2,8]{0,2,1:T(8,128)(4,1)} %copy-done.2) | copy-start | bytes 98308
Sparse Core Ops, SparseCore 0:
  98.6 124.0 reduce-scatter.2
  225.1 79.9 all-gather.1
  388.0 32.9 reduce-scatter.4

commit v2 on v1

--- a/solution.py
+++ b/solution.py
@@ -2,6 +2,7 @@
 import jax.numpy as jnp
 from jax import lax
 from jax.sharding import PartitionSpec as P
+from jax.experimental import pallas as pl
 
 
 def move_pages(prefill_cache, dest_col, dest_slot, pages_used):
@@ -38,6 +39,72 @@
     return received[:, source_of_slot]
 
 
+def gate_up_kernel(ids_ref, x_ref, g_ref, u_ref, go_ref, uo_ref):
+    x = x_ref[...]
+    ids = ids_ref[...]
+    zero = jnp.zeros_like(x)
+    rows = x.shape[0]
+    width = g_ref.shape[2]
+    acc_g = jnp.zeros((2 * rows, width), jnp.float32)
+    acc_u = jnp.zeros((2 * rows, width), jnp.float32)
+    for e in range(g_ref.shape[0]):
+        lhs = jnp.concatenate(
+            [jnp.where(ids[:, 0:1] == e, x, zero), jnp.where(ids[:, 1:2] == e, x, zero)], axis=0
+        )
+        acc_g = acc_g + jnp.dot(lhs, g_ref[e], preferred_element_type=jnp.float32)
+        acc_u = acc_u + jnp.dot(lhs, u_ref[e], preferred_element_type=jnp.float32)
+    go_ref[...] = acc_g.astype(go_ref.dtype).reshape(go_ref.shape)
+    uo_ref[...] = acc_u.astype(uo_ref.dtype).reshape(uo_ref.shape)
+
+
+def down_kernel(ids_ref, h_ref, d_ref, o_ref):
+    ids = ids_ref[...]
+    first = h_ref[0]
+    second = h_ref[1]
+    zero = jnp.zeros_like(first)
+    acc = jnp.zeros(o_ref.shape, jnp.float32)
+    for e in range(d_ref.shape[0]):
+        lhs = jnp.where(ids[:, 0:1] == e, first, jnp.where(ids[:, 1:2] == e, second, zero))
+        acc = acc + jnp.dot(lhs, d_ref[e], preferred_element_type=jnp.float32)
+    o_ref[...] = acc.astype(o_ref.dtype)
+
+
+def gate_up(route_ids, gathered, gate_weight, up_weight, tile):
+    token_count, width = gathered.shape
+    experts, _, hidden_width = gate_weight.shape
+    out = jax.ShapeDtypeStruct((2, token_count, hidden_width), jnp.bfloat16)
+    weight_spec = pl.BlockSpec((experts, width, hidden_width), lambda i: (0, 0, 0))
+    out_spec = pl.BlockSpec((2, tile, hidden_width), lambda i: (0, i, 0))
+    return pl.pallas_call(
+        gate_up_kernel,
+        grid=(token_count // tile,),
+        in_specs=[
+            pl.BlockSpec((tile, 2), lambda i: (i, 0)),
+            pl.BlockSpec((tile, width), lambda i: (i, 0)),
+            weight_spec,
+            weight_spec,
+        ],
+        out_specs=[out_spec, out_spec],
+        out_shape=[out, out],
+    )(route_ids, gathered, gate_weight, up_weight)
+
+
+def down(route_ids, hidden_all, down_weight, tile):
+    _, token_count, hidden_width = hidden_all.shape
+    experts, _, width = down_weight.shape
+    return pl.pallas_call(
+        down_kernel,
+        grid=(token_count // tile,),
+        in_specs=[
+            pl.BlockSpec((tile, 2), lambda i: (i, 0)),
+            pl.BlockSpec((2, tile, hidden_width), lambda i: (0, i, 0)),
+            pl.BlockSpec((experts, hidden_width, width), lambda i: (0, 0, 0)),
+        ],
+        out_specs=pl.BlockSpec((tile, width), lambda i: (i, 0)),
+        out_shape=jax.ShapeDtypeStruct((token_count, width), jnp.bfloat16),
+    )(route_ids, hidden_all, down_weight)
+
+
 def shards(
     tokens,
     gate_weight,
@@ -52,36 +119,25 @@
 ):
     decode_cache = move_pages(prefill_cache, dest_col, dest_slot, pages_used)
     gathered = lax.all_gather(tokens, "row", axis=0, tiled=True)
-    token_count, width = gathered.shape
-    experts = gate_weight.shape[0]
+    token_count = gathered.shape[0]
     hidden_width = gate_weight.shape[2]
-    labels = jnp.arange(experts, dtype=jnp.int32)
-    onehot = route_ids[:, :, None] == labels[None, None, :]
-    expanded = jnp.where(
-        onehot[:, :, :, None], gathered[:, None, None, :], jnp.zeros((), gathered.dtype)
-    ).reshape(token_count * 2, experts * width)
-    paired = jnp.concatenate([gate_weight, up_weight], axis=2).reshape(
-        experts * width, 2 * hidden_width
+    gate_part, up_part = gate_up(route_ids, gathered, gate_weight, up_weight, 256)
+    gate_sum = lax.psum_scatter(
+        gate_part.reshape(2 * token_count, hidden_width), "col", scatter_dimension=0, tiled=True
+    ).astype(jnp.float32)
+    up_sum = lax.psum_scatter(
+        up_part.reshape(2 * token_count, hidden_width), "col", scatter_dimension=0, tiled=True
+    ).astype(jnp.float32)
+    share_rows = gate_sum.shape[0]
+    own_weight = lax.dynamic_slice_in_dim(
+        route_weight.T.reshape(-1), lax.axis_index("col") * share_rows, share_rows, 0
     )
-    partial_sums = jnp.dot(expanded, paired, preferred_element_type=jnp.float32)
-    summed = lax.psum_scatter(
-        partial_sums.astype(jnp.bfloat16), "col", scatter_dimension=0, tiled=True
-    ).astype(jnp.float32)
-    share_rows = summed.shape[0]
-    own_weight = lax.dynamic_slice_in_dim(
-        route_weight.reshape(-1), lax.axis_index("col") * share_rows, share_rows, 0
+    hidden = (own_weight[:, None] * jax.nn.silu(gate_sum) * up_sum).astype(jnp.bfloat16)
+    hidden_all = lax.all_gather(hidden, "col", axis=0, tiled=True).reshape(
+        2, token_count, hidden_width
     )
-    hidden = (
-        own_weight[:, None] * jax.nn.silu(summed[:, :hidden_width]) * summed[:, hidden_width:]
-    ).astype(jnp.bfloat16)
-    hidden_all = lax.all_gather(hidden, "col", axis=0, tiled=True).reshape(
-        token_count, 2, 1, hidden_width
-    )
-    picked = jnp.where(onehot[:, :, :, None], hidden_all, jnp.zeros((), hidden_all.dtype))
-    by_expert = jnp.sum(picked, axis=1).reshape(token_count, experts * hidden_width)
-    down_flat = down_weight.reshape(experts * hidden_width, down_weight.shape[2])
-    per_token = jnp.dot(by_expert, down_flat, preferred_element_type=jnp.float32)
-    mixed = lax.psum_scatter(per_token.astype(jnp.bfloat16), "row", scatter_dimension=0, tiled=True)
+    per_token = down(route_ids, hidden_all, down_weight, 256)
+    mixed = lax.psum_scatter(per_token, "row", scatter_dimension=0, tiled=True)
     return (mixed, decode_cache)
 
 

time: 434 us -> 397 us (0.915)
  waiting for transfers between devices: 208 us -> 274 us
  local copies, waits for them, and re-layouts: 85.9 us -> 20.4 us
  other arithmetic: 54.6 us -> 5.22 us
  Pallas kernels: 0 us -> 44.4 us
  matrix products: 33.9 us -> 0 us
    reduce_scatter x2 -> x3, waiting for transfers between devices: 145 us -> 216 us  [the longest x1 94.3 us: shards(): lax.psum_scatter(up_part.reshape(2 * token_count, hidden_width), 'col', s...]
    pallas_call x0 -> x2, Pallas kernels: none -> 44.4 us  [the longest x1 31.5 us: gate_up(): pl.pallas_call(gate_up_kernel, grid=(token_count // tile,), in_specs=[pl....]
    dot_general x2 -> x0, matrix products: 33.9 us -> none  [the longest x1 21.7 us: shards(): partial_sums = jnp.dot(expanded, paired, preferred_element_type=jnp.float32)]
    reduce_sum x1 -> x0, other arithmetic: 32.7 us -> none  [shards(): jnp.sum(picked, axis=1).reshape(token_count, experts * hidden_width)]
    broadcast_in_dim x2 -> x0, local copies, waits for them, and re-layouts: 29.4 us -> none  [shards(): jnp.where(onehot[:, :, :, None], hidden_all, jnp.zeros((), hidden_all.dty...]
    select_n x1 -> x0, local copies, waits for them, and re-layouts: 25.4 us -> none  [shards(): jnp.where(onehot[:, :, :, None], gathered[:, None, None, :], jnp.zeros(()...]
    select_n x1 -> x0, other arithmetic: 9.86 us -> none  [shards(): jnp.where(onehot[:, :, :, None], gathered[:, None, None, :], jnp.zeros(()...]
    all_gather x2 -> x0, local copies, waits for them, and re-layouts: 9.81 us -> none  [the longest x1 8.54 us: shards(): lax.all_gather(hidden, 'col', axis=0, tiled=True)]
  transfers between devices with their start and end apart: 4 -> 5, of which waited for: 3 -> 4; matrix products, arithmetic and copies ran while one was open for 25% -> 5% of each run, Pallas kernels for 0% -> 3%
where the time goes in v2:
time: 397 us; the launch traced here: 392 us
  waiting for transfers between devices  274 us (69%)
  Pallas kernels  44.4 us (11%)
  blocking collectives  28.5 us (7%)
  local copies, waits for them, and re-layouts  20.4 us (5%)
  between operations  14 us (4%)
  starting transfers between devices  5.99 us (2%)
  other arithmetic  5.22 us (1%)
    reduce_scatter x1, waiting for transfers between devices, shards(): lax.psum_scatter(up_part.reshape(2 * token_count, hidden_width), 'col', s...  94.3 us
    reduce_scatter x1, waiting for transfers between devices, shards(): lax.psum_scatter(gate_part.reshape(2 * token_count, hidden_width), 'col',...  92.6 us
    all_gather x1, waiting for transfers between devices, shards(): lax.all_gather(hidden, 'col', axis=0, tiled=True)  57.3 us
    pallas_call x1, Pallas kernels, gate_up(): pl.pallas_call(gate_up_kernel, grid=(token_count // tile,), in_specs=[pl....  31.5 us
    reduce_scatter x1, waiting for transfers between devices, shards(): mixed = lax.psum_scatter(per_token, 'row', scatter_dimension=0, tiled=True)  28.7 us
    all_gather x1, blocking collectives, shards(): gathered = lax.all_gather(tokens, 'row', axis=0, tiled=True)  28.5 us
    pallas_call x1, Pallas kernels, down(): pl.pallas_call(down_kernel, grid=(token_count // tile,), in_specs=[pl.Blo...  12.9 us
    unnamed x14, local copies, waits for them, and re-layouts  10.8 us
  transfers between devices with their start and end apart: 5, of which 4 were waited for; matrix products, arithmetic and copies ran while one was open for 5% of the time, Pallas kernels for 3%

profile of v2, /device:TPU:1, one launch (start us, length us, event | category | flops | bytes accessed | tf_op | source)
XLA Modules:
  0.0 392.1 jit_solution(1472124104633863167)
XLA Ops:
  7.2 0.0 reduce-scatter.6.cloned.1.call-start
  7.2 2.1 copy.32.ids_ref
  9.4 1.0 copy.30
  10.3 28.5 %all_gather.6.x_ref = bf16[2048,144]{1,0:T(8,128)(2,1)} all-gather(bf16[256,144]{1,0:T(8,128)(2,1)S(1)} %copy.30), channel_id=1, replica_groups=mesh['row'=8,'col'=16] {'row'}, dimensions={0}, use_global_device_ids=true | all-gather | bytes 663552 | tf_op jit(solution)/shard_map/all_gather | solution.py:121
  38.9 31.5 %shard_map.113 = (bf16[2,2048,720]{2,1,0:T(8,128)(2,1)}, bf16[2,2048,720]{2,1,0:T(8,128)(2,1)}) custom-call(s32[2048,2]{1,0:T(8,128)} %copy.32.ids_ref, bf16[2048,144]{1,0:T(8,128)(2,1)} %all_gather.6.x_ref, bf16[8,144,720]{2,1,0:T(8,128)(2,1)} %g_ref.1, bf16[8,144,720]{2,1,0:T(8,128)(2,1)} %u_ref.1), custom_call_target="tpu_custom_call" | custom-call | tf_op jit(solution)/shard_map/pallas_call | solution.py:78
  70.4 0.0 reduce-scatter.4.cloned.1.call-start
  70.5 0.7 reduce-scatter.4.cloned.1.call-update
  71.2 0.0 all-gather.2.cloned.1.call-start
  71.3 0.1 dynamic_slice.11
  71.3 94.3 %reduce-scatter.6.cloned.1.call-done = bf16[256,720]{1,0:T(8,128)(2,1)} async-done(((bf16[4096,720]{1,0:T(8,128)(2,1)}), bf16[256,720]{1,0:T(8,128)(2,1)}) %reduce-scatter.6.cloned.1.call-update) | async-done | bytes 368656 | tf_op jit(solution)/shard_map/reduce_scatter | solution.py:128
  165.7 92.6 %reduce-scatter.4.cloned.1.call-done = bf16[256,720]{1,0:T(8,128)(2,1)} async-done(((bf16[4096,720]{1,0:T(8,128)(2,1)}), bf16[256,720]{1,0:T(8,128)(2,1)}) %reduce-scatter.4.cloned.1.call-update) | async-done | bytes 368656 | tf_op jit(solution)/shard_map/reduce_scatter | solution.py:125
  258.2 2.2 fusion.5
  260.5 0.1 eq.35
  260.6 0.4 convert_reduce_fusion
  261.0 0.1 add.78
  261.1 0.1 reshape.143
  261.2 0.6 constant_dynamic-slice_fusion.2
  261.8 1.4 scatter_custom_fusion.1
  263.2 0.6 scatter_custom_fusion
  263.8 0.7 iota_compare_fusion.1
  264.5 1.9 broadcast_select_fusion
  266.4 2.1 gather_fusion
  268.5 5.8 %all-to-all-start = ((bf16[2,16,16,2304]{3,2,0,1:T(8,128)(2,1)}), bf16[2,16,16,2304]{3,2,0,1:T(8,128)(2,1)S(1)}, u32[]{:S(2)}, u32[]{:S(2)}) async-start(bf16[2,16,16,2304]{3,2,0,1:T(8,128)(2,1)} %bitcast.19), calls=%async_computation.3 | async-start | bytes 4718592 | tf_op jit(solution)/shard_map/all_to_all | solution.py:28
  274.4 4.4 %copy.33.d_ref = bf16[8,720,144]{2,1,0:T(8,128)(2,1)} copy(bf16[8,720,144]{1,2,0:T(8,128)(2,1)} %param.13) | data formatting | bytes 3317760 | tf_op args[3]
  278.8 57.3 %all-gather.2.cloned.1.call-done = bf16[4096,720]{1,0:T(8,128)(2,1)} async-done(((bf16[256,720]{1,0:T(8,128)(2,1)}), bf16[4096,720]{1,0:T(8,128)(2,1)}) %all-gather.2.cloned.1.call-update) | async-done | bytes 5898256 | tf_op jit(solution)/shard_map/all_gather | solution.py:136
  336.1 12.9 %shard_map.114 = bf16[2048,144]{1,0:T(8,128)(2,1)} custom-call(s32[2048,2]{1,0:T(8,128)} %copy.32.ids_ref, bf16[2,2048,720]{2,1,0:T(8,128)(2,1)} %bitcast.23, bf16[8,720,144]{2,1,0:T(8,128)(2,1)} %copy.33.d_ref), custom_call_target="tpu_custom_call" | custom-call | tf_op jit(solution)/shard_map/pallas_call | solution.py:95
  349.0 0.6 scatter_custom_fusion.2
  349.7 1.6 copy.34
  351.3 2.4 gather_fusion.1
  353.6 1.6 copy.36
  355.2 28.7 %reduce-scatter.8.cloned.1.call-done = bf16[256,144]{1,0:T(8,128)(2,1)} async-done(((bf16[2048,144]{1,0:T(8,128)(2,1)}), bf16[256,144]{1,0:T(8,128)(2,1)}) %reduce-scatter.8.cloned.1.call-update) | async-done | bytes 73744 | tf_op jit(solution)/shard_map/reduce_scatter | solution.py:140
  383.9 1.6 copy.35
  (25 shorter events, 0.2 us)
Async XLA Ops:
  7.2 254.0 %copy-start = (s32[1,16]{1,0:T(1,128)S(1)}, s32[1,16]{1,0:T(1,128)}, u32[]{:S(2)}) copy-start(s32[1,16]{1,0:T(1,128)} %param.19) | copy-start | bytes 196
  7.2 158.5 %reduce-scatter.6.cloned.1.call-start = ((), (), s32[]{:S(2)}) async-start(), calls=%async_computation.5 | async-start | bytes 6684672 | tf_op jit(solution)/shard_map/reduce_scatter | solution.py:128
  70.4 187.8 %reduce-scatter.4.cloned.1.call-start = ((), (), s32[]{:S(2)}) async-start(), calls=%async_computation.4 | async-start | bytes 6684672 | tf_op jit(solution)/shard_map/reduce_scatter | solution.py:125
  70.5 0.8 copy-start.2
  70.5 190.0 %copy-start.1 = (s32[1,16,16]{2,1,0:T(8,128)S(1)}, s32[1,16,16]{2,1,0:T(8,128)}, u32[]{:S(2)}) copy-start(s32[1,16,16]{2,1,0:T(8,128)} %param.17) | copy-start | bytes 3076
  70.5 190.6 %copy-start.3 = (s32[1,16,16]{2,1,0:T(8,128)S(1)}, s32[1,16,16]{2,1,0:T(8,128)}, u32[]{:S(2)}) copy-start(s32[1,16,16]{2,1,0:T(8,128)} %param.18) | copy-start | bytes 3076
  71.2 264.9 %all-gather.2.cloned.1.call-start = ((), (), s32[]{:S(2)}) async-start(), calls=%async_computation.6 | async-start | bytes 6684672 | tf_op jit(solution)/shard_map/all_gather | solution.py:136
  268.5 81.2 %all-to-all-start = ((bf16[2,16,16,2304]{3,2,0,1:T(8,128)(2,1)}), bf16[2,16,16,2304]{3,2,0,1:T(8,128)(2,1)S(1)}, u32[]{:S(2)}, u32[]{:S(2)}) async-start(bf16[2,16,16,2304]{3,2,0,1:T(8,128)(2,1)} %bitcast.19), calls=%async_computation.3 | async-start | bytes 4718592 | tf_op jit(solution)/shard_map/all_to_all | solution.py:28
  274.4 109.5 %reduce-scatter.8.cloned.1.call-start = ((), (), s32[]{:S(2)}) async-start(), calls=%async_computation.7 | async-start | bytes 1179648 | tf_op jit(solution)/shard_map/reduce_scatter | solution.py:140
Sparse Core Ops, SparseCore 0:
  70.5 95.0 reduce-scatter.5
  169.8 88.3 reduce-scatter.3
  260.6 75.4 all-gather.1
  349.1 34.7 reduce-scatter.7

commit v3 on v2

--- a/solution.py
+++ b/solution.py
@@ -39,22 +39,18 @@
     return received[:, source_of_slot]
 
 
-def gate_up_kernel(ids_ref, x_ref, g_ref, u_ref, go_ref, uo_ref):
+def gate_up_kernel(ids_ref, x_ref, w_ref, o_ref):
     x = x_ref[...]
     ids = ids_ref[...]
     zero = jnp.zeros_like(x)
     rows = x.shape[0]
-    width = g_ref.shape[2]
-    acc_g = jnp.zeros((2 * rows, width), jnp.float32)
-    acc_u = jnp.zeros((2 * rows, width), jnp.float32)
-    for e in range(g_ref.shape[0]):
+    acc = jnp.zeros((2 * rows, w_ref.shape[2]), jnp.float32)
+    for e in range(w_ref.shape[0]):
         lhs = jnp.concatenate(
             [jnp.where(ids[:, 0:1] == e, x, zero), jnp.where(ids[:, 1:2] == e, x, zero)], axis=0
         )
-        acc_g = acc_g + jnp.dot(lhs, g_ref[e], preferred_element_type=jnp.float32)
-        acc_u = acc_u + jnp.dot(lhs, u_ref[e], preferred_element_type=jnp.float32)
-    go_ref[...] = acc_g.astype(go_ref.dtype).reshape(go_ref.shape)
-    uo_ref[...] = acc_u.astype(uo_ref.dtype).reshape(uo_ref.shape)
+        acc = acc + jnp.dot(lhs, w_ref[e], preferred_element_type=jnp.float32)
+    o_ref[...] = acc.astype(o_ref.dtype).reshape(o_ref.shape)
 
 
 def down_kernel(ids_ref, h_ref, d_ref, o_ref):
@@ -69,24 +65,34 @@
     o_ref[...] = acc.astype(o_ref.dtype)
 
 
-def gate_up(route_ids, gathered, gate_weight, up_weight, tile):
+def gate_up(route_ids, gathered, paired, tile):
     token_count, width = gathered.shape
-    experts, _, hidden_width = gate_weight.shape
-    out = jax.ShapeDtypeStruct((2, token_count, hidden_width), jnp.bfloat16)
-    weight_spec = pl.BlockSpec((experts, width, hidden_width), lambda i: (0, 0, 0))
-    out_spec = pl.BlockSpec((2, tile, hidden_width), lambda i: (0, i, 0))
+    experts, _, paired_width = paired.shape
     return pl.pallas_call(
         gate_up_kernel,
         grid=(token_count // tile,),
         in_specs=[
             pl.BlockSpec((tile, 2), lambda i: (i, 0)),
             pl.BlockSpec((tile, width), lambda i: (i, 0)),
-            weight_spec,
-            weight_spec,
+            pl.BlockSpec((experts, width, paired_width), lambda i: (0, 0, 0)),
         ],
-        out_specs=[out_spec, out_spec],
-        out_shape=[out, out],
-    )(route_ids, gathered, gate_weight, up_weight)
+        out_specs=pl.BlockSpec((2, tile, paired_width), lambda i: (0, i, 0)),
+        out_shape=jax.ShapeDtypeStruct((2, token_count, paired_width), jnp.bfloat16),
+    )(route_ids, gathered, paired)
+
+
+def gather_rows(x, axis_name):
+    count = lax.axis_size(axis_name)
+    copies = jnp.broadcast_to(x[None], (count,) + x.shape)
+    received = lax.all_to_all(copies, axis_name, 0, 0, tiled=False)
+    return received.reshape((count * x.shape[0],) + x.shape[1:])
+
+
+def sum_scatter_rows(x, axis_name):
+    count = lax.axis_size(axis_name)
+    pieces = x.reshape((count, x.shape[0] // count) + x.shape[1:])
+    received = lax.all_to_all(pieces, axis_name, 0, 0, tiled=False)
+    return jnp.sum(received.astype(jnp.float32), axis=0)
 
 
 def down(route_ids, hidden_all, down_weight, tile):
@@ -118,26 +124,24 @@
     pages_used,
 ):
     decode_cache = move_pages(prefill_cache, dest_col, dest_slot, pages_used)
-    gathered = lax.all_gather(tokens, "row", axis=0, tiled=True)
+    gathered = gather_rows(tokens, "row")
     token_count = gathered.shape[0]
     hidden_width = gate_weight.shape[2]
-    gate_part, up_part = gate_up(route_ids, gathered, gate_weight, up_weight, 256)
-    gate_sum = lax.psum_scatter(
-        gate_part.reshape(2 * token_count, hidden_width), "col", scatter_dimension=0, tiled=True
-    ).astype(jnp.float32)
-    up_sum = lax.psum_scatter(
-        up_part.reshape(2 * token_count, hidden_width), "col", scatter_dimension=0, tiled=True
-    ).astype(jnp.float32)
-    share_rows = gate_sum.shape[0]
+    paired = jnp.concatenate([gate_weight, up_weight], axis=2)
+    partial_sums = gate_up(route_ids, gathered, paired, 256)
+    summed = sum_scatter_rows(partial_sums.reshape(2 * token_count, 2 * hidden_width), "col")
+    share_rows = summed.shape[0]
     own_weight = lax.dynamic_slice_in_dim(
         route_weight.T.reshape(-1), lax.axis_index("col") * share_rows, share_rows, 0
     )
-    hidden = (own_weight[:, None] * jax.nn.silu(gate_sum) * up_sum).astype(jnp.bfloat16)
+    hidden = (
+        own_weight[:, None] * jax.nn.silu(summed[:, :hidden_width]) * summed[:, hidden_width:]
+    ).astype(jnp.bfloat16)
     hidden_all = lax.all_gather(hidden, "col", axis=0, tiled=True).reshape(
         2, token_count, hidden_width
     )
     per_token = down(route_ids, hidden_all, down_weight, 256)
-    mixed = lax.psum_scatter(per_token, "row", scatter_dimension=0, tiled=True)
+    mixed = sum_scatter_rows(per_token, "row").astype(jnp.bfloat16)
     return (mixed, decode_cache)
 
 

time: 397 us -> 403 us (1.015)
  blocking collectives: 28.5 us -> 0 us
  local copies, waits for them, and re-layouts: 20.4 us -> 47.2 us
  starting transfers between devices: 5.99 us -> 26.7 us
  waiting for transfers between devices: 274 us -> 254 us
  other arithmetic: 5.22 us -> 15.3 us
    reduce_scatter x3 -> x0, waiting for transfers between devices: 216 us -> none  [the longest x1 94.3 us: shards(): lax.psum_scatter(up_part.reshape(2 * token_count, hidden_width), 'col', s...]
    all_to_all x0 -> x3, waiting for transfers between devices: none -> 195 us  [the longest x2 190 us: sum_scatter_rows(): received = lax.all_to_all(pieces, axis_name, 0, 0, tiled=False)]
    all_gather x1 -> x0, blocking collectives: 28.5 us -> none  [shards(): gathered = lax.all_gather(tokens, 'row', axis=0, tiled=True)]
    all_to_all x0 -> x3, starting transfers between devices: none -> 18.5 us  [the longest x2 12.1 us: sum_scatter_rows(): received = lax.all_to_all(pieces, axis_name, 0, 0, tiled=False)]
    another operation x0 -> x1, local copies, waits for them, and re-layouts: none -> 15.7 us  [sum_scatter_rows(): pieces = x.reshape((count, x.shape[0] // count) + x.shape[1:])]
    all_gather x0 -> x1, local copies, waits for them, and re-layouts: none -> 8.54 us  [shards(): lax.all_gather(hidden, 'col', axis=0, tiled=True)]
    reduce_sum x0 -> x2, other arithmetic: none -> 6.88 us  [sum_scatter_rows(): return jnp.sum(received.astype(jnp.float32), axis=0)]
    concatenate x0 -> x1, other arithmetic: none -> 4.46 us  [shards(): paired = jnp.concatenate([gate_weight, up_weight], axis=2)]
  transfers between devices with their start and end apart: 5 -> 5, of which waited for: 4 -> 4; matrix products, arithmetic and copies ran while one was open for 5% -> 9% of each run, Pallas kernels for 3% -> 3%
where the time goes in v3:
time: 403 us; the launch traced here: 402 us
  waiting for transfers between devices  254 us (63%)
  local copies, waits for them, and re-layouts  47.2 us (12%)
  Pallas kernels  44.3 us (11%)
  starting transfers between devices  26.7 us (7%)
  other arithmetic  15.3 us (4%)
  between operations  14.2 us (4%)
    all_to_all x2, waiting for transfers between devices, sum_scatter_rows(): received = lax.all_to_all(pieces, axis_name, 0, 0, tiled=False)  190 us
    all_gather x1, waiting for transfers between devices, shards(): lax.all_gather(hidden, 'col', axis=0, tiled=True)  59.6 us
    pallas_call x1, Pallas kernels, gate_up(): pl.pallas_call(gate_up_kernel, grid=(token_count // tile,), in_specs=[pl....  31.4 us
    another operation x1, local copies, waits for them, and re-layouts, sum_scatter_rows(): pieces = x.reshape((count, x.shape[0] // count) + x.shape[1:])  15.7 us
    pallas_call x1, Pallas kernels, down(): pl.pallas_call(down_kernel, grid=(token_count // tile,), in_specs=[pl.Blo...  12.9 us
    all_to_all x2, starting transfers between devices, sum_scatter_rows(): received = lax.all_to_all(pieces, axis_name, 0, 0, tiled=False)  12.1 us
    all_gather x1, local copies, waits for them, and re-layouts, shards(): lax.all_gather(hidden, 'col', axis=0, tiled=True)  8.54 us
    all_to_all x1, starting transfers between devices, move_pages(): lax.all_to_all(masked_pages[:, inverse], 'col', split_axis=1, concat_axis...  8.18 us
  transfers between devices with their start and end apart: 5, of which 4 were waited for; matrix products, arithmetic and copies ran while one was open for 9% of the time, Pallas kernels for 3%

profile of v3, /device:TPU:1, one launch (start us, length us, event | category | flops | bytes accessed | tf_op | source)
XLA Modules:
  0.0 402.1 jit_solution(6207664354527131653)
XLA Ops:
  7.2 1.9 broadcast_in_dim.24
  9.1 6.4 %all-to-all-start = ((bf16[8,256,144]{1,2,0:T(8,128)(2,1)}), bf16[8,256,144]{1,2,0:T(8,128)(2,1)S(1)}, u32[]{:S(2)}, u32[]{:S(2)}) async-start(bf16[8,256,144]{1,2,0:T(8,128)(2,1)} %broadcast_in_dim.24), calls=%async_computation | async-start | bytes 1179648 | tf_op jit(solution)/shard_map/all_to_all | solution.py:87
  15.4 2.1 copy.52.ids_ref
  17.5 4.5 %pad_maximum_fusion.w_ref = bf16[8,144,1440]{2,1,0:T(8,128)(2,1)} fusion(bf16[8,144,720]{2,1,0:T(8,128)(2,1)S(1)} %copy-done.1, bf16[8,144,720]{2,1,0:T(8,128)(2,1)} %param.11), kind=kLoop, calls=%fused_computation.6 | loop fusion | flops 6635520 | bytes 6635520 | tf_op jit(solution)/shard_map/concatenate | solution.py:130
  22.0 4.4 %all-to-all-done = bf16[8,256,144]{1,2,0:T(8,128)(2,1)S(1)} async-done(((bf16[8,256,144]{1,2,0:T(8,128)(2,1)}), bf16[8,256,144]{1,2,0:T(8,128)(2,1)S(1)}, u32[]{:S(2)}, u32[]{:S(2)}) %all-to-all-start) | async-done | bytes 589856 | tf_op jit(solution)/shard_map/all_to_all | solution.py:87
  26.4 1.3 copy.48
  27.6 31.4 %shard_map.113 = bf16[2,2048,1440]{2,1,0:T(8,128)(2,1)} custom-call(s32[2048,2]{1,0:T(8,128)} %copy.52.ids_ref, bf16[2048,144]{1,0:T(8,128)(2,1)} %bitcast.24, bf16[8,144,1440]{2,1,0:T(8,128)(2,1)} %pad_maximum_fusion.w_ref), custom_call_target="tpu_custom_call" | custom-call | tf_op jit(solution)/shard_map/pallas_call | solution.py:71
  59.0 15.7 %copy.50 = bf16[16,256,1440]{1,2,0:T(8,128)(2,1)} copy(bf16[16,256,1440]{2,1,0:T(8,128)(2,1)} %bitcast.20) | data formatting | bytes 23592960 | tf_op jit(solution)/shard_map/reshape;reshape | solution.py:93
  74.7 8.3 %all-to-all-start.1 = ((bf16[16,256,1440]{1,2,0:T(8,128)(2,1)}), bf16[16,256,1440]{1,2,0:T(8,128)(2,1)}, u32[]{:S(2)}, u32[]{:S(2)}) async-start(bf16[16,256,1440]{1,2,0:T(8,128)(2,1)} %copy.50), calls=%async_computation.1 | async-start | bytes 23592960 | tf_op jit(solution)/shard_map/all_to_all | solution.py:94
  83.1 185.5 %all-to-all-done.1 = bf16[16,256,1440]{1,2,0:T(8,128)(2,1)} async-done(((bf16[16,256,1440]{1,2,0:T(8,128)(2,1)}), bf16[16,256,1440]{1,2,0:T(8,128)(2,1)}, u32[]{:S(2)}, u32[]{:S(2)}) %all-to-all-start.1) | async-done | bytes 11796512 | tf_op jit(solution)/shard_map/all_to_all | solution.py:94
  268.7 6.2 %convert_reduce_fusion = f32[256,1440]{0,1:T(8,128)S(1)} fusion(bf16[16,256,1440]{1,2,0:T(8,128)(2,1)} %all-to-all-done.1), kind=kLoop, calls=%fused_computation.5 | loop fusion | flops 11427840 | bytes 13271040 | tf_op jit(solution)/shard_map/reduce_sum | solution.py:95
  274.8 1.0 fusion
  275.9 0.4 convert_reduce_fusion.1
  276.5 0.6 constant_dynamic-slice_fusion.2
  277.1 1.4 scatter_custom_fusion.1
  278.6 0.6 scatter_custom_fusion
  279.2 0.7 iota_compare_fusion.1
  279.9 1.9 broadcast_select_fusion
  281.8 2.1 gather_fusion
  283.9 8.2 %all-to-all-start.3 = ((bf16[2,16,16,2304]{3,2,0,1:T(8,128)(2,1)}), bf16[2,16,16,2304]{3,2,0,1:T(8,128)(2,1)S(1)}, u32[]{:S(2)}, u32[]{:S(2)}) async-start(bf16[2,16,16,2304]{3,2,0,1:T(8,128)(2,1)} %bitcast.22), calls=%async_computation.3 | async-start | bytes 4718592 | tf_op jit(solution)/shard_map/all_to_all | solution.py:28
  292.1 4.4 %copy.53.d_ref = bf16[8,720,144]{2,1,0:T(8,128)(2,1)} copy(bf16[8,720,144]{1,2,0:T(8,128)(2,1)} %param.13) | data formatting | bytes 3317760 | tf_op args[3]
  296.5 59.6 %all-gather.2.cloned.1.call-done = bf16[4096,720]{0,1:T(8,128)(2,1)} async-done(((bf16[256,720]{0,1:T(8,128)(2,1)}), bf16[4096,720]{0,1:T(8,128)(2,1)}) %all-gather.2.cloned.1.call-update) | async-done | bytes 5898256 | tf_op jit(solution)/shard_map/all_gather | solution.py:140
  356.1 8.5 %copy.51 = bf16[4096,720]{1,0:T(8,128)(2,1)} copy(bf16[4096,720]{0,1:T(8,128)(2,1)} %all-gather.2.cloned.1.call-done) | data formatting | bytes 11796480 | tf_op jit(solution)/shard_map/all_gather | solution.py:140
  364.6 12.9 %shard_map.114 = bf16[2048,144]{1,0:T(8,128)(2,1)} custom-call(s32[2048,2]{1,0:T(8,128)} %copy.52.ids_ref, bf16[2,2048,720]{2,1,0:T(8,128)(2,1)} %bitcast.21, bf16[8,720,144]{2,1,0:T(8,128)(2,1)} %copy.53.d_ref), custom_call_target="tpu_custom_call" | custom-call | tf_op jit(solution)/shard_map/pallas_call | solution.py:101
  377.5 2.2 copy.54
  379.7 3.9 all-to-all-start.2
  383.6 0.6 scatter_custom_fusion.2
  384.2 1.6 copy.56
  385.8 2.4 gather_fusion.1
  388.1 1.6 copy.58
  389.7 4.8 %all-to-all-done.2 = bf16[8,256,144]{1,2,0:T(8,128)(2,1)S(1)} async-done(((bf16[8,256,144]{1,2,0:T(8,128)(2,1)}), bf16[8,256,144]{1,2,0:T(8,128)(2,1)S(1)}, u32[]{:S(2)}, u32[]{:S(2)}) %all-to-all-start.2) | async-done | bytes 589856 | tf_op jit(solution)/shard_map/all_to_all | solution.py:94
  394.5 0.7 reduce_sum.31
  (29 shorter events, 0.5 us)
Async XLA Ops:
  7.2 269.4 %copy-start = (s32[1,16]{1,0:T(1,128)S(1)}, s32[1,16]{1,0:T(1,128)}, u32[]{:S(2)}) copy-start(s32[1,16]{1,0:T(1,128)} %param.19) | copy-start | bytes 196
  7.2 10.4 %copy-start.1 = (bf16[8,144,720]{2,1,0:T(8,128)(2,1)S(1)}, bf16[8,144,720]{2,1,0:T(8,128)(2,1)}, u32[]{:S(2)}) copy-start(bf16[8,144,720]{2,1,0:T(8,128)(2,1)} %param.12) | copy-start | bytes 4976644
  9.1 17.3 %all-to-all-start = ((bf16[8,256,144]{1,2,0:T(8,128)(2,1)}), bf16[8,256,144]{1,2,0:T(8,128)(2,1)S(1)}, u32[]{:S(2)}, u32[]{:S(2)}) async-start(bf16[8,256,144]{1,2,0:T(8,128)(2,1)} %broadcast_in_dim.24), calls=%async_computation | async-start | bytes 1179648 | tf_op jit(solution)/shard_map/all_to_all | solution.py:87
  74.7 8.3 %copy-start.3 = (f32[2048,2]{0,1:T(2,128)S(1)}, f32[2048,2]{0,1:T(2,128)}, u32[]{:S(2)}) copy-start(f32[2048,2]{0,1:T(2,128)} %param.15) | copy-start | bytes 49156
  74.7 194.0 %all-to-all-start.1 = ((bf16[16,256,1440]{1,2,0:T(8,128)(2,1)}), bf16[16,256,1440]{1,2,0:T(8,128)(2,1)}, u32[]{:S(2)}, u32[]{:S(2)}) async-start(bf16[16,256,1440]{1,2,0:T(8,128)(2,1)} %copy.50), calls=%async_computation.1 | async-start | bytes 23592960 | tf_op jit(solution)/shard_map/all_to_all | solution.py:94
  83.0 273.1 %all-gather.2.cloned.1.call-start = ((), (), s32[]{:S(2)}) async-start(), calls=%async_computation.4 | async-start | bytes 6266880 | tf_op jit(solution)/shard_map/all_gather | solution.py:140
  83.1 192.7 %copy-start.2 = (s32[1,16,16]{2,1,0:T(8,128)S(1)}, s32[1,16,16]{2,1,0:T(8,128)}, u32[]{:S(2)}) copy-start(s32[1,16,16]{2,1,0:T(8,128)} %param.17) | copy-start | bytes 3076
  83.1 193.3 %copy-start.4 = (s32[1,16,16]{2,1,0:T(8,128)S(1)}, s32[1,16,16]{2,1,0:T(8,128)}, u32[]{:S(2)}) copy-start(s32[1,16,16]{2,1,0:T(8,128)} %param.18) | copy-start | bytes 3076
  283.9 95.8 %all-to-all-start.3 = ((bf16[2,16,16,2304]{3,2,0,1:T(8,128)(2,1)}), bf16[2,16,16,2304]{3,2,0,1:T(8,128)(2,1)S(1)}, u32[]{:S(2)}, u32[]{:S(2)}) async-start(bf16[2,16,16,2304]{3,2,0,1:T(8,128)(2,1)} %bitcast.22), calls=%async_computation.3 | async-start | bytes 4718592 | tf_op jit(solution)/shard_map/all_to_all | solution.py:28
  379.7 14.8 %all-to-all-start.2 = ((bf16[8,256,144]{1,2,0:T(8,128)(2,1)}), bf16[8,256,144]{1,2,0:T(8,128)(2,1)S(1)}, u32[]{:S(2)}, u32[]{:S(2)}) async-start(bf16[8,256,144]{1,2,0:T(8,128)(2,1)} %copy.54), calls=%async_computation.2 | async-start | bytes 1179648 | tf_op jit(solution)/shard_map/all_to_all | solution.py:94
Sparse Core Ops, SparseCore 0:
  275.9 80.0 all-gather.1

commit v4 on v3

--- a/solution.py
+++ b/solution.py
@@ -3,6 +3,7 @@
 from jax import lax
 from jax.sharding import PartitionSpec as P
 from jax.experimental import pallas as pl
+from jax.experimental.pallas import tpu as pltpu
 
 
 def move_pages(prefill_cache, dest_col, dest_slot, pages_used):
@@ -53,6 +54,18 @@
     o_ref[...] = acc.astype(o_ref.dtype).reshape(o_ref.shape)
 
 
+def hidden_kernel(w_ref, s_ref, o_ref, h_scr):
+    @pl.when(pl.program_id(1) == 0)
+    def _():
+        summed = jnp.sum(s_ref[...].astype(jnp.float32), axis=0)
+        half = summed.shape[1] // 2
+        gate = summed[:, :half]
+        hidden = w_ref[...] * (gate / (1.0 + jnp.exp(-gate))) * summed[:, half:]
+        h_scr[...] = hidden.astype(h_scr.dtype)
+
+    o_ref[0] = h_scr[...]
+
+
 def down_kernel(ids_ref, h_ref, d_ref, o_ref):
     ids = ids_ref[...]
     first = h_ref[0]
@@ -95,6 +108,21 @@
     return jnp.sum(received.astype(jnp.float32), axis=0)
 
 
+def hidden_copies(own_weight, received, hidden_width, block):
+    count, share_rows, paired_width = received.shape
+    return pl.pallas_call(
+        hidden_kernel,
+        grid=(share_rows // block, count),
+        in_specs=[
+            pl.BlockSpec((block, 1), lambda i, j: (i, 0)),
+            pl.BlockSpec((count, block, paired_width), lambda i, j: (0, i, 0)),
+        ],
+        out_specs=pl.BlockSpec((1, block, hidden_width), lambda i, j: (j, i, 0)),
+        out_shape=jax.ShapeDtypeStruct((count, share_rows, hidden_width), jnp.bfloat16),
+        scratch_shapes=[pltpu.VMEM((block, hidden_width), jnp.bfloat16)],
+    )(own_weight, received)
+
+
 def down(route_ids, hidden_all, down_weight, tile):
     _, token_count, hidden_width = hidden_all.shape
     experts, _, width = down_weight.shape
@@ -127,19 +155,27 @@
     gathered = gather_rows(tokens, "row")
     token_count = gathered.shape[0]
     hidden_width = gate_weight.shape[2]
-    paired = jnp.concatenate([gate_weight, up_weight], axis=2)
+    experts, width, _ = gate_weight.shape
+    padded_width = -(-hidden_width // 128) * 128
+    pad = jnp.zeros((experts, width, padded_width - hidden_width), gate_weight.dtype)
+    paired = jnp.concatenate([gate_weight, pad, up_weight, pad], axis=2)
     partial_sums = gate_up(route_ids, gathered, paired, 256)
-    summed = sum_scatter_rows(partial_sums.reshape(2 * token_count, 2 * hidden_width), "col")
-    share_rows = summed.shape[0]
+    col_count = lax.axis_size("col")
+    share_rows = 2 * token_count // col_count
+    received = lax.all_to_all(
+        partial_sums.reshape(col_count, share_rows, 2 * padded_width), "col", 0, 0, tiled=False
+    )
     own_weight = lax.dynamic_slice_in_dim(
         route_weight.T.reshape(-1), lax.axis_index("col") * share_rows, share_rows, 0
+    ).reshape(share_rows, 1)
+    copies = hidden_copies(own_weight, received, padded_width, 64)
+    hidden_all = lax.all_to_all(copies, "col", 0, 0, tiled=False).reshape(
+        2, token_count, padded_width
     )
-    hidden = (
-        own_weight[:, None] * jax.nn.silu(summed[:, :hidden_width]) * summed[:, hidden_width:]
-    ).astype(jnp.bfloat16)
-    hidden_all = lax.all_gather(hidden, "col", axis=0, tiled=True).reshape(
-        2, token_count, hidden_width
+    down_pad = jnp.zeros(
+        (experts, padded_width - hidden_width, down_weight.shape[2]), down_weight.dtype
     )
+    down_weight = jnp.concatenate([down_weight, down_pad], axis=1)
     per_token = down(route_ids, hidden_all, down_weight, 256)
     mixed = sum_scatter_rows(per_token, "row").astype(jnp.bfloat16)
     return (mixed, decode_cache)

time: 403 us -> 451 us (1.12)
  waiting for transfers between devices: 254 us -> 302 us
  Pallas kernels: 44.3 us -> 73.7 us
  local copies, waits for them, and re-layouts: 47.2 us -> 32.6 us
  between operations: 14.2 us -> 0.83 us
  other arithmetic: 15.3 us -> 3.74 us
  starting transfers between devices: 26.7 us -> 36.9 us
    all_to_all x0 -> x2, waiting for transfers between devices: none -> 285 us  [the longest x1 198 us: shards(): lax.all_to_all(partial_sums.reshape(col_count, share_rows, 2 * padded_wid...]
    all_to_all x2 -> x1, waiting for transfers between devices: 190 us -> 3.03 us  [sum_scatter_rows(): received = lax.all_to_all(pieces, axis_name, 0, 0, tiled=False)]
    all_gather x1 -> x0, waiting for transfers between devices: 59.6 us -> none  [shards(): lax.all_gather(hidden, 'col', axis=0, tiled=True)]
    pallas_call x0 -> x1, Pallas kernels: none -> 29.3 us  [hidden_copies(): pl.pallas_call(hidden_kernel, grid=(share_rows // block, count), in_specs...]
    all_to_all x0 -> x2, starting transfers between devices: none -> 16.6 us  [the longest x1 8.31 us: shards(): lax.all_to_all(copies, 'col', 0, 0, tiled=False)]
    another operation x1 -> x0, local copies, waits for them, and re-layouts: 15.7 us -> none  [sum_scatter_rows(): pieces = x.reshape((count, x.shape[0] // count) + x.shape[1:])]
    all_to_all x1, waiting for transfers between devices: 0.01 us -> 10.8 us  [move_pages(): lax.all_to_all(masked_pages[:, inverse], 'col', split_axis=1, concat_axis...]
    all_to_all x2 -> x1, starting transfers between devices: 12.1 us -> 3.54 us  [sum_scatter_rows(): received = lax.all_to_all(pieces, axis_name, 0, 0, tiled=False)]
  transfers between devices with their start and end apart: 5 -> 5, of which waited for: 4 -> 5; matrix products, arithmetic and copies ran while one was open for 9% -> 7% of each run, Pallas kernels for 3% -> 3%
where the time goes in v4:
time: 451 us; the launch traced here: 449 us
  waiting for transfers between devices  302 us (67%)
  Pallas kernels  73.7 us (16%)
  starting transfers between devices  36.9 us (8%)
  local copies, waits for them, and re-layouts  32.6 us (7%)
    all_to_all x1, waiting for transfers between devices, shards(): lax.all_to_all(partial_sums.reshape(col_count, share_rows, 2 * padded_wid...  198 us
    all_to_all x1, waiting for transfers between devices, shards(): lax.all_to_all(copies, 'col', 0, 0, tiled=False)  87.1 us
    pallas_call x1, Pallas kernels, gate_up(): pl.pallas_call(gate_up_kernel, grid=(token_count // tile,), in_specs=[pl....  31.4 us
    pallas_call x1, Pallas kernels, hidden_copies(): pl.pallas_call(hidden_kernel, grid=(share_rows // block, count), in_specs...  29.3 us
    pallas_call x1, Pallas kernels, down(): pl.pallas_call(down_kernel, grid=(token_count // tile,), in_specs=[pl.Blo...  13.1 us
    all_to_all x1, waiting for transfers between devices, move_pages(): lax.all_to_all(masked_pages[:, inverse], 'col', split_axis=1, concat_axis...  10.8 us
    all_to_all x1, starting transfers between devices, move_pages(): lax.all_to_all(masked_pages[:, inverse], 'col', split_axis=1, concat_axis...  10.5 us
  transfers between devices with their start and end apart: 5, of which 5 were waited for; matrix products, arithmetic and copies ran while one was open for 7% of the time, Pallas kernels for 3%

profile of v4, /device:TPU:1, one launch (start us, length us, event | category | flops | bytes accessed | tf_op | source)
XLA Modules:
  0.0 449.4 jit_solution(9555534130917368569)
XLA Ops:
  0.7 1.9 broadcast_in_dim.42
  2.5 6.4 %all-to-all-start = ((bf16[8,256,144]{1,2,0:T(8,128)(2,1)}), bf16[8,256,144]{1,2,0:T(8,128)(2,1)S(1)}, u32[]{:S(2)}, u32[]{:S(2)}) async-start(bf16[8,256,144]{1,2,0:T(8,128)(2,1)} %broadcast_in_dim.42), calls=%async_computation | async-start | bytes 1179648 | tf_op jit(solution)/shard_map/all_to_all | solution.py:100
  8.9 2.1 copy.43.ids_ref
  11.1 6.2 %concatenate.6.w_ref = bf16[8,144,1536]{2,1,0:T(8,128)(2,1)} concatenate(bf16[8,144,720]{2,1,0:T(8,128)(2,1)S(1)} %copy-done.1, bf16[8,144,48]{2,1,0:T(8,128)(2,1)S(1)} %broadcast_in_dim.43, bf16[8,144,720]{2,1,0:T(8,128)(2,1)} %param.12, bf16[8,144,48]{2,1,0:T(8,128)(2,1)S(1)} %broadcast_in_dim.43), dimensions={2} | concatenate | bytes 7077888 | tf_op jit(solution)/shard_map/concatenate | solution.py:161
  17.3 2.5 all-to-all-done
  19.8 1.3 copy.39
  21.1 31.4 %shard_map.113 = bf16[2,2048,1536]{2,1,0:T(8,128)(2,1)} custom-call(s32[2048,2]{1,0:T(8,128)} %copy.43.ids_ref, bf16[2048,144]{1,0:T(8,128)(2,1)} %bitcast.23, bf16[8,144,1536]{2,1,0:T(8,128)(2,1)} %concatenate.6.w_ref), custom_call_target="tpu_custom_call" | custom-call | tf_op jit(solution)/shard_map/pallas_call | solution.py:84
  52.5 8.3 %all-to-all-start.1 = ((bf16[16,256,1536]{2,1,0:T(8,128)(2,1)}), bf16[16,256,1536]{2,1,0:T(8,128)(2,1)}, u32[]{:S(2)}, u32[]{:S(2)}) async-start(bf16[16,256,1536]{2,1,0:T(8,128)(2,1)} %bitcast.21), calls=%async_computation.1 | async-start | bytes 25165824 | tf_op jit(solution)/shard_map/all_to_all | solution.py:165
  60.8 0.8 copy.41.w_ref
  61.6 198.1 %all-to-all-done.1.s_ref = bf16[16,256,1536]{2,1,0:T(8,128)(2,1)} async-done(((bf16[16,256,1536]{2,1,0:T(8,128)(2,1)}), bf16[16,256,1536]{2,1,0:T(8,128)(2,1)}, u32[]{:S(2)}, u32[]{:S(2)}) %all-to-all-start.1) | async-done | bytes 12582944 | tf_op jit(solution)/shard_map/all_to_all | solution.py:165
  259.7 29.3 %shard_map.114 = bf16[16,256,768]{2,1,0:T(8,128)(2,1)} custom-call(f32[256,1]{1,0:T(8,128)} %copy.41.w_ref, bf16[16,256,1536]{2,1,0:T(8,128)(2,1)} %all-to-all-done.1.s_ref), custom_call_target="tpu_custom_call" | custom-call | tf_op jit(solution)/shard_map/pallas_call | solution.py:113
  289.0 8.3 %all-to-all-start.2 = ((bf16[16,256,768]{2,1,0:T(8,128)(2,1)}), bf16[16,256,768]{2,1,0:T(8,128)(2,1)}, u32[]{:S(2)}, u32[]{:S(2)}) async-start(bf16[16,256,768]{2,1,0:T(8,128)(2,1)} %shard_map.114), calls=%async_computation.2 | async-start | bytes 12582912 | tf_op jit(solution)/shard_map/all_to_all | solution.py:172
  298.0 0.6 constant_dynamic-slice_fusion.2
  298.6 1.4 scatter_custom_fusion.1
  300.1 0.6 scatter_custom_fusion
  300.7 0.7 iota_compare_fusion.1
  301.4 1.9 broadcast_select_fusion
  303.3 2.1 gather_fusion
  305.4 87.1 %all-to-all-done.2 = bf16[16,256,768]{2,1,0:T(8,128)(2,1)} async-done(((bf16[16,256,768]{2,1,0:T(8,128)(2,1)}), bf16[16,256,768]{2,1,0:T(8,128)(2,1)}, u32[]{:S(2)}, u32[]{:S(2)}) %all-to-all-start.2) | async-done | bytes 6291488 | tf_op jit(solution)/shard_map/all_to_all | solution.py:172
  392.5 10.5 %all-to-all-start.4 = ((bf16[2,16,16,2304]{3,2,0,1:T(8,128)(2,1)}), bf16[2,16,16,2304]{3,2,0,1:T(8,128)(2,1)}, u32[]{:S(2)}, u32[]{:S(2)}) async-start(bf16[2,16,16,2304]{3,2,0,1:T(8,128)(2,1)} %bitcast.10), calls=%async_computation.4 | async-start | bytes 4718592 | tf_op jit(solution)/shard_map/all_to_all | solution.py:29
  403.0 2.9 copy.42
  405.9 2.2 concatenate.7.d_ref
  408.2 13.1 %shard_map.115 = bf16[2048,144]{1,0:T(8,128)(2,1)} custom-call(s32[2048,2]{1,0:T(8,128)} %copy.43.ids_ref, bf16[2,2048,768]{2,1,0:T(8,128)(2,1)} %bitcast.4.h_ref, bf16[8,768,144]{2,1,0:T(8,128)(2,1)} %concatenate.7.d_ref), custom_call_target="tpu_custom_call" | custom-call | tf_op jit(solution)/shard_map/pallas_call | solution.py:129
  421.2 2.2 copy.44
  423.4 10.8 %all-to-all-done.4 = bf16[2,16,16,2304]{3,2,0,1:T(8,128)(2,1)} async-done(((bf16[2,16,16,2304]{3,2,0,1:T(8,128)(2,1)}), bf16[2,16,16,2304]{3,2,0,1:T(8,128)(2,1)}, u32[]{:S(2)}, u32[]{:S(2)}) %all-to-all-start.4) | async-done | bytes 2359328 | tf_op jit(solution)/shard_map/all_to_all | solution.py:29
  434.2 3.5 all-to-all-start.3
  437.8 0.6 scatter_custom_fusion.2
  438.4 1.8 copy.46
  440.3 2.1 gather_fusion.1
  442.4 3.2 copy.48
  445.6 3.0 all-to-all-done.3
  448.7 0.7 reduce_sum.21
  (28 shorter events, 0.9 us)
Async XLA Ops:
  0.6 297.4 %copy-start = (s32[1,16]{1,0:T(1,128)S(1)}, s32[1,16]{1,0:T(1,128)}, u32[]{:S(2)}) copy-start(s32[1,16]{1,0:T(1,128)} %param.19) | copy-start | bytes 196
  0.6 10.4 %copy-start.1 = (bf16[8,144,720]{2,1,0:T(8,128)(2,1)S(1)}, bf16[8,144,720]{2,1,0:T(8,128)(2,1)}, u32[]{:S(2)}) copy-start(bf16[8,144,720]{2,1,0:T(8,128)(2,1)} %param.11) | copy-start | bytes 4976644
  2.5 17.3 %all-to-all-start = ((bf16[8,256,144]{1,2,0:T(8,128)(2,1)}), bf16[8,256,144]{1,2,0:T(8,128)(2,1)S(1)}, u32[]{:S(2)}, u32[]{:S(2)}) async-start(bf16[8,256,144]{1,2,0:T(8,128)(2,1)} %broadcast_in_dim.42), calls=%async_computation | async-start | bytes 1179648 | tf_op jit(solution)/shard_map/all_to_all | solution.py:100
  52.5 8.3 %copy-start.3 = (f32[2048,2]{0,1:T(2,128)S(1)}, f32[2048,2]{0,1:T(2,128)}, u32[]{:S(2)}) copy-start(f32[2048,2]{0,1:T(2,128)} %param.15) | copy-start | bytes 49156
  52.5 207.2 %all-to-all-start.1 = ((bf16[16,256,1536]{2,1,0:T(8,128)(2,1)}), bf16[16,256,1536]{2,1,0:T(8,128)(2,1)}, u32[]{:S(2)}, u32[]{:S(2)}) async-start(bf16[16,256,1536]{2,1,0:T(8,128)(2,1)} %bitcast.21), calls=%async_computation.1 | async-start | bytes 25165824 | tf_op jit(solution)/shard_map/all_to_all | solution.py:165
  289.0 8.3 %copy-start.2 = (s32[1,16,16]{2,1,0:T(8,128)S(1)}, s32[1,16,16]{2,1,0:T(8,128)}, u32[]{:S(2)}) copy-start(s32[1,16,16]{2,1,0:T(8,128)} %param.17) | copy-start | bytes 3076
  289.0 9.0 %copy-start.4 = (s32[1,16,16]{2,1,0:T(8,128)S(1)}, s32[1,16,16]{2,1,0:T(8,128)}, u32[]{:S(2)}) copy-start(s32[1,16,16]{2,1,0:T(8,128)} %param.18) | copy-start | bytes 3076
  289.0 103.5 %all-to-all-start.2 = ((bf16[16,256,768]{2,1,0:T(8,128)(2,1)}), bf16[16,256,768]{2,1,0:T(8,128)(2,1)}, u32[]{:S(2)}, u32[]{:S(2)}) async-start(bf16[16,256,768]{2,1,0:T(8,128)(2,1)} %shard_map.114), calls=%async_computation.2 | async-start | bytes 12582912 | tf_op jit(solution)/shard_map/all_to_all | solution.py:172
  392.5 41.7 %all-to-all-start.4 = ((bf16[2,16,16,2304]{3,2,0,1:T(8,128)(2,1)}), bf16[2,16,16,2304]{3,2,0,1:T(8,128)(2,1)}, u32[]{:S(2)}, u32[]{:S(2)}) async-start(bf16[2,16,16,2304]{3,2,0,1:T(8,128)(2,1)} %bitcast.10), calls=%async_computation.4 | async-start | bytes 4718592 | tf_op jit(solution)/shard_map/all_to_all | solution.py:29
  434.2 14.4 %all-to-all-start.3 = ((bf16[8,256,144]{1,2,0:T(8,128)(2,1)}), bf16[8,256,144]{1,2,0:T(8,128)(2,1)S(1)}, u32[]{:S(2)}, u32[]{:S(2)}) async-start(bf16[8,256,144]{1,2,0:T(8,128)(2,1)} %copy.44), calls=%async_computation.3 | async-start | bytes 1179648 | tf_op jit(solution)/shard_map/all_to_all | solution.py:107

commit v5 on v3

--- a/solution.py
+++ b/solution.py
@@ -129,7 +129,9 @@
     hidden_width = gate_weight.shape[2]
     paired = jnp.concatenate([gate_weight, up_weight], axis=2)
     partial_sums = gate_up(route_ids, gathered, paired, 256)
-    summed = sum_scatter_rows(partial_sums.reshape(2 * token_count, 2 * hidden_width), "col")
+    summed = lax.psum_scatter(
+        partial_sums.reshape(2 * token_count, 2 * hidden_width), "col", scatter_dimension=0, tiled=True
+    ).astype(jnp.float32)
     share_rows = summed.shape[0]
     own_weight = lax.dynamic_slice_in_dim(
         route_weight.T.reshape(-1), lax.axis_index("col") * share_rows, share_rows, 0

time: 403 us -> 297 us (0.74)
  waiting for transfers between devices: 254 us -> 187 us
  local copies, waits for them, and re-layouts: 47.2 us -> 23.6 us
  starting transfers between devices: 26.7 us -> 16.4 us
  other arithmetic: 15.3 us -> 10.6 us
    all_to_all x2 -> x1, waiting for transfers between devices: 190 us -> 4.77 us  [sum_scatter_rows(): received = lax.all_to_all(pieces, axis_name, 0, 0, tiled=False)]
    reduce_scatter x0 -> x1, waiting for transfers between devices: none -> 120 us  [shards(): lax.psum_scatter(partial_sums.reshape(2 * token_count, 2 * hidden_width),...]
    another operation x1 -> x0, local copies, waits for them, and re-layouts: 15.7 us -> none  [sum_scatter_rows(): pieces = x.reshape((count, x.shape[0] // count) + x.shape[1:])]
    all_gather x1 -> x0, local copies, waits for them, and re-layouts: 8.54 us -> none  [shards(): lax.all_gather(hidden, 'col', axis=0, tiled=True)]
    all_to_all x2 -> x1, starting transfers between devices: 12.1 us -> 4.79 us  [sum_scatter_rows(): received = lax.all_to_all(pieces, axis_name, 0, 0, tiled=False)]
    reduce_sum x2 -> x1, other arithmetic: 6.88 us -> 0.72 us  [sum_scatter_rows(): return jnp.sum(received.astype(jnp.float32), axis=0)]
  transfers between devices with their start and end apart: 5 -> 5, of which waited for: 4 -> 4; matrix products, arithmetic and copies ran while one was open for 9% -> 9% of each run, Pallas kernels for 3% -> 4%
where the time goes in v5:
time: 297 us; the launch traced here: 296 us
  waiting for transfers between devices  187 us (63%)
  Pallas kernels  44.3 us (15%)
  local copies, waits for them, and re-layouts  23.6 us (8%)
  starting transfers between devices  16.4 us (6%)
  between operations  14.2 us (5%)
  other arithmetic  10.6 us (4%)
    reduce_scatter x1, waiting for transfers between devices, shards(): lax.psum_scatter(partial_sums.reshape(2 * token_count, 2 * hidden_width),...  120 us
    all_gather x1, waiting for transfers between devices, shards(): lax.all_gather(hidden, 'col', axis=0, tiled=True)  57.2 us
    pallas_call x1, Pallas kernels, gate_up(): pl.pallas_call(gate_up_kernel, grid=(token_count // tile,), in_specs=[pl....  31.4 us
    pallas_call x1, Pallas kernels, down(): pl.pallas_call(down_kernel, grid=(token_count // tile,), in_specs=[pl.Blo...  12.9 us
    unnamed x14, local copies, waits for them, and re-layouts  8.71 us
    all_to_all x1, starting transfers between devices, gather_rows(): received = lax.all_to_all(copies, axis_name, 0, 0, tiled=False)  6.36 us
  transfers between devices with their start and end apart: 5, of which 4 were waited for; matrix products, arithmetic and copies ran while one was open for 9% of the time, Pallas kernels for 4%

profile of v5, /device:TPU:1, one launch (start us, length us, event | category | flops | bytes accessed | tf_op | source)
XLA Modules:
  0.0 295.9 jit_solution(7688828345312352099)
XLA Ops:
  7.2 1.9 broadcast_in_dim.24
  9.1 6.4 %all-to-all-start = ((bf16[8,256,144]{1,2,0:T(8,128)(2,1)}), bf16[8,256,144]{1,2,0:T(8,128)(2,1)S(1)}, u32[]{:S(2)}, u32[]{:S(2)}) async-start(bf16[8,256,144]{1,2,0:T(8,128)(2,1)} %broadcast_in_dim.24), calls=%async_computation | async-start | bytes 1179648 | tf_op jit(solution)/shard_map/all_to_all | solution.py:87
  15.5 2.1 copy.38.ids_ref
  17.5 4.5 %pad_maximum_fusion.w_ref = bf16[8,144,1440]{2,1,0:T(8,128)(2,1)} fusion(bf16[8,144,720]{2,1,0:T(8,128)(2,1)S(1)} %copy-done.1, bf16[8,144,720]{2,1,0:T(8,128)(2,1)} %param.11), kind=kLoop, calls=%fused_computation.5 | loop fusion | flops 6635520 | bytes 6635520 | tf_op jit(solution)/shard_map/concatenate | solution.py:130
  22.0 4.4 %all-to-all-done = bf16[8,256,144]{1,2,0:T(8,128)(2,1)S(1)} async-done(((bf16[8,256,144]{1,2,0:T(8,128)(2,1)}), bf16[8,256,144]{1,2,0:T(8,128)(2,1)S(1)}, u32[]{:S(2)}, u32[]{:S(2)}) %all-to-all-start) | async-done | bytes 589856 | tf_op jit(solution)/shard_map/all_to_all | solution.py:87
  26.4 1.3 copy.36
  27.6 31.4 %shard_map.113 = bf16[2,2048,1440]{2,1,0:T(8,128)(2,1)} custom-call(s32[2048,2]{1,0:T(8,128)} %copy.38.ids_ref, bf16[2048,144]{1,0:T(8,128)(2,1)} %bitcast.24, bf16[8,144,1440]{2,1,0:T(8,128)(2,1)} %pad_maximum_fusion.w_ref), custom_call_target="tpu_custom_call" | custom-call | tf_op jit(solution)/shard_map/pallas_call | solution.py:71
  59.1 0.6 copy-done.3
  59.8 120.4 %reduce-scatter.2.cloned.1.call-done = bf16[256,1440]{1,0:T(8,128)(2,1)} async-done(((bf16[4096,1440]{1,0:T(8,128)(2,1)}), bf16[256,1440]{1,0:T(8,128)(2,1)}) %reduce-scatter.2.cloned.1.call-update) | async-done | bytes 737296 | tf_op jit(solution)/shard_map/reduce_scatter | solution.py:132
  180.2 1.3 convert_element_type.11
  181.5 1.1 fusion
  182.7 0.1 eq.35
  182.8 0.4 convert_reduce_fusion
  183.3 0.1 reshape.148
  183.4 0.6 constant_dynamic-slice_fusion.2
  184.0 1.4 scatter_custom_fusion.1
  185.4 0.6 scatter_custom_fusion
  186.1 0.7 iota_compare_fusion.1
  186.8 1.9 broadcast_select_fusion
  188.7 2.1 gather_fusion
  190.8 5.2 %all-to-all-start.2 = ((bf16[2,16,16,2304]{3,2,0,1:T(8,128)(2,1)}), bf16[2,16,16,2304]{3,2,0,1:T(8,128)(2,1)S(1)}, u32[]{:S(2)}, u32[]{:S(2)}) async-start(bf16[2,16,16,2304]{3,2,0,1:T(8,128)(2,1)} %bitcast.21), calls=%async_computation.3 | async-start | bytes 4718592 | tf_op jit(solution)/shard_map/all_to_all | solution.py:28
  195.9 4.4 %copy.39.d_ref = bf16[8,720,144]{2,1,0:T(8,128)(2,1)} copy(bf16[8,720,144]{1,2,0:T(8,128)(2,1)} %param.13) | data formatting | bytes 3317760 | tf_op args[3]
  200.3 57.2 %all-gather.2.cloned.1.call-done = bf16[4096,720]{1,0:T(8,128)(2,1)} async-done(((bf16[256,720]{1,0:T(8,128)(2,1)}), bf16[4096,720]{1,0:T(8,128)(2,1)}) %all-gather.2.cloned.1.call-update) | async-done | bytes 5898256 | tf_op jit(solution)/shard_map/all_gather | solution.py:142
  257.6 12.9 %shard_map.114 = bf16[2048,144]{1,0:T(8,128)(2,1)} custom-call(s32[2048,2]{1,0:T(8,128)} %copy.38.ids_ref, bf16[2,2048,720]{2,1,0:T(8,128)(2,1)} %bitcast.23, bf16[8,720,144]{2,1,0:T(8,128)(2,1)} %copy.39.d_ref), custom_call_target="tpu_custom_call" | custom-call | tf_op jit(solution)/shard_map/pallas_call | solution.py:101
  270.5 2.2 copy.40
  272.6 4.8 %all-to-all-start.1 = ((bf16[8,256,144]{1,2,0:T(8,128)(2,1)}), bf16[8,256,144]{1,2,0:T(8,128)(2,1)S(1)}, u32[]{:S(2)}, u32[]{:S(2)}) async-start(bf16[8,256,144]{1,2,0:T(8,128)(2,1)} %copy.40), calls=%async_computation.2 | async-start | bytes 1179648 | tf_op jit(solution)/shard_map/all_to_all | solution.py:94
  277.4 0.6 scatter_custom_fusion.2
  278.1 1.6 copy.42
  279.7 2.4 gather_fusion.1
  282.0 1.6 copy.44
  283.6 4.8 %all-to-all-done.1 = bf16[8,256,144]{1,2,0:T(8,128)(2,1)S(1)} async-done(((bf16[8,256,144]{1,2,0:T(8,128)(2,1)}), bf16[8,256,144]{1,2,0:T(8,128)(2,1)S(1)}, u32[]{:S(2)}, u32[]{:S(2)}) %all-to-all-start.1) | async-done | bytes 589856 | tf_op jit(solution)/shard_map/all_to_all | solution.py:94
  288.4 0.7 reduce_sum.21
  (28 shorter events, 0.4 us)
Async XLA Ops:
  7.2 176.2 %copy-start = (s32[1,16]{1,0:T(1,128)S(1)}, s32[1,16]{1,0:T(1,128)}, u32[]{:S(2)}) copy-start(s32[1,16]{1,0:T(1,128)} %param.19) | copy-start | bytes 196
  7.2 10.4 %copy-start.1 = (bf16[8,144,720]{2,1,0:T(8,128)(2,1)S(1)}, bf16[8,144,720]{2,1,0:T(8,128)(2,1)}, u32[]{:S(2)}) copy-start(bf16[8,144,720]{2,1,0:T(8,128)(2,1)} %param.12) | copy-start | bytes 4976644
  9.1 17.3 %all-to-all-start = ((bf16[8,256,144]{1,2,0:T(8,128)(2,1)}), bf16[8,256,144]{1,2,0:T(8,128)(2,1)S(1)}, u32[]{:S(2)}, u32[]{:S(2)}) async-start(bf16[8,256,144]{1,2,0:T(8,128)(2,1)} %broadcast_in_dim.24), calls=%async_computation | async-start | bytes 1179648 | tf_op jit(solution)/shard_map/all_to_all | solution.py:87
  15.4 164.8 %reduce-scatter.2.cloned.1.call-start = ((), (), s32[]{:S(2)}) async-start(), calls=%async_computation.4 | async-start | bytes 13369344 | tf_op jit(solution)/shard_map/reduce_scatter | solution.py:132
  59.0 0.7 copy-start.3
  59.0 198.5 %all-gather.2.cloned.1.call-start = ((), (), s32[]{:S(2)}) async-start(), calls=%async_computation.5 | async-start | bytes 6684672 | tf_op jit(solution)/shard_map/all_gather | solution.py:142
  59.8 122.9 %copy-start.2 = (s32[1,16,16]{2,1,0:T(8,128)S(1)}, s32[1,16,16]{2,1,0:T(8,128)}, u32[]{:S(2)}) copy-start(s32[1,16,16]{2,1,0:T(8,128)} %param.17) | copy-start | bytes 3076
  59.8 123.5 %copy-start.4 = (s32[1,16,16]{2,1,0:T(8,128)S(1)}, s32[1,16,16]{2,1,0:T(8,128)}, u32[]{:S(2)}) copy-start(s32[1,16,16]{2,1,0:T(8,128)} %param.18) | copy-start | bytes 3076
  190.8 81.9 %all-to-all-start.2 = ((bf16[2,16,16,2304]{3,2,0,1:T(8,128)(2,1)}), bf16[2,16,16,2304]{3,2,0,1:T(8,128)(2,1)S(1)}, u32[]{:S(2)}, u32[]{:S(2)}) async-start(bf16[2,16,16,2304]{3,2,0,1:T(8,128)(2,1)} %bitcast.21), calls=%async_computation.3 | async-start | bytes 4718592 | tf_op jit(solution)/shard_map/all_to_all | solution.py:28
  272.6 15.7 %all-to-all-start.1 = ((bf16[8,256,144]{1,2,0:T(8,128)(2,1)}), bf16[8,256,144]{1,2,0:T(8,128)(2,1)S(1)}, u32[]{:S(2)}, u32[]{:S(2)}) async-start(bf16[8,256,144]{1,2,0:T(8,128)(2,1)} %copy.40), calls=%async_computation.2 | async-start | bytes 1179648 | tf_op jit(solution)/shard_map/all_to_all | solution.py:94
Sparse Core Ops, SparseCore 0:
  59.2 121.0 reduce-scatter.1
  182.8 74.7 all-gather.1

commit v6 on v5

--- a/solution.py
+++ b/solution.py
@@ -128,10 +128,29 @@
     token_count = gathered.shape[0]
     hidden_width = gate_weight.shape[2]
     paired = jnp.concatenate([gate_weight, up_weight], axis=2)
-    partial_sums = gate_up(route_ids, gathered, paired, 256)
-    summed = lax.psum_scatter(
-        partial_sums.reshape(2 * token_count, 2 * hidden_width), "col", scatter_dimension=0, tiled=True
+    col_count = lax.axis_size("col")
+    share = 2 * token_count // col_count
+    lead = share * 5 // 8
+    blocks = token_count // share
+    tokens_by_block = gathered.reshape(blocks, share, gathered.shape[1])
+    ids_by_block = route_ids.reshape(blocks, share, 2)
+    lead_part = gate_up(
+        ids_by_block[:, :lead].reshape(-1, 2),
+        tokens_by_block[:, :lead].reshape(-1, gathered.shape[1]),
+        paired,
+        lead,
+    )
+    lead_sum = lax.psum_scatter(
+        lead_part.reshape(col_count * lead, 2 * hidden_width), "col", scatter_dimension=0, tiled=True
     ).astype(jnp.float32)
+    tail_part = gate_up(
+        ids_by_block[:, lead:].reshape(-1, 2),
+        tokens_by_block[:, lead:].reshape(-1, gathered.shape[1]),
+        paired,
+        share - lead,
+    )
+    tail_sum = sum_scatter_rows(tail_part.reshape(col_count * (share - lead), 2 * hidden_width), "col")
+    summed = jnp.concatenate([lead_sum, tail_sum], axis=0)
     share_rows = summed.shape[0]
     own_weight = lax.dynamic_slice_in_dim(
         route_weight.T.reshape(-1), lax.axis_index("col") * share_rows, share_rows, 0

time: 297 us -> 298 us (level)
  waiting for transfers between devices: 187 us -> 171 us
  starting transfers between devices: 16.4 us -> 25.3 us
  Pallas kernels: 44.3 us -> 48.5 us
    reduce_scatter x1, waiting for transfers between devices: 120 us -> 37.1 us  [shards(): lax.psum_scatter(lead_part.reshape(col_count * lead, 2 * hidden_width), '...]
    all_to_all x1 -> x2, waiting for transfers between devices: 4.77 us -> 72.4 us  [sum_scatter_rows(): received = lax.all_to_all(pieces, axis_name, 0, 0, tiled=False)]
    all_to_all x1 -> x2, starting transfers between devices: 4.79 us -> 13 us  [sum_scatter_rows(): received = lax.all_to_all(pieces, axis_name, 0, 0, tiled=False)]
    pallas_call x1 -> x2, Pallas kernels: 31.4 us -> 35.6 us  [gate_up(): pl.pallas_call(gate_up_kernel, grid=(token_count // tile,), in_specs=[pl....]
    slice x0 -> x5, local copies, waits for them, and re-layouts: none -> 4.02 us  [the longest x1 1.19 us: shards(): tokens_by_block[:, :lead].reshape(-1, gathered.shape[1])]
    reduce_sum x1 -> x2, other arithmetic: 0.72 us -> 3.8 us  [sum_scatter_rows(): return jnp.sum(received.astype(jnp.float32), axis=0)]
    unnamed x14 -> x16, local copies, waits for them, and re-layouts: 8.71 us -> 7.09 us
  transfers between devices with their start and end apart: 5 -> 6, of which waited for: 4 -> 5; matrix products, arithmetic and copies ran while one was open for 9% -> 11% of each run, Pallas kernels for 4% -> 9%
where the time goes in v6:
time: 298 us
  waiting for transfers between devices  171 us (57%)
  Pallas kernels  48.5 us (16%)
  starting transfers between devices  25.3 us (8%)
  local copies, waits for them, and re-layouts  24.8 us (8%)
  between operations  14.3 us (5%)
  other arithmetic  13.5 us (5%)
    all_to_all x2, waiting for transfers between devices, sum_scatter_rows(): received = lax.all_to_all(pieces, axis_name, 0, 0, tiled=False)  72.4 us
    all_gather x1, waiting for transfers between devices, shards(): lax.all_gather(hidden, 'col', axis=0, tiled=True)  57.2 us
    reduce_scatter x1, waiting for transfers between devices, shards(): lax.psum_scatter(lead_part.reshape(col_count * lead, 2 * hidden_width), '...  37.1 us
    pallas_call x2, Pallas kernels, gate_up(): pl.pallas_call(gate_up_kernel, grid=(token_count // tile,), in_specs=[pl....  35.6 us
    all_to_all x2, starting transfers between devices, sum_scatter_rows(): received = lax.all_to_all(pieces, axis_name, 0, 0, tiled=False)  13 us
    pallas_call x1, Pallas kernels, down(): pl.pallas_call(down_kernel, grid=(token_count // tile,), in_specs=[pl.Blo...  12.9 us
    unnamed x16, local copies, waits for them, and re-layouts  7.09 us
    all_to_all x1, starting transfers between devices, gather_rows(): received = lax.all_to_all(copies, axis_name, 0, 0, tiled=False)  6.36 us
  transfers between devices with their start and end apart: 6, of which 5 were waited for; matrix products, arithmetic and copies ran while one was open for 11% of the time, Pallas kernels for 9%

profile of v6, /device:TPU:1, one launch (start us, length us, event | category | flops | bytes accessed | tf_op | source)
XLA Modules:
  0.0 297.6 jit_solution(4322351695325224859)
XLA Ops:
  7.2 1.9 broadcast_in_dim.24
  9.1 6.4 %all-to-all-start = ((bf16[8,256,144]{1,2,0:T(8,128)(2,1)}), bf16[8,256,144]{1,2,0:T(8,128)(2,1)S(1)}, u32[]{:S(2)}, u32[]{:S(2)}) async-start(bf16[8,256,144]{1,2,0:T(8,128)(2,1)} %broadcast_in_dim.24), calls=%async_computation | async-start | bytes 1179648 | tf_op jit(solution)/shard_map/all_to_all | solution.py:87
  15.5 1.1 copy.45.ids_ref
  16.6 0.9 slice.32
  17.5 4.5 %pad_maximum_fusion.w_ref = bf16[8,144,1440]{2,1,0:T(8,128)(2,1)} fusion(bf16[8,144,720]{2,1,0:T(8,128)(2,1)S(1)} %copy-done.2, bf16[8,144,720]{2,1,0:T(8,128)(2,1)} %param.11), kind=kLoop, calls=%fused_computation.6 | loop fusion | flops 6635520 | bytes 6635520 | tf_op jit(solution)/shard_map/concatenate | solution.py:130
  22.0 4.4 %all-to-all-done = bf16[8,256,144]{1,2,0:T(8,128)(2,1)S(1)} async-done(((bf16[8,256,144]{1,2,0:T(8,128)(2,1)}), bf16[8,256,144]{1,2,0:T(8,128)(2,1)S(1)}, u32[]{:S(2)}, u32[]{:S(2)}) %all-to-all-start) | async-done | bytes 589856 | tf_op jit(solution)/shard_map/all_to_all | solution.py:87
  26.4 1.2 copy.42
  27.6 21.1 %shard_map.113 = bf16[2,1280,1440]{2,1,0:T(8,128)(2,1)} custom-call(s32[1280,2]{1,0:T(8,128)} %bitcast.35, bf16[1280,144]{1,0:T(8,128)(2,1)} %bitcast.36, bf16[8,144,1440]{2,1,0:T(8,128)(2,1)} %pad_maximum_fusion.w_ref), custom_call_target="tpu_custom_call" | custom-call | tf_op jit(solution)/shard_map/pallas_call | solution.py:71
  48.7 0.8 slice.34
  49.6 1.0 copy.44
  50.6 14.5 %shard_map.114 = bf16[2,768,1440]{2,1,0:T(8,128)(2,1)} custom-call(s32[768,2]{1,0:T(8,128)} %bitcast.37, bf16[768,144]{1,0:T(8,128)(2,1)} %bitcast.38, bf16[8,144,1440]{2,1,0:T(8,128)(2,1)} %pad_maximum_fusion.w_ref), custom_call_target="tpu_custom_call" | custom-call | tf_op jit(solution)/shard_map/pallas_call | solution.py:71
  65.1 8.3 %all-to-all-start.1 = ((bf16[16,96,1440]{2,1,0:T(8,128)(2,1)}), bf16[16,96,1440]{2,1,0:T(8,128)(2,1)}, u32[]{:S(2)}, u32[]{:S(2)}) async-start(bf16[16,96,1440]{2,1,0:T(8,128)(2,1)} %bitcast.27), calls=%async_computation.2 | async-start | bytes 9437184 | tf_op jit(solution)/shard_map/all_to_all | solution.py:94
  73.5 67.6 %all-to-all-done.1 = bf16[16,96,1440]{2,1,0:T(8,128)(2,1)} async-done(((bf16[16,96,1440]{2,1,0:T(8,128)(2,1)}), bf16[16,96,1440]{2,1,0:T(8,128)(2,1)}, u32[]{:S(2)}, u32[]{:S(2)}) %all-to-all-start.1) | async-done | bytes 4423712 | tf_op jit(solution)/shard_map/all_to_all | solution.py:94
  141.2 3.1 %convert_reduce_fusion = f32[96,1440]{1,0:T(8,128)S(1)} fusion(bf16[16,96,1440]{2,1,0:T(8,128)(2,1)} %all-to-all-done.1), kind=kLoop, calls=%fused_computation.5 | loop fusion | flops 4285440 | bytes 4976640 | tf_op jit(solution)/shard_map/reduce_sum | solution.py:95
  144.3 37.1 %reduce-scatter.2.cloned.1.call-done = bf16[160,1440]{1,0:T(8,128)(2,1)} async-done(((bf16[2560,1440]{1,0:T(8,128)(2,1)}), bf16[160,1440]{1,0:T(8,128)(2,1)}) %reduce-scatter.2.cloned.1.call-update) | async-done | bytes 460816 | tf_op jit(solution)/shard_map/reduce_scatter | solution.py:143
  181.4 1.1 convert_element_type.14
  182.5 1.1 fusion.2
  185.0 1.4 scatter_custom_fusion.1
  187.0 0.7 iota_compare_fusion.1
  187.7 1.9 broadcast_select_fusion
  189.6 2.1 gather_fusion
  191.7 5.8 %all-to-all-start.3 = ((bf16[2,16,16,2304]{3,2,0,1:T(8,128)(2,1)}), bf16[2,16,16,2304]{3,2,0,1:T(8,128)(2,1)S(1)}, u32[]{:S(2)}, u32[]{:S(2)}) async-start(bf16[2,16,16,2304]{3,2,0,1:T(8,128)(2,1)} %bitcast.28), calls=%async_computation.4 | async-start | bytes 4718592 | tf_op jit(solution)/shard_map/all_to_all | solution.py:28
  197.6 4.4 %copy.46.d_ref = bf16[8,720,144]{2,1,0:T(8,128)(2,1)} copy(bf16[8,720,144]{1,2,0:T(8,128)(2,1)} %param.13) | data formatting | bytes 3317760 | tf_op args[3]
  202.0 57.2 %all-gather.2.cloned.1.call-done = bf16[4096,720]{1,0:T(8,128)(2,1)} async-done(((bf16[256,720]{1,0:T(8,128)(2,1)}), bf16[4096,720]{1,0:T(8,128)(2,1)}) %all-gather.2.cloned.1.call-update) | async-done | bytes 5898256 | tf_op jit(solution)/shard_map/all_gather | solution.py:161
  259.2 12.9 %shard_map.115 = bf16[2048,144]{1,0:T(8,128)(2,1)} custom-call(s32[2048,2]{1,0:T(8,128)} %copy-done.1, bf16[2,2048,720]{2,1,0:T(8,128)(2,1)} %bitcast.32, bf16[8,720,144]{2,1,0:T(8,128)(2,1)} %copy.46.d_ref), custom_call_target="tpu_custom_call" | custom-call | tf_op jit(solution)/shard_map/pallas_call | solution.py:101
  272.1 2.2 copy.47
  274.3 4.7 %all-to-all-start.2 = ((bf16[8,256,144]{1,2,0:T(8,128)(2,1)}), bf16[8,256,144]{1,2,0:T(8,128)(2,1)S(1)}, u32[]{:S(2)}, u32[]{:S(2)}) async-start(bf16[8,256,144]{1,2,0:T(8,128)(2,1)} %copy.47), calls=%async_computation.3 | async-start | bytes 1179648 | tf_op jit(solution)/shard_map/all_to_all | solution.py:94
  279.7 1.6 copy.49
  281.3 2.4 gather_fusion.1
  283.7 1.6 copy.51
  285.2 4.8 %all-to-all-done.2 = bf16[8,256,144]{1,2,0:T(8,128)(2,1)S(1)} async-done(((bf16[8,256,144]{1,2,0:T(8,128)(2,1)}), bf16[8,256,144]{1,2,0:T(8,128)(2,1)S(1)}, u32[]{:S(2)}, u32[]{:S(2)}) %all-to-all-start.2) | async-done | bytes 589856 | tf_op jit(solution)/shard_map/all_to_all | solution.py:94
  290.0 0.7 reduce_sum.31
  (38 shorter events, 2.9 us)
Async XLA Ops:
  7.2 177.2 %copy-start = (s32[1,16]{1,0:T(1,128)S(1)}, s32[1,16]{1,0:T(1,128)}, u32[]{:S(2)}) copy-start(s32[1,16]{1,0:T(1,128)} %param.19) | copy-start | bytes 196
  7.2 10.3 %copy-start.2 = (bf16[8,144,720]{2,1,0:T(8,128)(2,1)S(1)}, bf16[8,144,720]{2,1,0:T(8,128)(2,1)}, u32[]{:S(2)}) copy-start(bf16[8,144,720]{2,1,0:T(8,128)(2,1)} %param.12) | copy-start | bytes 4976644
  9.1 17.3 %all-to-all-start = ((bf16[8,256,144]{1,2,0:T(8,128)(2,1)}), bf16[8,256,144]{1,2,0:T(8,128)(2,1)S(1)}, u32[]{:S(2)}, u32[]{:S(2)}) async-start(bf16[8,256,144]{1,2,0:T(8,128)(2,1)} %broadcast_in_dim.24), calls=%async_computation | async-start | bytes 1179648 | tf_op jit(solution)/shard_map/all_to_all | solution.py:87
  15.4 165.9 %reduce-scatter.2.cloned.1.call-start = ((), (), s32[]{:S(2)}) async-start(), calls=%async_computation.5 | async-start | bytes 8355840 | tf_op jit(solution)/shard_map/reduce_scatter | solution.py:143
  16.6 32.1 %copy-start.1 = (s32[2048,2]{1,0:T(8,128)}, s32[2048,2]{1,0:T(8,128)S(1)}, u32[]{:S(2)}) copy-start(s32[2048,2]{1,0:T(8,128)S(1)} %copy.45.ids_ref) | copy-start | bytes 49156
  65.1 8.3 %copy-start.4 = (f32[2048,2]{0,1:T(2,128)S(1)}, f32[2048,2]{0,1:T(2,128)}, u32[]{:S(2)}) copy-start(f32[2048,2]{0,1:T(2,128)} %param.15) | copy-start | bytes 49156
  65.1 76.0 %all-to-all-start.1 = ((bf16[16,96,1440]{2,1,0:T(8,128)(2,1)}), bf16[16,96,1440]{2,1,0:T(8,128)(2,1)}, u32[]{:S(2)}, u32[]{:S(2)}) async-start(bf16[16,96,1440]{2,1,0:T(8,128)(2,1)} %bitcast.27), calls=%async_computation.2 | async-start | bytes 9437184 | tf_op jit(solution)/shard_map/all_to_all | solution.py:94
  73.4 185.8 %all-gather.2.cloned.1.call-start = ((), (), s32[]{:S(2)}) async-start(), calls=%async_computation.6 | async-start | bytes 6684672 | tf_op jit(solution)/shard_map/all_gather | solution.py:161
  144.2 39.4 %copy-start.3 = (s32[1,16,16]{2,1,0:T(8,128)S(1)}, s32[1,16,16]{2,1,0:T(8,128)}, u32[]{:S(2)}) copy-start(s32[1,16,16]{2,1,0:T(8,128)} %param.17) | copy-start | bytes 3076
  144.3 40.0 %copy-start.5 = (s32[1,16,16]{2,1,0:T(8,128)S(1)}, s32[1,16,16]{2,1,0:T(8,128)}, u32[]{:S(2)}) copy-start(s32[1,16,16]{2,1,0:T(8,128)} %param.18) | copy-start | bytes 3076
  191.7 82.6 %all-to-all-start.3 = ((bf16[2,16,16,2304]{3,2,0,1:T(8,128)(2,1)}), bf16[2,16,16,2304]{3,2,0,1:T(8,128)(2,1)S(1)}, u32[]{:S(2)}, u32[]{:S(2)}) async-start(bf16[2,16,16,2304]{3,2,0,1:T(8,128)(2,1)} %bitcast.28), calls=%async_computation.4 | async-start | bytes 4718592 | tf_op jit(solution)/shard_map/all_to_all | solution.py:28
  274.3 15.7 %all-to-all-start.2 = ((bf16[8,256,144]{1,2,0:T(8,128)(2,1)}), bf16[8,256,144]{1,2,0:T(8,128)(2,1)S(1)}, u32[]{:S(2)}, u32[]{:S(2)}) async-start(bf16[8,256,144]{1,2,0:T(8,128)(2,1)} %copy.47), calls=%async_computation.3 | async-start | bytes 1179648 | tf_op jit(solution)/shard_map/all_to_all | solution.py:94
Sparse Core Ops, SparseCore 0:
  48.8 132.4 reduce-scatter.1
  183.8 75.3 all-gather.1

commit v7 on v3

--- a/solution.py
+++ b/solution.py
@@ -109,6 +109,77 @@
         out_specs=pl.BlockSpec((tile, width), lambda i: (i, 0)),
         out_shape=jax.ShapeDtypeStruct((token_count, width), jnp.bfloat16),
     )(route_ids, hidden_all, down_weight)
+
+
+def col_perm(axis_name, move):
+    count = lax.axis_size(axis_name)
+    return [(c, move(c)) for c in range(count)]
+
+
+def x_step(c, step):
+    return ((c // 4 + step) % 4) * 4 + c % 4
+
+
+def pick(chunks, index, axis=0):
+    return lax.dynamic_index_in_dim(chunks, index, axis, keepdims=False)
+
+
+def ring_reduce(chunks, xi, axis_name, direction):
+    count = chunks.shape[0]
+    perm = col_perm(axis_name, lambda c: x_step(c, direction))
+    cur = pick(chunks, (xi - direction) % count)
+    for s in range(1, count):
+        recv = lax.ppermute(cur, axis_name, perm)
+        cur = recv.astype(jnp.float32) + pick(chunks, (xi - direction * (s + 1)) % count).astype(
+            jnp.float32
+        )
+        if s < count - 1:
+            cur = cur.astype(chunks.dtype)
+    return cur
+
+
+def ring_gather(block, xi, axis_name, direction, count):
+    perm = col_perm(axis_name, lambda c: x_step(c, direction))
+    out = jnp.zeros((count,) + block.shape, block.dtype)
+    out = lax.dynamic_update_index_in_dim(out, block, xi, 0)
+    cur = block
+    for s in range(1, count):
+        cur = lax.ppermute(cur, axis_name, perm)
+        out = lax.dynamic_update_index_in_dim(out, cur, (xi - direction * s) % count, 0)
+    return out
+
+
+def col_reduce_scatter(partial, axis_name):
+    c = lax.axis_index(axis_name)
+    xi, zi, co = c // 4, (c // 2) % 2, c % 2
+    rows = partial.shape[0] // 16
+    blocks = partial.reshape(4, 2, 2, rows, partial.shape[1])
+    recv = lax.ppermute(pick(blocks, 1 - co, 2), axis_name, col_perm(axis_name, lambda q: q ^ 1))
+    core_sum = (pick(blocks, co, 2).astype(jnp.float32) + recv.astype(jnp.float32)).astype(
+        partial.dtype
+    )
+    half = rows // 2
+    plus = ring_reduce(core_sum[:, :, :half], xi, axis_name, 1)
+    minus = ring_reduce(core_sum[:, :, half:], xi, axis_name, -1)
+    x_sum = jnp.concatenate([plus, minus], axis=1)
+    recv = lax.ppermute(
+        pick(x_sum, 1 - zi).astype(partial.dtype), axis_name, col_perm(axis_name, lambda q: q ^ 2)
+    )
+    return pick(x_sum, zi) + recv.astype(jnp.float32)
+
+
+def col_all_gather(block, axis_name):
+    c = lax.axis_index(axis_name)
+    xi, zi, co = c // 4, (c // 2) % 2, c % 2
+    recv = lax.ppermute(block, axis_name, col_perm(axis_name, lambda q: q ^ 2))
+    z_pair = jnp.where(zi == 0, jnp.stack([block, recv]), jnp.stack([recv, block]))
+    half = block.shape[0] // 2
+    plus = ring_gather(z_pair[:, :half], xi, axis_name, 1, 4)
+    minus = ring_gather(z_pair[:, half:], xi, axis_name, -1, 4)
+    x_all = jnp.concatenate([plus, minus], axis=2)
+    recv = lax.ppermute(x_all, axis_name, col_perm(axis_name, lambda q: q ^ 1))
+    full = jnp.where(co == 0, jnp.stack([x_all, recv], axis=2), jnp.stack([recv, x_all], axis=2))
+    return full.reshape((-1,) + block.shape[1:])
 
 
 def shards(
@@ -129,7 +200,7 @@
     hidden_width = gate_weight.shape[2]
     paired = jnp.concatenate([gate_weight, up_weight], axis=2)
     partial_sums = gate_up(route_ids, gathered, paired, 256)
-    summed = sum_scatter_rows(partial_sums.reshape(2 * token_count, 2 * hidden_width), "col")
+    summed = col_reduce_scatter(partial_sums.reshape(2 * token_count, 2 * hidden_width), "col")
     share_rows = summed.shape[0]
     own_weight = lax.dynamic_slice_in_dim(
         route_weight.T.reshape(-1), lax.axis_index("col") * share_rows, share_rows, 0
@@ -137,7 +208,7 @@
     hidden = (
         own_weight[:, None] * jax.nn.silu(summed[:, :hidden_width]) * summed[:, hidden_width:]
     ).astype(jnp.bfloat16)
-    hidden_all = lax.all_gather(hidden, "col", axis=0, tiled=True).reshape(
+    hidden_all = col_all_gather(hidden, "col").reshape(
         2, token_count, hidden_width
     )
     per_token = down(route_ids, hidden_all, down_weight, 256)

time: 403 us -> 293 us (0.73)
  waiting for transfers between devices: 254 us -> 87.7 us
  starting transfers between devices: 26.7 us -> 51.1 us
  other arithmetic: 15.3 us -> 39.1 us
  local copies, waits for them, and re-layouts: 47.2 us -> 67.9 us
  between operations: 14.2 us -> 0.93 us
    all_to_all x2 -> x1, waiting for transfers between devices: 190 us -> 3 us  [sum_scatter_rows(): received = lax.all_to_all(pieces, axis_name, 0, 0, tiled=False)]
    ppermute x0 -> x16, waiting for transfers between devices: none -> 80.3 us  [the longest x6 43.3 us: ring_reduce(): recv = lax.ppermute(cur, axis_name, perm)]
    all_gather x1 -> x0, waiting for transfers between devices: 59.6 us -> none  [shards(): lax.all_gather(hidden, 'col', axis=0, tiled=True)]
    ppermute x0 -> x16, starting transfers between devices: none -> 32.9 us  [the longest x6 9.31 us: ring_reduce(): recv = lax.ppermute(cur, axis_name, perm)]
    dynamic_slice x0 -> x2, local copies, waits for them, and re-layouts: none -> 18.8 us  [pick(): return lax.dynamic_index_in_dim(chunks, index, axis, keepdims=False)]
    convert_element_type x0 -> x6, other arithmetic: none -> 15.9 us  [the longest x4 9.16 us: ring_reduce(): cur = cur.astype(chunks.dtype)]
    another operation x1 -> x2, local copies, waits for them, and re-layouts: 15.7 us -> 0.38 us  [sum_scatter_rows(): pieces = x.reshape((count, x.shape[0] // count) + x.shape[1:])]
    unnamed x14 -> x21, local copies, waits for them, and re-layouts: 8.11 us -> 19.9 us
  transfers between devices with their start and end apart: 5 -> 19, of which waited for: 4 -> 13; matrix products, arithmetic and copies ran while one was open for 9% -> 23% of each run, Pallas kernels for 3% -> 4%
where the time goes in v7:
time: 293 us; the launch traced here: 291 us
  waiting for transfers between devices  87.7 us (30%)
  local copies, waits for them, and re-layouts  67.9 us (23%)
  starting transfers between devices  51.1 us (17%)
  Pallas kernels  44.3 us (15%)
  other arithmetic  39.1 us (13%)
    ppermute x6, waiting for transfers between devices, ring_reduce(): recv = lax.ppermute(cur, axis_name, perm)  43.3 us
    pallas_call x1, Pallas kernels, gate_up(): pl.pallas_call(gate_up_kernel, grid=(token_count // tile,), in_specs=[pl....  31.4 us
    unnamed x21, local copies, waits for them, and re-layouts  19.9 us
    dynamic_slice x2, local copies, waits for them, and re-layouts, pick(): return lax.dynamic_index_in_dim(chunks, index, axis, keepdims=False)  18.8 us
    ppermute x6, waiting for transfers between devices, ring_gather(): cur = lax.ppermute(cur, axis_name, perm)  18.4 us
    pallas_call x1, Pallas kernels, down(): pl.pallas_call(down_kernel, grid=(token_count // tile,), in_specs=[pl.Blo...  12.9 us
    ppermute x1, waiting for transfers between devices, col_reduce_scatter(): lax.ppermute(pick(x_sum, 1 - zi).astype(partial.dtype), axis_name, col_pe...  12.6 us
    ppermute x6, starting transfers between devices, ring_reduce(): recv = lax.ppermute(cur, axis_name, perm)  9.31 us
  transfers between devices with their start and end apart: 19, of which 13 were waited for; matrix products, arithmetic and copies ran while one was open for 23% of the time, Pallas kernels for 4%

profile of v7, /device:TPU:1, one launch (start us, length us, event | category | flops | bytes accessed | tf_op | source)
XLA Modules:
  0.0 291.0 jit_solution(15239506695094276062)
XLA Ops:
  2.5 6.4 %all-to-all-start = ((bf16[8,256,144]{1,2,0:T(8,128)(2,1)}), bf16[8,256,144]{1,2,0:T(8,128)(2,1)S(1)}, u32[]{:S(2)}, u32[]{:S(2)}) async-start(bf16[8,256,144]{1,2,0:T(8,128)(2,1)} %broadcast_in_dim.64), calls=%async_computation | async-start | bytes 1179648 | tf_op jit(solution)/shard_map/all_to_all | solution.py:87
  11.0 4.4 %pad_maximum_fusion.w_ref = bf16[8,144,1440]{2,1,0:T(8,128)(2,1)} fusion(bf16[8,144,720]{2,1,0:T(8,128)(2,1)S(1)} %copy-done.4, bf16[8,144,720]{2,1,0:T(8,128)(2,1)} %param.11), kind=kLoop, calls=%fused_computation.8 | loop fusion | flops 6635520 | bytes 6635520 | tf_op jit(solution)/shard_map/concatenate | solution.py:201
  15.5 4.4 %all-to-all-done = bf16[8,256,144]{1,2,0:T(8,128)(2,1)S(1)} async-done(((bf16[8,256,144]{1,2,0:T(8,128)(2,1)}), bf16[8,256,144]{1,2,0:T(8,128)(2,1)S(1)}, u32[]{:S(2)}, u32[]{:S(2)}) %all-to-all-start) | async-done | bytes 589856 | tf_op jit(solution)/shard_map/all_to_all | solution.py:87
  21.1 31.4 %shard_map.113 = bf16[2,2048,1440]{2,1,0:T(8,128)(2,1)} custom-call(s32[2048,2]{1,0:T(8,128)} %copy.47.ids_ref, bf16[2048,144]{1,0:T(8,128)(2,1)} %bitcast.77, bf16[8,144,1440]{2,1,0:T(8,128)(2,1)} %pad_maximum_fusion.w_ref), custom_call_target="tpu_custom_call" | custom-call | tf_op jit(solution)/shard_map/pallas_call | solution.py:71
  52.5 10.2 %constant_dynamic-slice_fusion.4 = (bf16[4,2,1,256,1440]{4,3,2,1,0:T(8,128)(2,1)}, bf16[4,2,1,256,1440]{4,3,2,1,0:T(8,128)(2,1)}) fusion(bf16[4,2,2,256,1440]{4,3,2,1,0:T(8,128)(2,1)} %bitcast.72, s32[]{:T(128)S(6)} %select_n.198, s32[]{:T(128)S(6)} %select_n.199), kind=kLoop, calls=%fused_computation.51 | loop fusion | bytes 23592968 | tf_op jit(solution)/shard_map/jit(dynamic_index_in_dim)/dynamic_slice | solution.py:124
  62.7 8.6 %copy.45 = bf16[4,2,1,256,1440]{3,4,1,0,2:T(8,128)(2,1)} copy(bf16[4,2,1,256,1440]{4,3,2,1,0:T(8,128)(2,1)} %get-tuple-element.11) | data formatting | bytes 11796480 | tf_op jit(solution)/shard_map/jit(dynamic_index_in_dim)/dynamic_slice | solution.py:124
  72.1 8.5 %copy.55 = bf16[4,2,1,256,1440]{3,4,1,0,2:T(8,128)(2,1)} copy(bf16[4,2,1,256,1440]{4,3,2,1,0:T(8,128)(2,1)} %get-tuple-element.10) | data formatting | bytes 11796480
  81.6 5.8 %fusion = bf16[4,2,256,1440]{2,3,1,0:T(8,128)(2,1)S(1)} fusion(bf16[4,2,256,1440]{2,3,1,0:T(8,128)(2,1)} %collective-permute-done, bf16[4,2,1,256,1440]{3,4,1,0,2:T(8,128)(2,1)} %copy.55), kind=kLoop, calls=%fused_computation.6 | loop fusion | flops 11796480 | bytes 17694720 | tf_op jit(solution)/shard_map/convert_element_type | solution.py:158
  94.6 14.9 %collective-permute-done.4 = bf16[2,128,1440]{1,2,0:T(8,128)(2,1)} collective-permute-done((bf16[2,128,1440]{1,2,0:T(8,128)(2,1)}, bf16[2,128,1440]{1,2,0:T(8,128)(2,1)}, u32[]{:S(2)}, u32[]{:S(2)}) %collective-permute-start.4) | collective-permute-done | bytes 737312 | tf_op jit(solution)/shard_map/ppermute | solution.py:132
  111.9 3.4 %collective-permute-start.5 = (bf16[2,128,1440]{1,2,0:T(8,128)(2,1)}, bf16[2,128,1440]{1,2,0:T(8,128)(2,1)}, u32[]{:S(2)}, u32[]{:S(2)}) collective-permute-start(bf16[2,128,1440]{1,2,0:T(8,128)(2,1)} %fusion.7), channel_id=1, source_target_pairs={{0,12},{1,13},{2,14},{3,15},{4,0},{5,1},{6,2},{7,3},{8,4},{9,5},{1... | collective-permute-start | bytes 2211848 | tf_op jit(solution)/shard_map/ppermute | solution.py:132
  117.5 12.7 %collective-permute-done.5 = bf16[2,128,1440]{1,2,0:T(8,128)(2,1)} collective-permute-done((bf16[2,128,1440]{1,2,0:T(8,128)(2,1)}, bf16[2,128,1440]{1,2,0:T(8,128)(2,1)}, u32[]{:S(2)}, u32[]{:S(2)}) %collective-permute-start.5) | collective-permute-done | bytes 737312 | tf_op jit(solution)/shard_map/ppermute | solution.py:132
  132.6 3.4 %collective-permute-start.6 = (bf16[2,128,1440]{1,2,0:T(8,128)(2,1)}, bf16[2,128,1440]{1,2,0:T(8,128)(2,1)}, u32[]{:S(2)}, u32[]{:S(2)}) collective-permute-start(bf16[2,128,1440]{1,2,0:T(8,128)(2,1)} %fusion.6), channel_id=1, source_target_pairs={{0,12},{1,13},{2,14},{3,15},{4,0},{5,1},{6,2},{7,3},{8,4},{9,5},{1... | collective-permute-start | bytes 2211848 | tf_op jit(solution)/shard_map/ppermute | solution.py:132
  138.2 11.9 %collective-permute-done.6 = bf16[2,128,1440]{1,2,0:T(8,128)(2,1)} collective-permute-done((bf16[2,128,1440]{1,2,0:T(8,128)(2,1)}, bf16[2,128,1440]{1,2,0:T(8,128)(2,1)}, u32[]{:S(2)}, u32[]{:S(2)}) %collective-permute-start.6) | collective-permute-done | bytes 737312 | tf_op jit(solution)/shard_map/ppermute | solution.py:132
  151.6 3.8 %collective-permute-done.3 = bf16[2,128,1440]{1,2,0:T(8,128)(2,1)} collective-permute-done((bf16[2,128,1440]{1,2,0:T(8,128)(2,1)}, bf16[2,128,1440]{1,2,0:T(8,128)(2,1)}, u32[]{:S(2)}, u32[]{:S(2)}) %collective-permute-start.3) | collective-permute-done | bytes 737312 | tf_op jit(solution)/shard_map/ppermute | solution.py:132
  157.9 3.3 %collective-permute-start.7 = (bf16[256,1440]{0,1:T(8,128)(2,1)}, bf16[256,1440]{0,1:T(8,128)(2,1)}, u32[]{:S(2)}, u32[]{:S(2)}) collective-permute-start(bf16[256,1440]{0,1:T(8,128)(2,1)} %fusion.10), channel_id=1, source_target_pairs={{0,2},{1,3},{2,0},{3,1},{4,6},{5,7},{6,4},{7,5},{8,10},{9,11},{10,... | collective-permute-start | bytes 2211848 | tf_op jit(solution)/shard_map/ppermute | solution.py:165
  162.6 12.6 %collective-permute-done.7 = bf16[256,1440]{0,1:T(8,128)(2,1)} collective-permute-done((bf16[256,1440]{0,1:T(8,128)(2,1)}, bf16[256,1440]{0,1:T(8,128)(2,1)}, u32[]{:S(2)}, u32[]{:S(2)}) %collective-permute-start.7) | collective-permute-done | bytes 737312 | tf_op jit(solution)/shard_map/ppermute | solution.py:165
  179.7 4.9 %collective-permute-done.8 = bf16[256,720]{0,1:T(8,128)(2,1)S(1)} collective-permute-done((bf16[256,720]{0,1:T(8,128)(2,1)S(1)}, bf16[256,720]{0,1:T(8,128)(2,1)S(1)}, u32[]{:S(2)}, u32[]{:S(2)}) %collective-permute-start.8) | collective-permute-done | bytes 368672 | tf_op jit(solution)/shard_map/ppermute | solution.py:174
  188.2 4.4 %collective-permute-done.9 = bf16[2,128,720]{1,2,0:T(8,128)(2,1)S(1)} collective-permute-done((bf16[2,128,720]{1,2,0:T(8,128)(2,1)S(1)}, bf16[2,128,720]{1,2,0:T(8,128)(2,1)S(1)}, u32[]{:S(2)}, u32[]{:S(2)}) %collective-permute-start.9) | collective-permute-done | bytes 368672 | tf_op jit(solution)/shard_map/ppermute | solution.py:147
  195.4 6.6 %collective-permute-done.10 = bf16[2,128,720]{1,2,0:T(8,128)(2,1)S(1)} collective-permute-done((bf16[2,128,720]{1,2,0:T(8,128)(2,1)S(1)}, bf16[2,128,720]{1,2,0:T(8,128)(2,1)S(1)}, u32[]{:S(2)}, u32[]{:S(2)}) %collective-permute-start.10) | collective-permute-done | bytes 368672 | tf_op jit(solution)/shard_map/ppermute | solution.py:147
  201.9 3.0 %collective-permute-start.14 = (bf16[2,128,720]{1,2,0:T(8,128)(2,1)S(1)}, bf16[2,128,720]{1,2,0:T(8,128)(2,1)S(1)}, u32[]{:S(2)}, u32[]{:S(2)}) collective-permute-start(bf16[2,128,720]{1,2,0:T(8,128)(2,1)S(1)} %collective-permute-done.13), channel_id=1, source_target_pairs={{0,12},{1,13},{2,14},{3,15},{4,0},{5,1},{6,2},{7,3},{8,4},{9,5},{1... | collective-permute-start | bytes 1105928 | tf_op jit(solution)/shard_map/ppermute | solution.py:147
  205.0 7.4 %collective-permute-done.11 = bf16[2,128,720]{1,2,0:T(8,128)(2,1)S(1)} collective-permute-done((bf16[2,128,720]{1,2,0:T(8,128)(2,1)S(1)}, bf16[2,128,720]{1,2,0:T(8,128)(2,1)S(1)}, u32[]{:S(2)}, u32[]{:S(2)}) %collective-permute-start.11) | collective-permute-done | bytes 368672 | tf_op jit(solution)/shard_map/ppermute | solution.py:147
  214.7 8.4 %collective-permute-start.15 = (bf16[4,2,256,720]{2,3,1,0:T(8,128)(2,1)}, bf16[4,2,256,720]{2,3,1,0:T(8,128)(2,1)}, u32[]{:S(2)}, u32[]{:S(2)}) collective-permute-start(bf16[4,2,256,720]{2,3,1,0:T(8,128)(2,1)} %get-tuple-element.15), channel_id=1, source_target_pairs={{0,1},{1,0},{2,3},{3,2},{4,5},{5,4},{6,7},{7,6},{8,9},{9,8},{10,11... | collective-permute-start | bytes 8847368 | tf_op jit(solution)/shard_map/ppermute | solution.py:180
  225.8 3.3 %broadcast_select_fusion = bf16[2,16,16,2304]{3,2,1,0:T(8,128)(2,1)} fusion(bf16[2,16,16,2304]{3,2,1,0:T(8,128)(2,1)} %param.16, pred[16]{0:T(512)(128)(4,1)S(1)} %iota_compare_fusion.1), kind=kLoop, calls=%fused_computation.14 | loop fusion | flops 1179648 | bytes 4718608 | tf_op jit(solution)/shard_map/jit(_where)/select_n | solution.py:25
  229.1 3.8 %gather_fusion = bf16[16,2,16,2304]{3,2,1,0:T(8,128)(2,1)} fusion(bf16[2,16,16,2304]{3,2,1,0:T(8,128)(2,1)} %broadcast_select_fusion, s32[1024]{0:T(1024)S(1)} %pad_clamp_fusion.1), kind=kCustom, calls=%fused_computation | custom fusion | bytes 4718656 | tf_op jit(solution)/shard_map/gather | solution.py:29
  232.9 8.3 %all-to-all-start.2 = ((bf16[2,16,16,2304]{3,2,0,1:T(8,128)(2,1)}), bf16[2,16,16,2304]{3,2,0,1:T(8,128)(2,1)}, u32[]{:S(2)}, u32[]{:S(2)}) async-start(bf16[2,16,16,2304]{3,2,0,1:T(8,128)(2,1)} %bitcast.74), calls=%async_computation.2 | async-start | bytes 4718592 | tf_op jit(solution)/shard_map/all_to_all | solution.py:28
  241.2 4.4 %copy.48.d_ref = bf16[8,720,144]{2,1,0:T(8,128)(2,1)} copy(bf16[8,720,144]{1,2,0:T(8,128)(2,1)} %param.13) | data formatting | bytes 3317760 | tf_op args[3]
  245.6 6.6 %maximum_select_fusion = bf16[4,2,2,256,720]{3,4,1,0,2:T(8,128)(2,1)} fusion(bf16[4,2,1,256,720]{3,4,1,0,2:T(8,128)(2,1)} %bitcast.26, bf16[4,2,1,256,720]{3,4,1,0,2:T(8,128)(2,1)S(1)} %get-tuple-element.14, pred[]{:T(512)S(6)} %eq.55), kind=kLoop, calls=%fused_computation.7 | loop fusion | flops 8847360 | bytes 11796481 | tf_op jit(solution)/shard_map/jit(_where)/select_n | solution.py:181
  252.2 8.6 %copy.46 = bf16[4,2,2,256,720]{4,3,2,1,0:T(8,128)(2,1)} copy(bf16[4,2,2,256,720]{3,4,1,0,2:T(8,128)(2,1)} %maximum_select_fusion) | data formatting | bytes 11796480 | tf_op jit(solution)/shard_map/jit(_where)/select_n | solution.py:181
  260.8 12.9 %shard_map.114 = bf16[2048,144]{1,0:T(8,128)(2,1)} custom-call(s32[2048,2]{1,0:T(8,128)} %copy.47.ids_ref, bf16[2,2048,720]{2,1,0:T(8,128)(2,1)} %bitcast.73, bf16[8,720,144]{2,1,0:T(8,128)(2,1)} %copy.48.d_ref), custom_call_target="tpu_custom_call" | custom-call | tf_op jit(solution)/shard_map/pallas_call | solution.py:101
  275.9 3.5 %all-to-all-start.1 = ((bf16[8,256,144]{1,2,0:T(8,128)(2,1)}), bf16[8,256,144]{1,2,0:T(8,128)(2,1)S(1)}, u32[]{:S(2)}, u32[]{:S(2)}) async-start(bf16[8,256,144]{1,2,0:T(8,128)(2,1)} %copy.49), calls=%async_computation.1 | async-start | bytes 1179648 | tf_op jit(solution)/shard_map/all_to_all | solution.py:94
  284.0 3.3 %copy.53 = bf16[2,16,16,2304]{3,2,1,0:T(8,128)(2,1)} copy(bf16[2,16,16,2304]{3,2,0,1:T(8,128)(2,1)} %bitcast.75) | data formatting | bytes 4718592
  287.3 3.0 %all-to-all-done.1 = bf16[8,256,144]{1,2,0:T(8,128)(2,1)S(1)} async-done(((bf16[8,256,144]{1,2,0:T(8,128)(2,1)}), bf16[8,256,144]{1,2,0:T(8,128)(2,1)S(1)}, u32[]{:S(2)}, u32[]{:S(2)}) %all-to-all-start.1) | async-done | bytes 589856 | tf_op jit(solution)/shard_map/all_to_all | solution.py:94
  (90 shorter events, 52.1 us)
Async XLA Ops:
  0.6 161.4 %copy-start = (s32[1,16]{1,0:T(1,128)S(1)}, s32[1,16]{1,0:T(1,128)}, u32[]{:S(2)}) copy-start(s32[1,16]{1,0:T(1,128)} %param.19) | copy-start | bytes 196
  0.6 10.4 %copy-start.4 = (bf16[8,144,720]{2,1,0:T(8,128)(2,1)S(1)}, bf16[8,144,720]{2,1,0:T(8,128)(2,1)}, u32[]{:S(2)}) copy-start(bf16[8,144,720]{2,1,0:T(8,128)(2,1)} %param.12) | copy-start | bytes 4976644
  2.5 17.3 %all-to-all-start = ((bf16[8,256,144]{1,2,0:T(8,128)(2,1)}), bf16[8,256,144]{1,2,0:T(8,128)(2,1)S(1)}, u32[]{:S(2)}, u32[]{:S(2)}) async-start(bf16[8,256,144]{1,2,0:T(8,128)(2,1)} %broadcast_in_dim.64), calls=%async_computation | async-start | bytes 1179648 | tf_op jit(solution)/shard_map/all_to_all | solution.py:87
  71.3 10.4 %collective-permute-start = (bf16[4,2,256,1440]{2,3,1,0:T(8,128)(2,1)}, bf16[4,2,256,1440]{2,3,1,0:T(8,128)(2,1)}, u32[]{:S(2)}, u32[]{:S(2)}) collective-permute-start(bf16[4,2,256,1440]{2,3,1,0:T(8,128)(2,1)} %bitcast.76), channel_id=1, source_target_pairs={{0,1},{1,0},{2,3},{3,2},{4,5},{5,4},{6,7},{7,6},{8,9},{9,8},{10,11... | collective-permute-start | bytes 17694728 | tf_op jit(solution)/shard_map/ppermute | solution.py:157
  88.5 1.6 copy-start.3
  88.6 47.5 %copy-start.2 = (bf16[4,2,128,1440]{2,3,1,0:T(8,128)(2,1)}, bf16[4,2,128,1440]{2,3,1,0:T(8,128)(2,1)S(1)}, u32[]{:S(2)}) copy-start(bf16[4,2,128,1440]{2,3,1,0:T(8,128)(2,1)S(1)} %get-tuple-element.13) | copy-start | bytes 8847364
  91.2 18.3 %collective-permute-start.4 = (bf16[2,128,1440]{1,2,0:T(8,128)(2,1)}, bf16[2,128,1440]{1,2,0:T(8,128)(2,1)}, u32[]{:S(2)}, u32[]{:S(2)}) collective-permute-start(bf16[2,128,1440]{1,2,0:T(8,128)(2,1)} %dynamic-slice_bitcast_fusion), channel_id=1, source_target_pairs={{0,12},{1,13},{2,14},{3,15},{4,0},{5,1},{6,2},{7,3},{8,4},{9,5},{1... | collective-permute-start | bytes 2211848 | tf_op jit(solution)/shard_map/ppermute | solution.py:132
  94.6 20.7 %collective-permute-start.1 = (bf16[2,128,1440]{1,2,0:T(8,128)(2,1)}, bf16[2,128,1440]{1,2,0:T(8,128)(2,1)}, u32[]{:S(2)}, u32[]{:S(2)}) collective-permute-start(bf16[2,128,1440]{1,2,0:T(8,128)(2,1)} %dynamic-slice_bitcast_fusion.1), channel_id=1, source_target_pairs={{0,4},{1,5},{2,6},{3,7},{4,8},{5,9},{6,10},{7,11},{8,12},{9,13},{1... | collective-permute-start | bytes 2211848 | tf_op jit(solution)/shard_map/ppermute | solution.py:132
  111.9 18.3 %collective-permute-start.5 = (bf16[2,128,1440]{1,2,0:T(8,128)(2,1)}, bf16[2,128,1440]{1,2,0:T(8,128)(2,1)}, u32[]{:S(2)}, u32[]{:S(2)}) collective-permute-start(bf16[2,128,1440]{1,2,0:T(8,128)(2,1)} %fusion.7), channel_id=1, source_target_pairs={{0,12},{1,13},{2,14},{3,15},{4,0},{5,1},{6,2},{7,3},{8,4},{9,5},{1... | collective-permute-start | bytes 2211848 | tf_op jit(solution)/shard_map/ppermute | solution.py:132
  117.5 18.6 %collective-permute-start.2 = (bf16[2,128,1440]{1,2,0:T(8,128)(2,1)}, bf16[2,128,1440]{1,2,0:T(8,128)(2,1)}, u32[]{:S(2)}, u32[]{:S(2)}) collective-permute-start(bf16[2,128,1440]{1,2,0:T(8,128)(2,1)} %fusion.9), channel_id=1, source_target_pairs={{0,4},{1,5},{2,6},{3,7},{4,8},{5,9},{6,10},{7,11},{8,12},{9,13},{1... | collective-permute-start | bytes 2211848 | tf_op jit(solution)/shard_map/ppermute | solution.py:132
  132.6 17.5 %collective-permute-start.6 = (bf16[2,128,1440]{1,2,0:T(8,128)(2,1)}, bf16[2,128,1440]{1,2,0:T(8,128)(2,1)}, u32[]{:S(2)}, u32[]{:S(2)}) collective-permute-start(bf16[2,128,1440]{1,2,0:T(8,128)(2,1)} %fusion.6), channel_id=1, source_target_pairs={{0,12},{1,13},{2,14},{3,15},{4,0},{5,1},{6,2},{7,3},{8,4},{9,5},{1... | collective-permute-start | bytes 2211848 | tf_op jit(solution)/shard_map/ppermute | solution.py:132
  138.2 17.2 %collective-permute-start.3 = (bf16[2,128,1440]{1,2,0:T(8,128)(2,1)}, bf16[2,128,1440]{1,2,0:T(8,128)(2,1)}, u32[]{:S(2)}, u32[]{:S(2)}) collective-permute-start(bf16[2,128,1440]{1,2,0:T(8,128)(2,1)} %fusion.8), channel_id=1, source_target_pairs={{0,4},{1,5},{2,6},{3,7},{4,8},{5,9},{6,10},{7,11},{8,12},{9,13},{1... | collective-permute-start | bytes 2211848 | tf_op jit(solution)/shard_map/ppermute | solution.py:132
  156.9 4.3 %copy-start.6 = (f32[2048,2]{0,1:T(2,128)S(1)}, f32[2048,2]{0,1:T(2,128)}, u32[]{:S(2)}) copy-start(f32[2048,2]{0,1:T(2,128)} %param.15) | copy-start | bytes 49156
  156.9 4.3 %copy-start.5 = (s32[1,16,16]{2,1,0:T(8,128)S(1)}, s32[1,16,16]{2,1,0:T(8,128)}, u32[]{:S(2)}) copy-start(s32[1,16,16]{2,1,0:T(8,128)} %param.17) | copy-start | bytes 3076
  157.0 4.9 %copy-start.7 = (s32[1,16,16]{2,1,0:T(8,128)S(1)}, s32[1,16,16]{2,1,0:T(8,128)}, u32[]{:S(2)}) copy-start(s32[1,16,16]{2,1,0:T(8,128)} %param.18) | copy-start | bytes 3076
  157.9 17.3 %collective-permute-start.7 = (bf16[256,1440]{0,1:T(8,128)(2,1)}, bf16[256,1440]{0,1:T(8,128)(2,1)}, u32[]{:S(2)}, u32[]{:S(2)}) collective-permute-start(bf16[256,1440]{0,1:T(8,128)(2,1)} %fusion.10), channel_id=1, source_target_pairs={{0,2},{1,3},{2,0},{3,1},{4,6},{5,7},{6,4},{7,5},{8,10},{9,11},{10,... | collective-permute-start | bytes 2211848 | tf_op jit(solution)/shard_map/ppermute | solution.py:165
  176.7 7.9 %collective-permute-start.8 = (bf16[256,720]{0,1:T(8,128)(2,1)S(1)}, bf16[256,720]{0,1:T(8,128)(2,1)S(1)}, u32[]{:S(2)}, u32[]{:S(2)}) collective-permute-start(bf16[256,720]{0,1:T(8,128)(2,1)S(1)} %fusion.11), channel_id=1, source_target_pairs={{0,2},{1,3},{2,0},{3,1},{4,6},{5,7},{6,4},{7,5},{8,10},{9,11},{10,... | collective-permute-start | bytes 1105928 | tf_op jit(solution)/shard_map/ppermute | solution.py:174
  184.9 7.6 %collective-permute-start.9 = (bf16[2,128,720]{1,2,0:T(8,128)(2,1)S(1)}, bf16[2,128,720]{1,2,0:T(8,128)(2,1)S(1)}, u32[]{:S(2)}, u32[]{:S(2)}) collective-permute-start(bf16[2,128,720]{1,2,0:T(8,128)(2,1)S(1)} %get-tuple-element.16), channel_id=1, source_target_pairs={{0,4},{1,5},{2,6},{3,7},{4,8},{5,9},{6,10},{7,11},{8,12},{9,13},{1... | collective-permute-start | bytes 1105928 | tf_op jit(solution)/shard_map/ppermute | solution.py:147
  185.0 7.6 %collective-permute-start.12 = (bf16[2,128,720]{1,2,0:T(8,128)(2,1)S(1)}, bf16[2,128,720]{1,2,0:T(8,128)(2,1)S(1)}, u32[]{:S(2)}, u32[]{:S(2)}) collective-permute-start(bf16[2,128,720]{1,2,0:T(8,128)(2,1)S(1)} %get-tuple-element.17), channel_id=1, source_target_pairs={{0,12},{1,13},{2,14},{3,15},{4,0},{5,1},{6,2},{7,3},{8,4},{9,5},{1... | collective-permute-start | bytes 1105928 | tf_op jit(solution)/shard_map/ppermute | solution.py:147
  192.6 9.4 %collective-permute-start.10 = (bf16[2,128,720]{1,2,0:T(8,128)(2,1)S(1)}, bf16[2,128,720]{1,2,0:T(8,128)(2,1)S(1)}, u32[]{:S(2)}, u32[]{:S(2)}) collective-permute-start(bf16[2,128,720]{1,2,0:T(8,128)(2,1)S(1)} %collective-permute-done.9), channel_id=1, source_target_pairs={{0,4},{1,5},{2,6},{3,7},{4,8},{5,9},{6,10},{7,11},{8,12},{9,13},{1... | collective-permute-start | bytes 1105928 | tf_op jit(solution)/shard_map/ppermute | solution.py:147
  192.6 9.4 %collective-permute-start.13 = (bf16[2,128,720]{1,2,0:T(8,128)(2,1)S(1)}, bf16[2,128,720]{1,2,0:T(8,128)(2,1)S(1)}, u32[]{:S(2)}, u32[]{:S(2)}) collective-permute-start(bf16[2,128,720]{1,2,0:T(8,128)(2,1)S(1)} %collective-permute-done.12), channel_id=1, source_target_pairs={{0,12},{1,13},{2,14},{3,15},{4,0},{5,1},{6,2},{7,3},{8,4},{9,5},{1... | collective-permute-start | bytes 1105928 | tf_op jit(solution)/shard_map/ppermute | solution.py:147
  201.9 10.5 %collective-permute-start.11 = (bf16[2,128,720]{1,2,0:T(8,128)(2,1)S(1)}, bf16[2,128,720]{1,2,0:T(8,128)(2,1)S(1)}, u32[]{:S(2)}, u32[]{:S(2)}) collective-permute-start(bf16[2,128,720]{1,2,0:T(8,128)(2,1)S(1)} %collective-permute-done.10), channel_id=1, source_target_pairs={{0,4},{1,5},{2,6},{3,7},{4,8},{5,9},{6,10},{7,11},{8,12},{9,13},{1... | collective-permute-start | bytes 1105928 | tf_op jit(solution)/shard_map/ppermute | solution.py:147
  201.9 10.6 %collective-permute-start.14 = (bf16[2,128,720]{1,2,0:T(8,128)(2,1)S(1)}, bf16[2,128,720]{1,2,0:T(8,128)(2,1)S(1)}, u32[]{:S(2)}, u32[]{:S(2)}) collective-permute-start(bf16[2,128,720]{1,2,0:T(8,128)(2,1)S(1)} %collective-permute-done.13), channel_id=1, source_target_pairs={{0,12},{1,13},{2,14},{3,15},{4,0},{5,1},{6,2},{7,3},{8,4},{9,5},{1... | collective-permute-start | bytes 1105928 | tf_op jit(solution)/shard_map/ppermute | solution.py:147
  214.7 30.9 %collective-permute-start.15 = (bf16[4,2,256,720]{2,3,1,0:T(8,128)(2,1)}, bf16[4,2,256,720]{2,3,1,0:T(8,128)(2,1)}, u32[]{:S(2)}, u32[]{:S(2)}) collective-permute-start(bf16[4,2,256,720]{2,3,1,0:T(8,128)(2,1)} %get-tuple-element.15), channel_id=1, source_target_pairs={{0,1},{1,0},{2,3},{3,2},{4,5},{5,4},{6,7},{7,6},{8,9},{9,8},{10,11... | collective-permute-start | bytes 8847368 | tf_op jit(solution)/shard_map/ppermute | solution.py:180
  232.9 43.0 %all-to-all-start.2 = ((bf16[2,16,16,2304]{3,2,0,1:T(8,128)(2,1)}), bf16[2,16,16,2304]{3,2,0,1:T(8,128)(2,1)}, u32[]{:S(2)}, u32[]{:S(2)}) async-start(bf16[2,16,16,2304]{3,2,0,1:T(8,128)(2,1)} %bitcast.74), calls=%async_computation.2 | async-start | bytes 4718592 | tf_op jit(solution)/shard_map/all_to_all | solution.py:28
  275.9 14.4 %all-to-all-start.1 = ((bf16[8,256,144]{1,2,0:T(8,128)(2,1)}), bf16[8,256,144]{1,2,0:T(8,128)(2,1)S(1)}, u32[]{:S(2)}, u32[]{:S(2)}) async-start(bf16[8,256,144]{1,2,0:T(8,128)(2,1)} %copy.49), calls=%async_computation.1 | async-start | bytes 1179648 | tf_op jit(solution)/shard_map/all_to_all | solution.py:94
  284.0 7.0 %copy-start.1 = (s32[1,16]{1,0:T(1,128)S(1)}, s32[1,16]{1,0:T(1,128)}, u32[]{:S(2)}) copy-start(s32[1,16]{1,0:T(1,128)} %param.19) | copy-start | bytes 196

commit v8 on v7

--- a/solution.py
+++ b/solution.py
@@ -3,6 +3,7 @@
 from jax import lax
 from jax.sharding import PartitionSpec as P
 from jax.experimental import pallas as pl
+from jax.experimental.pallas import tpu as pltpu
 
 
 def move_pages(prefill_cache, dest_col, dest_slot, pages_used):
@@ -39,7 +40,7 @@
     return received[:, source_of_slot]
 
 
-def gate_up_kernel(ids_ref, x_ref, w_ref, o_ref):
+def gate_up_kernel(sel_ref, ids_ref, x_ref, w_ref, o_ref):
     x = x_ref[...]
     ids = ids_ref[...]
     zero = jnp.zeros_like(x)
@@ -65,20 +66,24 @@
     o_ref[...] = acc.astype(o_ref.dtype)
 
 
-def gate_up(route_ids, gathered, paired, tile):
+def gate_up(route_ids, gathered, paired, tile, sel):
     token_count, width = gathered.shape
     experts, _, paired_width = paired.shape
+    steps = token_count // tile // 2
     return pl.pallas_call(
         gate_up_kernel,
-        grid=(token_count // tile,),
-        in_specs=[
-            pl.BlockSpec((tile, 2), lambda i: (i, 0)),
-            pl.BlockSpec((tile, width), lambda i: (i, 0)),
-            pl.BlockSpec((experts, width, paired_width), lambda i: (0, 0, 0)),
-        ],
-        out_specs=pl.BlockSpec((2, tile, paired_width), lambda i: (0, i, 0)),
-        out_shape=jax.ShapeDtypeStruct((2, token_count, paired_width), jnp.bfloat16),
-    )(route_ids, gathered, paired)
+        grid_spec=pltpu.PrefetchScalarGridSpec(
+            num_scalar_prefetch=1,
+            grid=(steps,),
+            in_specs=[
+                pl.BlockSpec((tile, 2), lambda j, sel_ref: (2 * j + sel_ref[0], 0)),
+                pl.BlockSpec((tile, width), lambda j, sel_ref: (2 * j + sel_ref[0], 0)),
+                pl.BlockSpec((experts, width, paired_width), lambda j, sel_ref: (0, 0, 0)),
+            ],
+            out_specs=pl.BlockSpec((2, tile, paired_width), lambda j, sel_ref: (0, j, 0)),
+        ),
+        out_shape=jax.ShapeDtypeStruct((2, steps * tile, paired_width), jnp.bfloat16),
+    )(sel.reshape(1), route_ids, gathered, paired)
 
 
 def gather_rows(x, axis_name):
@@ -149,21 +154,21 @@
     return out
 
 
-def col_reduce_scatter(partial, axis_name):
+def col_reduce_scatter(other, mine, axis_name):
     c = lax.axis_index(axis_name)
-    xi, zi, co = c // 4, (c // 2) % 2, c % 2
-    rows = partial.shape[0] // 16
-    blocks = partial.reshape(4, 2, 2, rows, partial.shape[1])
-    recv = lax.ppermute(pick(blocks, 1 - co, 2), axis_name, col_perm(axis_name, lambda q: q ^ 1))
-    core_sum = (pick(blocks, co, 2).astype(jnp.float32) + recv.astype(jnp.float32)).astype(
-        partial.dtype
+    xi, zi = c // 4, (c // 2) % 2
+    rows = other.shape[1] // 4
+    shape = (4, 2, rows, other.shape[2])
+    recv = lax.ppermute(other.reshape(shape), axis_name, col_perm(axis_name, lambda q: q ^ 1))
+    core_sum = (mine.reshape(shape).astype(jnp.float32) + recv.astype(jnp.float32)).astype(
+        other.dtype
     )
     half = rows // 2
     plus = ring_reduce(core_sum[:, :, :half], xi, axis_name, 1)
     minus = ring_reduce(core_sum[:, :, half:], xi, axis_name, -1)
     x_sum = jnp.concatenate([plus, minus], axis=1)
     recv = lax.ppermute(
-        pick(x_sum, 1 - zi).astype(partial.dtype), axis_name, col_perm(axis_name, lambda q: q ^ 2)
+        pick(x_sum, 1 - zi).astype(other.dtype), axis_name, col_perm(axis_name, lambda q: q ^ 2)
     )
     return pick(x_sum, zi) + recv.astype(jnp.float32)
 
@@ -199,8 +204,10 @@
     token_count = gathered.shape[0]
     hidden_width = gate_weight.shape[2]
     paired = jnp.concatenate([gate_weight, up_weight], axis=2)
-    partial_sums = gate_up(route_ids, gathered, paired, 256)
-    summed = col_reduce_scatter(partial_sums.reshape(2 * token_count, 2 * hidden_width), "col")
+    core = lax.axis_index("col") % 2
+    other = gate_up(route_ids, gathered, paired, 256, 1 - core)
+    mine = gate_up(route_ids, gathered, paired, 256, core)
+    summed = col_reduce_scatter(other, mine, "col")
     share_rows = summed.shape[0]
     own_weight = lax.dynamic_slice_in_dim(
         route_weight.T.reshape(-1), lax.axis_index("col") * share_rows, share_rows, 0

time: 293 us -> 292 us (level)
  local copies, waits for them, and re-layouts: 67.9 us -> 60.3 us
  other arithmetic: 39.1 us -> 43.2 us
  Pallas kernels: 44.3 us -> 47.6 us
    dynamic_slice x2 -> x0, local copies, waits for them, and re-layouts: 18.8 us -> none  [pick(): return lax.dynamic_index_in_dim(chunks, index, axis, keepdims=False)]
    convert_element_type x0 -> x1, local copies, waits for them, and re-layouts: none -> 9.25 us  [col_reduce_scatter(): mine.reshape(shape).astype(jnp.float32) + recv.astype(jnp.float32)]
    unnamed x21 -> x20, local copies, waits for them, and re-layouts: 19.9 us -> 11.3 us
    reshape x0 -> x1, local copies, waits for them, and re-layouts: none -> 8.49 us  [col_reduce_scatter(): other.reshape(shape)]
    convert_element_type x2, other arithmetic: 6.78 us -> 10.9 us  [the longest x1 9.91 us: col_reduce_scatter(): (mine.reshape(shape).astype(jnp.float32) + recv.astype(jnp.float32)).asty...]
    pallas_call x1 -> x2, Pallas kernels: 31.4 us -> 34.7 us  [gate_up(): pl.pallas_call(gate_up_kernel, grid_spec=pltpu.PrefetchScalarGridSpec(num...]
  transfers between devices with their start and end apart: 19 -> 19, of which waited for: 13 -> 12; matrix products, arithmetic and copies ran while one was open for 23% -> 24% of each run, Pallas kernels for 4% -> 10%
where the time goes in v8:
time: 292 us; the launch traced here: 290 us
  waiting for transfers between devices  87 us (30%)
  local copies, waits for them, and re-layouts  60.3 us (21%)
  starting transfers between devices  51.1 us (18%)
  Pallas kernels  47.6 us (16%)
  other arithmetic  43.2 us (15%)
    ppermute x6, waiting for transfers between devices, ring_reduce(): recv = lax.ppermute(cur, axis_name, perm)  44.4 us
    pallas_call x2, Pallas kernels, gate_up(): pl.pallas_call(gate_up_kernel, grid_spec=pltpu.PrefetchScalarGridSpec(num...  34.7 us
    ppermute x6, waiting for transfers between devices, ring_gather(): cur = lax.ppermute(cur, axis_name, perm)  17.2 us
    pallas_call x1, Pallas kernels, down(): pl.pallas_call(down_kernel, grid=(token_count // tile,), in_specs=[pl.Blo...  12.9 us
    ppermute x1, waiting for transfers between devices, col_reduce_scatter(): lax.ppermute(pick(x_sum, 1 - zi).astype(other.dtype), axis_name, col_perm...  12.9 us
    unnamed x20, local copies, waits for them, and re-layouts  11.3 us
    convert_element_type x1, other arithmetic, col_reduce_scatter(): (mine.reshape(shape).astype(jnp.float32) + recv.astype(jnp.float32)).asty...  9.91 us
    ppermute x6, starting transfers between devices, ring_reduce(): recv = lax.ppermute(cur, axis_name, perm)  9.31 us
  transfers between devices with their start and end apart: 19, of which 12 were waited for; matrix products, arithmetic and copies ran while one was open for 24% of the time, Pallas kernels for 10%

profile of v8, /device:TPU:1, one launch (start us, length us, event | category | flops | bytes accessed | tf_op | source)
XLA Modules:
  0.0 290.2 jit_solution(9829158735535835509)
XLA Ops:
  2.5 6.4 %all-to-all-start = ((bf16[8,256,144]{1,2,0:T(8,128)(2,1)}), bf16[8,256,144]{1,2,0:T(8,128)(2,1)S(1)}, u32[]{:S(2)}, u32[]{:S(2)}) async-start(bf16[8,256,144]{1,2,0:T(8,128)(2,1)} %broadcast_in_dim.64), calls=%async_computation | async-start | bytes 1179648 | tf_op jit(solution)/shard_map/all_to_all | solution.py:92
  10.9 4.5 %pad_maximum_fusion.w_ref = bf16[8,144,1440]{2,1,0:T(8,128)(2,1)} fusion(bf16[8,144,720]{2,1,0:T(8,128)(2,1)S(1)} %copy-done.4, bf16[8,144,720]{2,1,0:T(8,128)(2,1)} %param.11), kind=kLoop, calls=%fused_computation.7 | loop fusion | flops 6635520 | bytes 6635520 | tf_op jit(solution)/shard_map/concatenate | solution.py:206
  15.5 4.4 %all-to-all-done = bf16[8,256,144]{1,2,0:T(8,128)(2,1)S(1)} async-done(((bf16[8,256,144]{1,2,0:T(8,128)(2,1)}), bf16[8,256,144]{1,2,0:T(8,128)(2,1)S(1)}, u32[]{:S(2)}, u32[]{:S(2)}) %all-to-all-start) | async-done | bytes 589856 | tf_op jit(solution)/shard_map/all_to_all | solution.py:92
  21.1 17.4 %shard_map.114 = bf16[2,1024,1440]{2,1,0:T(8,128)(2,1)} custom-call(s32[1]{0:T(128)} %bitcast.4.sel_ref, s32[2048,2]{1,0:T(8,128)} %copy.49.ids_ref, bf16[2048,144]{1,0:T(8,128)(2,1)} %bitcast.75, bf16[8,144,1440]{2,1,0:T(8,128)(2,1)} %pad_maximum_fusion.w_ref), custom_call_target="tpu_custom_call" | custom-call | tf_op jit(solution)/shard_map/pallas_call | solution.py:73
  38.5 8.5 %copy.46 = bf16[4,2,256,1440]{2,3,1,0:T(8,128)(2,1)} copy(bf16[4,2,256,1440]{3,2,1,0:T(8,128)(2,1)} %bitcast.73) | data formatting | bytes 11796480 | tf_op jit(solution)/shard_map/reshape | solution.py:162
  47.7 17.4 %shard_map.113 = bf16[2,1024,1440]{2,1,0:T(8,128)(2,1)} custom-call(s32[1]{0:T(128)} %bitcast.1.sel_ref, s32[2048,2]{1,0:T(8,128)} %copy.49.ids_ref, bf16[2048,144]{1,0:T(8,128)(2,1)} %bitcast.76, bf16[8,144,1440]{2,1,0:T(8,128)(2,1)} %pad_maximum_fusion.w_ref), custom_call_target="tpu_custom_call" | custom-call | tf_op jit(solution)/shard_map/pallas_call | solution.py:73
  65.1 9.2 %copy.47 = f32[4,2,256,1440]{2,3,1,0:T(8,128)} copy(bf16[4,2,256,1440]{3,2,1,0:T(8,128)(2,1)} %bitcast.72) | data formatting | bytes 17694720 | tf_op jit(solution)/shard_map/convert_element_type | solution.py:163
  74.4 9.9 %add_convert_fusion = bf16[4,2,256,1440]{2,3,1,0:T(8,128)(2,1)} fusion(f32[4,2,256,1440]{2,3,1,0:T(8,128)} %copy.47, bf16[4,2,256,1440]{2,3,1,0:T(8,128)(2,1)} %collective-permute-done), kind=kLoop, calls=%fused_computation.5 | loop fusion | flops 8847360 | bytes 23592960 | tf_op jit(solution)/shard_map/convert_element_type | solution.py:163
  84.3 3.1 %fusion.21 = (bf16[4,2,128,1440]{2,3,1,0:T(8,128)(2,1)S(1)}, bf16[4,2,128,1440]{2,3,1,0:T(8,128)(2,1)S(1)}) fusion(bf16[4,2,256,1440]{2,3,1,0:T(8,128)(2,1)} %add_convert_fusion), kind=kLoop, calls=%fused_computation.68 | loop fusion | bytes 11796480 | tf_op jit(solution)/shard_map/slice | solution.py:168
  93.5 15.2 %collective-permute-done.4 = bf16[2,128,1440]{1,2,0:T(8,128)(2,1)} collective-permute-done((bf16[2,128,1440]{1,2,0:T(8,128)(2,1)}, bf16[2,128,1440]{1,2,0:T(8,128)(2,1)}, u32[]{:S(2)}, u32[]{:S(2)}) %collective-permute-start.4) | collective-permute-done | bytes 737312 | tf_op jit(solution)/shard_map/ppermute | solution.py:137
  111.1 3.4 %collective-permute-start.5 = (bf16[2,128,1440]{1,2,0:T(8,128)(2,1)}, bf16[2,128,1440]{1,2,0:T(8,128)(2,1)}, u32[]{:S(2)}, u32[]{:S(2)}) collective-permute-start(bf16[2,128,1440]{1,2,0:T(8,128)(2,1)} %fusion.6), channel_id=1, source_target_pairs={{0,12},{1,13},{2,14},{3,15},{4,0},{5,1},{6,2},{7,3},{8,4},{9,5},{1... | collective-permute-start | bytes 2211848 | tf_op jit(solution)/shard_map/ppermute | solution.py:137
  116.7 13.1 %collective-permute-done.5 = bf16[2,128,1440]{1,2,0:T(8,128)(2,1)} collective-permute-done((bf16[2,128,1440]{1,2,0:T(8,128)(2,1)}, bf16[2,128,1440]{1,2,0:T(8,128)(2,1)}, u32[]{:S(2)}, u32[]{:S(2)}) %collective-permute-start.5) | collective-permute-done | bytes 737312 | tf_op jit(solution)/shard_map/ppermute | solution.py:137
  132.2 3.4 %collective-permute-start.6 = (bf16[2,128,1440]{1,2,0:T(8,128)(2,1)}, bf16[2,128,1440]{1,2,0:T(8,128)(2,1)}, u32[]{:S(2)}, u32[]{:S(2)}) collective-permute-start(bf16[2,128,1440]{1,2,0:T(8,128)(2,1)} %fusion.5), channel_id=1, source_target_pairs={{0,12},{1,13},{2,14},{3,15},{4,0},{5,1},{6,2},{7,3},{8,4},{9,5},{1... | collective-permute-start | bytes 2211848 | tf_op jit(solution)/shard_map/ppermute | solution.py:137
  137.8 12.2 %collective-permute-done.6 = bf16[2,128,1440]{1,2,0:T(8,128)(2,1)} collective-permute-done((bf16[2,128,1440]{1,2,0:T(8,128)(2,1)}, bf16[2,128,1440]{1,2,0:T(8,128)(2,1)}, u32[]{:S(2)}, u32[]{:S(2)}) %collective-permute-start.6) | collective-permute-done | bytes 737312 | tf_op jit(solution)/shard_map/ppermute | solution.py:137
  151.5 3.8 %collective-permute-done.3 = bf16[2,128,1440]{1,2,0:T(8,128)(2,1)} collective-permute-done((bf16[2,128,1440]{1,2,0:T(8,128)(2,1)}, bf16[2,128,1440]{1,2,0:T(8,128)(2,1)}, u32[]{:S(2)}, u32[]{:S(2)}) %collective-permute-start.3) | collective-permute-done | bytes 737312 | tf_op jit(solution)/shard_map/ppermute | solution.py:137
  157.8 3.3 %collective-permute-start.7 = (bf16[256,1440]{0,1:T(8,128)(2,1)}, bf16[256,1440]{0,1:T(8,128)(2,1)}, u32[]{:S(2)}, u32[]{:S(2)}) collective-permute-start(bf16[256,1440]{0,1:T(8,128)(2,1)} %fusion.9), channel_id=1, source_target_pairs={{0,2},{1,3},{2,0},{3,1},{4,6},{5,7},{6,4},{7,5},{8,10},{9,11},{10,... | collective-permute-start | bytes 2211848 | tf_op jit(solution)/shard_map/ppermute | solution.py:170
  162.6 12.9 %collective-permute-done.7 = bf16[256,1440]{0,1:T(8,128)(2,1)} collective-permute-done((bf16[256,1440]{0,1:T(8,128)(2,1)}, bf16[256,1440]{0,1:T(8,128)(2,1)}, u32[]{:S(2)}, u32[]{:S(2)}) %collective-permute-start.7) | collective-permute-done | bytes 737312 | tf_op jit(solution)/shard_map/ppermute | solution.py:170
  180.0 5.3 %collective-permute-done.8 = bf16[256,720]{0,1:T(8,128)(2,1)S(1)} collective-permute-done((bf16[256,720]{0,1:T(8,128)(2,1)S(1)}, bf16[256,720]{0,1:T(8,128)(2,1)S(1)}, u32[]{:S(2)}, u32[]{:S(2)}) %collective-permute-start.8) | collective-permute-done | bytes 368672 | tf_op jit(solution)/shard_map/ppermute | solution.py:179
  188.8 4.4 %collective-permute-done.9 = bf16[2,128,720]{1,2,0:T(8,128)(2,1)S(1)} collective-permute-done((bf16[2,128,720]{1,2,0:T(8,128)(2,1)S(1)}, bf16[2,128,720]{1,2,0:T(8,128)(2,1)S(1)}, u32[]{:S(2)}, u32[]{:S(2)}) %collective-permute-start.9) | collective-permute-done | bytes 368672 | tf_op jit(solution)/shard_map/ppermute | solution.py:152
  196.0 5.9 %collective-permute-done.10 = bf16[2,128,720]{1,2,0:T(8,128)(2,1)S(1)} collective-permute-done((bf16[2,128,720]{1,2,0:T(8,128)(2,1)S(1)}, bf16[2,128,720]{1,2,0:T(8,128)(2,1)S(1)}, u32[]{:S(2)}, u32[]{:S(2)}) %collective-permute-start.10) | collective-permute-done | bytes 368672 | tf_op jit(solution)/shard_map/ppermute | solution.py:152
  205.0 6.8 %collective-permute-done.11 = bf16[2,128,720]{1,2,0:T(8,128)(2,1)S(1)} collective-permute-done((bf16[2,128,720]{1,2,0:T(8,128)(2,1)S(1)}, bf16[2,128,720]{1,2,0:T(8,128)(2,1)S(1)}, u32[]{:S(2)}, u32[]{:S(2)}) %collective-permute-start.11) | collective-permute-done | bytes 368672 | tf_op jit(solution)/shard_map/ppermute | solution.py:152
  214.0 7.7 %collective-permute-start.15 = (bf16[4,2,256,720]{2,3,1,0:T(8,128)(2,1)}, bf16[4,2,256,720]{2,3,1,0:T(8,128)(2,1)}, u32[]{:S(2)}, u32[]{:S(2)}) collective-permute-start(bf16[4,2,256,720]{2,3,1,0:T(8,128)(2,1)} %get-tuple-element.13), channel_id=1, source_target_pairs={{0,1},{1,0},{2,3},{3,2},{4,5},{5,4},{6,7},{7,6},{8,9},{9,8},{10,11... | collective-permute-start | bytes 8847368 | tf_op jit(solution)/shard_map/ppermute | solution.py:185
  224.5 3.3 %broadcast_select_fusion = bf16[2,16,16,2304]{3,2,1,0:T(8,128)(2,1)} fusion(bf16[2,16,16,2304]{3,2,1,0:T(8,128)(2,1)} %param.16, pred[16]{0:T(512)(128)(4,1)S(1)} %iota_compare_fusion.1), kind=kLoop, calls=%fused_computation.13 | loop fusion | flops 1179648 | bytes 4718608 | tf_op jit(solution)/shard_map/jit(_where)/select_n | solution.py:26
  227.8 3.8 %gather_fusion = bf16[16,2,16,2304]{3,2,1,0:T(8,128)(2,1)} fusion(bf16[2,16,16,2304]{3,2,1,0:T(8,128)(2,1)} %broadcast_select_fusion, s32[1024]{0:T(1024)S(1)} %pad_clamp_fusion.1), kind=kCustom, calls=%fused_computation | custom fusion | bytes 4718656 | tf_op jit(solution)/shard_map/gather | solution.py:30
  231.5 8.9 %all-to-all-start.2 = ((bf16[2,16,16,2304]{3,2,0,1:T(8,128)(2,1)}), bf16[2,16,16,2304]{3,2,0,1:T(8,128)(2,1)}, u32[]{:S(2)}, u32[]{:S(2)}) async-start(bf16[2,16,16,2304]{3,2,0,1:T(8,128)(2,1)} %bitcast.77), calls=%async_computation.2 | async-start | bytes 4718592 | tf_op jit(solution)/shard_map/all_to_all | solution.py:29
  240.4 4.4 %copy.50.d_ref = bf16[8,720,144]{2,1,0:T(8,128)(2,1)} copy(bf16[8,720,144]{1,2,0:T(8,128)(2,1)} %param.13) | data formatting | bytes 3317760 | tf_op args[3]
  244.8 6.6 %maximum_select_fusion = bf16[4,2,2,256,720]{3,4,1,0,2:T(8,128)(2,1)} fusion(bf16[4,2,1,256,720]{3,4,1,0,2:T(8,128)(2,1)} %bitcast.27, bf16[4,2,1,256,720]{3,4,1,0,2:T(8,128)(2,1)S(1)} %get-tuple-element.12, pred[]{:T(512)S(6)} %eq.55), kind=kLoop, calls=%fused_computation.6 | loop fusion | flops 8847360 | bytes 11796481 | tf_op jit(solution)/shard_map/jit(_where)/select_n | solution.py:186
  251.4 8.5 %copy.48 = bf16[4,2,2,256,720]{4,3,2,1,0:T(8,128)(2,1)} copy(bf16[4,2,2,256,720]{3,4,1,0,2:T(8,128)(2,1)} %maximum_select_fusion) | data formatting | bytes 11796480 | tf_op jit(solution)/shard_map/jit(_where)/select_n | solution.py:186
  259.9 12.9 %shard_map.115 = bf16[2048,144]{1,0:T(8,128)(2,1)} custom-call(s32[2048,2]{1,0:T(8,128)} %copy.49.ids_ref, bf16[2,2048,720]{2,1,0:T(8,128)(2,1)} %bitcast.74, bf16[8,720,144]{2,1,0:T(8,128)(2,1)} %copy.50.d_ref), custom_call_target="tpu_custom_call" | custom-call | tf_op jit(solution)/shard_map/pallas_call | solution.py:106
  275.0 3.5 %all-to-all-start.1 = ((bf16[8,256,144]{1,2,0:T(8,128)(2,1)}), bf16[8,256,144]{1,2,0:T(8,128)(2,1)S(1)}, u32[]{:S(2)}, u32[]{:S(2)}) async-start(bf16[8,256,144]{1,2,0:T(8,128)(2,1)} %copy.51), calls=%async_computation.1 | async-start | bytes 1179648 | tf_op jit(solution)/shard_map/all_to_all | solution.py:99
  283.2 3.3 %copy.55 = bf16[2,16,16,2304]{3,2,1,0:T(8,128)(2,1)} copy(bf16[2,16,16,2304]{3,2,0,1:T(8,128)(2,1)} %bitcast.78) | data formatting | bytes 4718592
  286.5 3.0 %all-to-all-done.1 = bf16[8,256,144]{1,2,0:T(8,128)(2,1)S(1)} async-done(((bf16[8,256,144]{1,2,0:T(8,128)(2,1)}), bf16[8,256,144]{1,2,0:T(8,128)(2,1)S(1)}, u32[]{:S(2)}, u32[]{:S(2)}) %all-to-all-start.1) | async-done | bytes 589856 | tf_op jit(solution)/shard_map/all_to_all | solution.py:99
  (90 shorter events, 52.9 us)
Async XLA Ops:
  0.6 161.3 %copy-start = (s32[1,16]{1,0:T(1,128)S(1)}, s32[1,16]{1,0:T(1,128)}, u32[]{:S(2)}) copy-start(s32[1,16]{1,0:T(1,128)} %param.19) | copy-start | bytes 196
  0.6 10.3 %copy-start.4 = (bf16[8,144,720]{2,1,0:T(8,128)(2,1)S(1)}, bf16[8,144,720]{2,1,0:T(8,128)(2,1)}, u32[]{:S(2)}) copy-start(bf16[8,144,720]{2,1,0:T(8,128)(2,1)} %param.12) | copy-start | bytes 4976644
  2.5 17.3 %all-to-all-start = ((bf16[8,256,144]{1,2,0:T(8,128)(2,1)}), bf16[8,256,144]{1,2,0:T(8,128)(2,1)S(1)}, u32[]{:S(2)}, u32[]{:S(2)}) async-start(bf16[8,256,144]{1,2,0:T(8,128)(2,1)} %broadcast_in_dim.64), calls=%async_computation | async-start | bytes 1179648 | tf_op jit(solution)/shard_map/all_to_all | solution.py:92
  47.0 27.4 %collective-permute-start = (bf16[4,2,256,1440]{2,3,1,0:T(8,128)(2,1)}, bf16[4,2,256,1440]{2,3,1,0:T(8,128)(2,1)}, u32[]{:S(2)}, u32[]{:S(2)}) collective-permute-start(bf16[4,2,256,1440]{2,3,1,0:T(8,128)(2,1)} %copy.46), channel_id=1, source_target_pairs={{0,1},{1,0},{2,3},{3,2},{4,5},{5,4},{6,7},{7,6},{8,9},{9,8},{10,11... | collective-permute-start | bytes 17694728 | tf_op jit(solution)/shard_map/ppermute | solution.py:162
  87.4 1.6 copy-start.3
  87.4 48.2 %copy-start.2 = (bf16[4,2,128,1440]{2,3,1,0:T(8,128)(2,1)}, bf16[4,2,128,1440]{2,3,1,0:T(8,128)(2,1)S(1)}, u32[]{:S(2)}) copy-start(bf16[4,2,128,1440]{2,3,1,0:T(8,128)(2,1)S(1)} %get-tuple-element.11) | copy-start | bytes 8847364
  90.1 18.6 %collective-permute-start.4 = (bf16[2,128,1440]{1,2,0:T(8,128)(2,1)}, bf16[2,128,1440]{1,2,0:T(8,128)(2,1)}, u32[]{:S(2)}, u32[]{:S(2)}) collective-permute-start(bf16[2,128,1440]{1,2,0:T(8,128)(2,1)} %dynamic-slice_bitcast_fusion), channel_id=1, source_target_pairs={{0,12},{1,13},{2,14},{3,15},{4,0},{5,1},{6,2},{7,3},{8,4},{9,5},{1... | collective-permute-start | bytes 2211848 | tf_op jit(solution)/shard_map/ppermute | solution.py:137
  93.5 21.0 %collective-permute-start.1 = (bf16[2,128,1440]{1,2,0:T(8,128)(2,1)}, bf16[2,128,1440]{1,2,0:T(8,128)(2,1)}, u32[]{:S(2)}, u32[]{:S(2)}) collective-permute-start(bf16[2,128,1440]{1,2,0:T(8,128)(2,1)} %dynamic-slice_bitcast_fusion.1), channel_id=1, source_target_pairs={{0,4},{1,5},{2,6},{3,7},{4,8},{5,9},{6,10},{7,11},{8,12},{9,13},{1... | collective-permute-start | bytes 2211848 | tf_op jit(solution)/shard_map/ppermute | solution.py:137
  111.1 18.7 %collective-permute-start.5 = (bf16[2,128,1440]{1,2,0:T(8,128)(2,1)}, bf16[2,128,1440]{1,2,0:T(8,128)(2,1)}, u32[]{:S(2)}, u32[]{:S(2)}) collective-permute-start(bf16[2,128,1440]{1,2,0:T(8,128)(2,1)} %fusion.6), channel_id=1, source_target_pairs={{0,12},{1,13},{2,14},{3,15},{4,0},{5,1},{6,2},{7,3},{8,4},{9,5},{1... | collective-permute-start | bytes 2211848 | tf_op jit(solution)/shard_map/ppermute | solution.py:137
  116.7 18.9 %collective-permute-start.2 = (bf16[2,128,1440]{1,2,0:T(8,128)(2,1)}, bf16[2,128,1440]{1,2,0:T(8,128)(2,1)}, u32[]{:S(2)}, u32[]{:S(2)}) collective-permute-start(bf16[2,128,1440]{1,2,0:T(8,128)(2,1)} %fusion.8), channel_id=1, source_target_pairs={{0,4},{1,5},{2,6},{3,7},{4,8},{5,9},{6,10},{7,11},{8,12},{9,13},{1... | collective-permute-start | bytes 2211848 | tf_op jit(solution)/shard_map/ppermute | solution.py:137
  132.2 17.8 %collective-permute-start.6 = (bf16[2,128,1440]{1,2,0:T(8,128)(2,1)}, bf16[2,128,1440]{1,2,0:T(8,128)(2,1)}, u32[]{:S(2)}, u32[]{:S(2)}) collective-permute-start(bf16[2,128,1440]{1,2,0:T(8,128)(2,1)} %fusion.5), channel_id=1, source_target_pairs={{0,12},{1,13},{2,14},{3,15},{4,0},{5,1},{6,2},{7,3},{8,4},{9,5},{1... | collective-permute-start | bytes 2211848 | tf_op jit(solution)/shard_map/ppermute | solution.py:137
  137.8 17.6 %collective-permute-start.3 = (bf16[2,128,1440]{1,2,0:T(8,128)(2,1)}, bf16[2,128,1440]{1,2,0:T(8,128)(2,1)}, u32[]{:S(2)}, u32[]{:S(2)}) collective-permute-start(bf16[2,128,1440]{1,2,0:T(8,128)(2,1)} %fusion.7), channel_id=1, source_target_pairs={{0,4},{1,5},{2,6},{3,7},{4,8},{5,9},{6,10},{7,11},{8,12},{9,13},{1... | collective-permute-start | bytes 2211848 | tf_op jit(solution)/shard_map/ppermute | solution.py:137
  156.9 4.3 %copy-start.6 = (f32[2048,2]{0,1:T(2,128)S(1)}, f32[2048,2]{0,1:T(2,128)}, u32[]{:S(2)}) copy-start(f32[2048,2]{0,1:T(2,128)} %param.15) | copy-start | bytes 49156
  156.9 4.3 %copy-start.5 = (s32[1,16,16]{2,1,0:T(8,128)S(1)}, s32[1,16,16]{2,1,0:T(8,128)}, u32[]{:S(2)}) copy-start(s32[1,16,16]{2,1,0:T(8,128)} %param.17) | copy-start | bytes 3076
  156.9 4.9 %copy-start.7 = (s32[1,16,16]{2,1,0:T(8,128)S(1)}, s32[1,16,16]{2,1,0:T(8,128)}, u32[]{:S(2)}) copy-start(s32[1,16,16]{2,1,0:T(8,128)} %param.18) | copy-start | bytes 3076
  157.8 17.6 %collective-permute-start.7 = (bf16[256,1440]{0,1:T(8,128)(2,1)}, bf16[256,1440]{0,1:T(8,128)(2,1)}, u32[]{:S(2)}, u32[]{:S(2)}) collective-permute-start(bf16[256,1440]{0,1:T(8,128)(2,1)} %fusion.9), channel_id=1, source_target_pairs={{0,2},{1,3},{2,0},{3,1},{4,6},{5,7},{6,4},{7,5},{8,10},{9,11},{10,... | collective-permute-start | bytes 2211848 | tf_op jit(solution)/shard_map/ppermute | solution.py:170
  177.0 8.3 %collective-permute-start.8 = (bf16[256,720]{0,1:T(8,128)(2,1)S(1)}, bf16[256,720]{0,1:T(8,128)(2,1)S(1)}, u32[]{:S(2)}, u32[]{:S(2)}) collective-permute-start(bf16[256,720]{0,1:T(8,128)(2,1)S(1)} %fusion.10), channel_id=1, source_target_pairs={{0,2},{1,3},{2,0},{3,1},{4,6},{5,7},{6,4},{7,5},{8,10},{9,11},{10,... | collective-permute-start | bytes 1105928 | tf_op jit(solution)/shard_map/ppermute | solution.py:179
  185.5 7.6 %collective-permute-start.9 = (bf16[2,128,720]{1,2,0:T(8,128)(2,1)S(1)}, bf16[2,128,720]{1,2,0:T(8,128)(2,1)S(1)}, u32[]{:S(2)}, u32[]{:S(2)}) collective-permute-start(bf16[2,128,720]{1,2,0:T(8,128)(2,1)S(1)} %get-tuple-element.14), channel_id=1, source_target_pairs={{0,4},{1,5},{2,6},{3,7},{4,8},{5,9},{6,10},{7,11},{8,12},{9,13},{1... | collective-permute-start | bytes 1105928 | tf_op jit(solution)/shard_map/ppermute | solution.py:152
  185.6 7.6 %collective-permute-start.12 = (bf16[2,128,720]{1,2,0:T(8,128)(2,1)S(1)}, bf16[2,128,720]{1,2,0:T(8,128)(2,1)S(1)}, u32[]{:S(2)}, u32[]{:S(2)}) collective-permute-start(bf16[2,128,720]{1,2,0:T(8,128)(2,1)S(1)} %get-tuple-element.15), channel_id=1, source_target_pairs={{0,12},{1,13},{2,14},{3,15},{4,0},{5,1},{6,2},{7,3},{8,4},{9,5},{1... | collective-permute-start | bytes 1105928 | tf_op jit(solution)/shard_map/ppermute | solution.py:152
  193.2 8.7 %collective-permute-start.10 = (bf16[2,128,720]{1,2,0:T(8,128)(2,1)S(1)}, bf16[2,128,720]{1,2,0:T(8,128)(2,1)S(1)}, u32[]{:S(2)}, u32[]{:S(2)}) collective-permute-start(bf16[2,128,720]{1,2,0:T(8,128)(2,1)S(1)} %collective-permute-done.9), channel_id=1, source_target_pairs={{0,4},{1,5},{2,6},{3,7},{4,8},{5,9},{6,10},{7,11},{8,12},{9,13},{1... | collective-permute-start | bytes 1105928 | tf_op jit(solution)/shard_map/ppermute | solution.py:152
  193.2 8.7 %collective-permute-start.13 = (bf16[2,128,720]{1,2,0:T(8,128)(2,1)S(1)}, bf16[2,128,720]{1,2,0:T(8,128)(2,1)S(1)}, u32[]{:S(2)}, u32[]{:S(2)}) collective-permute-start(bf16[2,128,720]{1,2,0:T(8,128)(2,1)S(1)} %collective-permute-done.12), channel_id=1, source_target_pairs={{0,12},{1,13},{2,14},{3,15},{4,0},{5,1},{6,2},{7,3},{8,4},{9,5},{1... | collective-permute-start | bytes 1105928 | tf_op jit(solution)/shard_map/ppermute | solution.py:152
  201.9 9.9 %collective-permute-start.11 = (bf16[2,128,720]{1,2,0:T(8,128)(2,1)S(1)}, bf16[2,128,720]{1,2,0:T(8,128)(2,1)S(1)}, u32[]{:S(2)}, u32[]{:S(2)}) collective-permute-start(bf16[2,128,720]{1,2,0:T(8,128)(2,1)S(1)} %collective-permute-done.10), channel_id=1, source_target_pairs={{0,4},{1,5},{2,6},{3,7},{4,8},{5,9},{6,10},{7,11},{8,12},{9,13},{1... | collective-permute-start | bytes 1105928 | tf_op jit(solution)/shard_map/ppermute | solution.py:152
  201.9 10.0 %collective-permute-start.14 = (bf16[2,128,720]{1,2,0:T(8,128)(2,1)S(1)}, bf16[2,128,720]{1,2,0:T(8,128)(2,1)S(1)}, u32[]{:S(2)}, u32[]{:S(2)}) collective-permute-start(bf16[2,128,720]{1,2,0:T(8,128)(2,1)S(1)} %collective-permute-done.13), channel_id=1, source_target_pairs={{0,12},{1,13},{2,14},{3,15},{4,0},{5,1},{6,2},{7,3},{8,4},{9,5},{1... | collective-permute-start | bytes 1105928 | tf_op jit(solution)/shard_map/ppermute | solution.py:152
  214.0 30.8 %collective-permute-start.15 = (bf16[4,2,256,720]{2,3,1,0:T(8,128)(2,1)}, bf16[4,2,256,720]{2,3,1,0:T(8,128)(2,1)}, u32[]{:S(2)}, u32[]{:S(2)}) collective-permute-start(bf16[4,2,256,720]{2,3,1,0:T(8,128)(2,1)} %get-tuple-element.13), channel_id=1, source_target_pairs={{0,1},{1,0},{2,3},{3,2},{4,5},{5,4},{6,7},{7,6},{8,9},{9,8},{10,11... | collective-permute-start | bytes 8847368 | tf_op jit(solution)/shard_map/ppermute | solution.py:185
  231.5 43.5 %all-to-all-start.2 = ((bf16[2,16,16,2304]{3,2,0,1:T(8,128)(2,1)}), bf16[2,16,16,2304]{3,2,0,1:T(8,128)(2,1)}, u32[]{:S(2)}, u32[]{:S(2)}) async-start(bf16[2,16,16,2304]{3,2,0,1:T(8,128)(2,1)} %bitcast.77), calls=%async_computation.2 | async-start | bytes 4718592 | tf_op jit(solution)/shard_map/all_to_all | solution.py:29
  275.0 14.4 %all-to-all-start.1 = ((bf16[8,256,144]{1,2,0:T(8,128)(2,1)}), bf16[8,256,144]{1,2,0:T(8,128)(2,1)S(1)}, u32[]{:S(2)}, u32[]{:S(2)}) async-start(bf16[8,256,144]{1,2,0:T(8,128)(2,1)} %copy.51), calls=%async_computation.1 | async-start | bytes 1179648 | tf_op jit(solution)/shard_map/all_to_all | solution.py:99
  283.2 7.0 %copy-start.1 = (s32[1,16]{1,0:T(1,128)S(1)}, s32[1,16]{1,0:T(1,128)}, u32[]{:S(2)}) copy-start(s32[1,16]{1,0:T(1,128)} %param.19) | copy-start | bytes 196

commit v9 on v8

--- a/solution.py
+++ b/solution.py
@@ -129,15 +129,17 @@
     return lax.dynamic_index_in_dim(chunks, index, axis, keepdims=False)
 
 
-def ring_reduce(chunks, xi, axis_name, direction):
+def ring_reduce(chunks, xi, axis_name, direction, sub):
     count = chunks.shape[0]
     perm = col_perm(axis_name, lambda c: x_step(c, direction))
-    cur = pick(chunks, (xi - direction) % count)
+
+    def own(index):
+        return pick(chunks, index % count)[:, sub]
+
+    cur = own(xi - direction)
     for s in range(1, count):
         recv = lax.ppermute(cur, axis_name, perm)
-        cur = recv.astype(jnp.float32) + pick(chunks, (xi - direction * (s + 1)) % count).astype(
-            jnp.float32
-        )
+        cur = recv.astype(jnp.float32) + own(xi - direction * (s + 1)).astype(jnp.float32)
         if s < count - 1:
             cur = cur.astype(chunks.dtype)
     return cur
@@ -158,14 +160,13 @@
     c = lax.axis_index(axis_name)
     xi, zi = c // 4, (c // 2) % 2
     rows = other.shape[1] // 4
-    shape = (4, 2, rows, other.shape[2])
+    shape = (4, 2, 2, rows // 2, other.shape[2])
     recv = lax.ppermute(other.reshape(shape), axis_name, col_perm(axis_name, lambda q: q ^ 1))
     core_sum = (mine.reshape(shape).astype(jnp.float32) + recv.astype(jnp.float32)).astype(
         other.dtype
     )
-    half = rows // 2
-    plus = ring_reduce(core_sum[:, :, :half], xi, axis_name, 1)
-    minus = ring_reduce(core_sum[:, :, half:], xi, axis_name, -1)
+    plus = ring_reduce(core_sum, xi, axis_name, 1, 0)
+    minus = ring_reduce(core_sum, xi, axis_name, -1, 1)
     x_sum = jnp.concatenate([plus, minus], axis=1)
     recv = lax.ppermute(
         pick(x_sum, 1 - zi).astype(other.dtype), axis_name, col_perm(axis_name, lambda q: q ^ 2)
@@ -203,7 +204,10 @@
     gathered = gather_rows(tokens, "row")
     token_count = gathered.shape[0]
     hidden_width = gate_weight.shape[2]
-    paired = jnp.concatenate([gate_weight, up_weight], axis=2)
+    experts, width, _ = gate_weight.shape
+    padded_width = -(-hidden_width // 128) * 128
+    pad = jnp.zeros((experts, width, padded_width - hidden_width), gate_weight.dtype)
+    paired = jnp.concatenate([gate_weight, pad, up_weight, pad], axis=2)
     core = lax.axis_index("col") % 2
     other = gate_up(route_ids, gathered, paired, 256, 1 - core)
     mine = gate_up(route_ids, gathered, paired, 256, core)
@@ -213,12 +217,13 @@
         route_weight.T.reshape(-1), lax.axis_index("col") * share_rows, share_rows, 0
     )
     hidden = (
-        own_weight[:, None] * jax.nn.silu(summed[:, :hidden_width]) * summed[:, hidden_width:]
+        own_weight[:, None] * jax.nn.silu(summed[:, :padded_width]) * summed[:, padded_width:]
     ).astype(jnp.bfloat16)
-    hidden_all = col_all_gather(hidden, "col").reshape(
-        2, token_count, hidden_width
-    )
-    per_token = down(route_ids, hidden_all, down_weight, 256)
+    hidden_all = col_all_gather(hidden, "col").reshape(2, token_count, padded_width)
+    down_pad = jnp.zeros(
+        (experts, padded_width - hidden_width, down_weight.shape[2]), down_weight.dtype
+    )
+    per_token = down(route_ids, hidden_all, jnp.concatenate([down_weight, down_pad], axis=1), 256)
     mixed = sum_scatter_rows(per_token, "row").astype(jnp.bfloat16)
     return (mixed, decode_cache)
 

time: 292 us -> 264 us (0.904)
  local copies, waits for them, and re-layouts: 60.3 us -> 42.5 us
  other arithmetic: 43.2 us -> 27 us
  waiting for transfers between devices: 87 us -> 93 us
    concatenate x0 -> x2, local copies, waits for them, and re-layouts: none -> 10.3 us  [the longest x1 6.28 us: shards(): paired = jnp.concatenate([gate_weight, pad, up_weight, pad], axis=2)]
    convert_element_type x1 -> x0, local copies, waits for them, and re-layouts: 9.25 us -> none  [col_reduce_scatter(): mine.reshape(shape).astype(jnp.float32) + recv.astype(jnp.float32)]
    select_n x1 -> x0, local copies, waits for them, and re-layouts: 8.54 us -> none  [col_all_gather(): jnp.where(co == 0, jnp.stack([x_all, recv], axis=2), jnp.stack([recv, x_a...]
    reshape x1 -> x0, local copies, waits for them, and re-layouts: 8.49 us -> none  [col_reduce_scatter(): other.reshape(shape)]
    convert_element_type x4, other arithmetic: 9.16 us -> 3.12 us  [ring_reduce(): cur = cur.astype(chunks.dtype)]
    concatenate x1 -> x0, other arithmetic: 4.51 us -> none  [shards(): paired = jnp.concatenate([gate_weight, up_weight], axis=2)]
    ppermute x6, waiting for transfers between devices: 44.4 us -> 48.2 us  [ring_reduce(): recv = lax.ppermute(cur, axis_name, perm)]
    dynamic_slice x0 -> x7, local copies, waits for them, and re-layouts: none -> 3.55 us  [pick(): return lax.dynamic_index_in_dim(chunks, index, axis, keepdims=False)]
  transfers between devices with their start and end apart: 19 -> 19, of which waited for: 12 -> 13; matrix products, arithmetic and copies ran while one was open for 24% -> 19% of each run, Pallas kernels for 10% -> 12%
where the time goes in v9:
time: 264 us; the launch traced here: 262 us
  waiting for transfers between devices  93 us (35%)
  starting transfers between devices  50.9 us (19%)
  Pallas kernels  47.8 us (18%)
  local copies, waits for them, and re-layouts  42.5 us (16%)
  other arithmetic  27 us (10%)
    ppermute x6, waiting for transfers between devices, ring_reduce(): recv = lax.ppermute(cur, axis_name, perm)  48.2 us
    pallas_call x2, Pallas kernels, gate_up(): pl.pallas_call(gate_up_kernel, grid_spec=pltpu.PrefetchScalarGridSpec(num...  34.8 us
    ppermute x6, waiting for transfers between devices, ring_gather(): cur = lax.ppermute(cur, axis_name, perm)  18.3 us
    ppermute x1, waiting for transfers between devices, col_reduce_scatter(): lax.ppermute(pick(x_sum, 1 - zi).astype(other.dtype), axis_name, col_perm...  14.5 us
    pallas_call x1, Pallas kernels, down(): pl.pallas_call(down_kernel, grid=(token_count // tile,), in_specs=[pl.Blo...  13.1 us
    unnamed x26, local copies, waits for them, and re-layouts  11.3 us
    ppermute x6, starting transfers between devices, ring_reduce(): recv = lax.ppermute(cur, axis_name, perm)  10 us
    ppermute x6, starting transfers between devices, ring_gather(): cur = lax.ppermute(cur, axis_name, perm)  8.37 us
  transfers between devices with their start and end apart: 19, of which 13 were waited for; matrix products, arithmetic and copies ran while one was open for 19% of the time, Pallas kernels for 12%

profile of v9, /device:TPU:1, one launch (start us, length us, event | category | flops | bytes accessed | tf_op | source)
XLA Modules:
  0.0 262.5 jit_solution(1966157796020235247)
XLA Ops:
  2.5 6.4 %all-to-all-start = ((bf16[8,256,144]{1,2,0:T(8,128)(2,1)}), bf16[8,256,144]{1,2,0:T(8,128)(2,1)S(1)}, u32[]{:S(2)}, u32[]{:S(2)}) async-start(bf16[8,256,144]{1,2,0:T(8,128)(2,1)} %broadcast_in_dim.68), calls=%async_computation | async-start | bytes 1179648 | tf_op jit(solution)/shard_map/all_to_all | solution.py:92
  10.3 6.3 %concatenate.12.w_ref = bf16[8,144,1536]{2,1,0:T(8,128)(2,1)} concatenate(bf16[8,144,720]{2,1,0:T(8,128)(2,1)S(1)} %copy-done.6, bf16[8,144,48]{2,1,0:T(8,128)(2,1)S(1)} %broadcast_in_dim.69, bf16[8,144,720]{2,1,0:T(8,128)(2,1)} %param.12, bf16[8,144,48]{2,1,0:T(8,128)(2,1)S(1)} %broadcast_in_dim.69), dimensions={2} | concatenate | bytes 7077888 | tf_op jit(solution)/shard_map/concatenate | solution.py:210
  16.6 3.2 %all-to-all-done = bf16[8,256,144]{1,2,0:T(8,128)(2,1)S(1)} async-done(((bf16[8,256,144]{1,2,0:T(8,128)(2,1)}), bf16[8,256,144]{1,2,0:T(8,128)(2,1)S(1)}, u32[]{:S(2)}, u32[]{:S(2)}) %all-to-all-start) | async-done | bytes 589856 | tf_op jit(solution)/shard_map/all_to_all | solution.py:92
  21.1 17.4 %shard_map.114 = bf16[2,1024,1536]{2,1,0:T(8,128)(2,1)} custom-call(s32[1]{0:T(128)} %bitcast.4.sel_ref, s32[2048,2]{1,0:T(8,128)} %copy.84.ids_ref, bf16[2048,144]{1,0:T(8,128)(2,1)} %bitcast.108, bf16[8,144,1536]{2,1,0:T(8,128)(2,1)} %concatenate.12.w_ref), custom_call_target="tpu_custom_call" | custom-call | tf_op jit(solution)/shard_map/pallas_call | solution.py:73
  39.3 17.4 %shard_map.113 = bf16[2,1024,1536]{2,1,0:T(8,128)(2,1)} custom-call(s32[1]{0:T(128)} %bitcast.1.sel_ref, s32[2048,2]{1,0:T(8,128)} %copy.84.ids_ref, bf16[2048,144]{1,0:T(8,128)(2,1)} %bitcast.109, bf16[8,144,1536]{2,1,0:T(8,128)(2,1)} %concatenate.12.w_ref), custom_call_target="tpu_custom_call" | custom-call | tf_op jit(solution)/shard_map/pallas_call | solution.py:73
  56.7 6.8 %fusion = bf16[4,2,2,128,1536]{4,3,2,1,0:T(8,128)(2,1)S(1)} fusion(bf16[4,2,2,128,1536]{4,3,2,1,0:T(8,128)(2,1)} %bitcast.106, bf16[4,2,2,128,1536]{4,3,2,1,0:T(8,128)(2,1)} %collective-permute-done), kind=kLoop, calls=%fused_computation.6 | loop fusion | flops 12582912 | bytes 18874368 | tf_op jit(solution)/shard_map/convert_element_type | solution.py:165
  63.4 2.9 %constant_dynamic-slice_fusion.3 = (bf16[1,2,2,128,1536]{4,3,2,1,0:T(8,128)(2,1)}, bf16[1,2,2,128,1536]{4,3,2,1,0:T(8,128)(2,1)}, bf16[1,2,2,128,1536]{4,3,2,1,0...) fusion(bf16[4,2,2,128,1536]{4,3,2,1,0:T(8,128)(2,1)S(1)} %fusio, ...), kind=kLoop, calls=%fused_computation.64 | loop fusion | bytes 25165856 | tf_op jit(solution)/shard_map/jit(dynamic_index_in_dim)/dynamic_slice | solution.py:129
  69.6 16.4 %collective-permute-done.4 = bf16[2,128,1536]{2,1,0:T(8,128)(2,1)S(1)} collective-permute-done((bf16[2,128,1536]{2,1,0:T(8,128)(2,1)S(1)}, bf16[2,128,1536]{2,1,0:T(8,128)(2,1)S(1)}, u32[]{:S(2)}, u32[]{:S(2)}) %collective-permute-start.4) | collective-permute-done | bytes 786464 | tf_op jit(solution)/shard_map/ppermute | solution.py:141
  86.2 3.5 %collective-permute-start.5 = (bf16[2,128,1536]{2,1,0:T(8,128)(2,1)S(1)}, bf16[2,128,1536]{2,1,0:T(8,128)(2,1)}, u32[]{:S(2)}, u32[]{:S(2)}) collective-permute-start(bf16[2,128,1536]{2,1,0:T(8,128)(2,1)S(1)} %fusion.7), channel_id=1, source_target_pairs={{0,12},{1,13},{2,14},{3,15},{4,0},{5,1},{6,2},{7,3},{8,4},{9,5},{1... | collective-permute-start | bytes 2359304 | tf_op jit(solution)/shard_map/ppermute | solution.py:141
  91.7 14.0 %collective-permute-done.5 = bf16[2,128,1536]{2,1,0:T(8,128)(2,1)} collective-permute-done((bf16[2,128,1536]{2,1,0:T(8,128)(2,1)S(1)}, bf16[2,128,1536]{2,1,0:T(8,128)(2,1)}, u32[]{:S(2)}, u32[]{:S(2)}) %collective-permute-start.5) | collective-permute-done | bytes 786464 | tf_op jit(solution)/shard_map/ppermute | solution.py:141
  107.1 3.6 %collective-permute-start.6 = (bf16[2,128,1536]{2,1,0:T(8,128)(2,1)S(1)}, bf16[2,128,1536]{2,1,0:T(8,128)(2,1)S(1)}, u32[]{:S(2)}, u32[]{:S(2)}) collective-permute-start(bf16[2,128,1536]{2,1,0:T(8,128)(2,1)S(1)} %fusion.6), channel_id=1, source_target_pairs={{0,12},{1,13},{2,14},{3,15},{4,0},{5,1},{6,2},{7,3},{8,4},{9,5},{1... | collective-permute-start | bytes 2359304 | tf_op jit(solution)/shard_map/ppermute | solution.py:141
  112.3 13.5 %collective-permute-done.6 = bf16[2,128,1536]{2,1,0:T(8,128)(2,1)S(1)} collective-permute-done((bf16[2,128,1536]{2,1,0:T(8,128)(2,1)S(1)}, bf16[2,128,1536]{2,1,0:T(8,128)(2,1)S(1)}, u32[]{:S(2)}, u32[]{:S(2)}) %collective-permute-start.6) | collective-permute-done | bytes 786464 | tf_op jit(solution)/shard_map/ppermute | solution.py:141
  126.1 4.3 %collective-permute-done.3 = bf16[2,128,1536]{2,1,0:T(8,128)(2,1)S(1)} collective-permute-done((bf16[2,128,1536]{2,1,0:T(8,128)(2,1)S(1)}, bf16[2,128,1536]{2,1,0:T(8,128)(2,1)S(1)}, u32[]{:S(2)}, u32[]{:S(2)}) %collective-permute-start.3) | collective-permute-done | bytes 786464 | tf_op jit(solution)/shard_map/ppermute | solution.py:141
  131.8 3.3 %collective-permute-start.7 = (bf16[256,1536]{1,0:T(8,128)(2,1)S(1)}, bf16[256,1536]{1,0:T(8,128)(2,1)}, u32[]{:S(2)}, u32[]{:S(2)}) collective-permute-start(bf16[256,1536]{1,0:T(8,128)(2,1)S(1)} %fusion.10), channel_id=1, source_target_pairs={{0,2},{1,3},{2,0},{3,1},{4,6},{5,7},{6,4},{7,5},{8,10},{9,11},{10,... | collective-permute-start | bytes 2359304 | tf_op jit(solution)/shard_map/ppermute | solution.py:171
  135.7 14.5 %collective-permute-done.7 = bf16[256,1536]{1,0:T(8,128)(2,1)} collective-permute-done((bf16[256,1536]{1,0:T(8,128)(2,1)S(1)}, bf16[256,1536]{1,0:T(8,128)(2,1)}, u32[]{:S(2)}, u32[]{:S(2)}) %collective-permute-start.7) | collective-permute-done | bytes 786464 | tf_op jit(solution)/shard_map/ppermute | solution.py:171
  152.1 2.8 %collective-permute-start.8 = (bf16[256,768]{1,0:T(8,128)(2,1)S(1)}, bf16[256,768]{1,0:T(8,128)(2,1)S(1)}, u32[]{:S(2)}, u32[]{:S(2)}) collective-permute-start(bf16[256,768]{1,0:T(8,128)(2,1)S(1)} %fusion.11), channel_id=1, source_target_pairs={{0,2},{1,3},{2,0},{3,1},{4,6},{5,7},{6,4},{7,5},{8,10},{9,11},{10,... | collective-permute-start | bytes 1179656 | tf_op jit(solution)/shard_map/ppermute | solution.py:180
  155.9 5.0 %collective-permute-done.8 = bf16[256,768]{1,0:T(8,128)(2,1)S(1)} collective-permute-done((bf16[256,768]{1,0:T(8,128)(2,1)S(1)}, bf16[256,768]{1,0:T(8,128)(2,1)S(1)}, u32[]{:S(2)}, u32[]{:S(2)}) %collective-permute-start.8) | collective-permute-done | bytes 393248 | tf_op jit(solution)/shard_map/ppermute | solution.py:180
  164.2 4.9 %collective-permute-done.9 = bf16[2,128,768]{2,1,0:T(8,128)(2,1)S(1)} collective-permute-done((bf16[2,128,768]{2,1,0:T(8,128)(2,1)S(1)}, bf16[2,128,768]{2,1,0:T(8,128)(2,1)S(1)}, u32[]{:S(2)}, u32[]{:S(2)}) %collective-permute-start.9) | collective-permute-done | bytes 393248 | tf_op jit(solution)/shard_map/ppermute | solution.py:154
  171.8 6.2 %collective-permute-done.10 = bf16[2,128,768]{2,1,0:T(8,128)(2,1)S(1)} collective-permute-done((bf16[2,128,768]{2,1,0:T(8,128)(2,1)S(1)}, bf16[2,128,768]{2,1,0:T(8,128)(2,1)S(1)}, u32[]{:S(2)}, u32[]{:S(2)}) %collective-permute-start.10) | collective-permute-done | bytes 393248 | tf_op jit(solution)/shard_map/ppermute | solution.py:154
  178.0 3.0 %collective-permute-start.14 = (bf16[2,128,768]{2,1,0:T(8,128)(2,1)S(1)}, bf16[2,128,768]{2,1,0:T(8,128)(2,1)S(1)}, u32[]{:S(2)}, u32[]{:S(2)}) collective-permute-start(bf16[2,128,768]{2,1,0:T(8,128)(2,1)S(1)} %collective-permute-done.13), channel_id=1, source_target_pairs={{0,12},{1,13},{2,14},{3,15},{4,0},{5,1},{6,2},{7,3},{8,4},{9,5},{1... | collective-permute-start | bytes 1179656 | tf_op jit(solution)/shard_map/ppermute | solution.py:154
  181.0 7.1 %collective-permute-done.11 = bf16[2,128,768]{2,1,0:T(8,128)(2,1)S(1)} collective-permute-done((bf16[2,128,768]{2,1,0:T(8,128)(2,1)S(1)}, bf16[2,128,768]{2,1,0:T(8,128)(2,1)S(1)}, u32[]{:S(2)}, u32[]{:S(2)}) %collective-permute-start.11) | collective-permute-done | bytes 393248 | tf_op jit(solution)/shard_map/ppermute | solution.py:154
  190.5 7.7 %collective-permute-start.15 = (bf16[4,2,256,768]{3,2,1,0:T(8,128)(2,1)}, bf16[4,2,256,768]{3,2,1,0:T(8,128)(2,1)}, u32[]{:S(2)}, u32[]{:S(2)}) collective-permute-start(bf16[4,2,256,768]{3,2,1,0:T(8,128)(2,1)} %get-tuple-element.19), channel_id=1, source_target_pairs={{0,1},{1,0},{2,3},{3,2},{4,5},{5,4},{6,7},{7,6},{8,9},{9,8},{10,11... | collective-permute-start | bytes 9437192 | tf_op jit(solution)/shard_map/ppermute | solution.py:186
  201.0 3.3 %broadcast_select_fusion = bf16[2,16,16,2304]{3,2,1,0:T(8,128)(2,1)} fusion(bf16[2,16,16,2304]{3,2,1,0:T(8,128)(2,1)} %param.16, pred[16]{0:T(512)(128)(4,1)S(1)} %iota_compare_fusion.1), kind=kLoop, calls=%fused_computation.13 | loop fusion | flops 1179648 | bytes 4718608 | tf_op jit(solution)/shard_map/jit(_where)/select_n | solution.py:26
  204.3 3.7 %gather_fusion = bf16[16,2,16,2304]{3,2,1,0:T(8,128)(2,1)} fusion(bf16[2,16,16,2304]{3,2,1,0:T(8,128)(2,1)} %broadcast_select_fusion, s32[1024]{0:T(1024)S(1)} %pad_clamp_fusion.1), kind=kCustom, calls=%fused_computation | custom fusion | bytes 4718656 | tf_op jit(solution)/shard_map/gather | solution.py:30
  208.0 8.1 %all-to-all-start.2 = ((bf16[2,16,16,2304]{3,2,0,1:T(8,128)(2,1)}), bf16[2,16,16,2304]{3,2,0,1:T(8,128)(2,1)}, u32[]{:S(2)}, u32[]{:S(2)}) async-start(bf16[2,16,16,2304]{3,2,0,1:T(8,128)(2,1)} %bitcast.110), calls=%async_computation.2 | async-start | bytes 4718592 | tf_op jit(solution)/shard_map/all_to_all | solution.py:29
  216.1 4.3 %copy.83 = bf16[8,720,144]{2,1,0:T(8,128)(2,1)} copy(bf16[8,720,144]{1,2,0:T(8,128)(2,1)} %param.13) | data formatting | bytes 3317760 | tf_op args[3]
  220.5 4.0 %concatenate.15.d_ref = bf16[8,768,144]{2,1,0:T(8,128)(2,1)} pad(bf16[8,720,144]{2,1,0:T(8,128)(2,1)} %copy.83, bf16[]{:T(256)} %constant.178.clone.1), padding=0_0x0_48x0_0 | pad | bytes 3428354 | tf_op jit(solution)/shard_map/concatenate | solution.py:226
  224.4 6.9 %maximum_select_fusion = bf16[4,2,2,256,768]{4,3,2,1,0:T(8,128)(2,1)} fusion(bf16[4,2,1,256,768]{4,3,2,1,0:T(8,128)(2,1)} %bitcast.35, bf16[4,2,1,256,768]{4,3,2,1,0:T(8,128)(2,1)S(1)} %get-tuple-element.18, pred[]{:T(512)S(6)} %eq.55), kind=kLoop, calls=%fused_computation.7 | loop fusion | flops 9437184 | bytes 12582913 | tf_op jit(solution)/shard_map/jit(_where)/select_n | solution.py:187
  231.3 13.1 %shard_map.115 = bf16[2048,144]{1,0:T(8,128)(2,1)} custom-call(s32[2048,2]{1,0:T(8,128)} %copy.84.ids_ref, bf16[2,2048,768]{2,1,0:T(8,128)(2,1)} %bitcast.107, bf16[8,768,144]{2,1,0:T(8,128)(2,1)} %concatenate.15.d_ref), custom_call_target="tpu_custom_call" | custom-call | tf_op jit(solution)/shard_map/pallas_call | solution.py:106
  247.3 3.5 %all-to-all-start.1 = ((bf16[8,256,144]{1,2,0:T(8,128)(2,1)}), bf16[8,256,144]{1,2,0:T(8,128)(2,1)S(1)}, u32[]{:S(2)}, u32[]{:S(2)}) async-start(bf16[8,256,144]{1,2,0:T(8,128)(2,1)} %copy.85), calls=%async_computation.1 | async-start | bytes 1179648 | tf_op jit(solution)/shard_map/all_to_all | solution.py:99
  255.5 3.2 %copy.89 = bf16[2,16,16,2304]{3,2,1,0:T(8,128)(2,1)} copy(bf16[2,16,16,2304]{3,2,0,1:T(8,128)(2,1)} %bitcast.111) | data formatting | bytes 4718592
  258.8 3.0 %all-to-all-done.1 = bf16[8,256,144]{1,2,0:T(8,128)(2,1)S(1)} async-done(((bf16[8,256,144]{1,2,0:T(8,128)(2,1)}), bf16[8,256,144]{1,2,0:T(8,128)(2,1)S(1)}, u32[]{:S(2)}, u32[]{:S(2)}) %all-to-all-start.1) | async-done | bytes 589856 | tf_op jit(solution)/shard_map/all_to_all | solution.py:99
  (102 shorter events, 38.1 us)
Async XLA Ops:
  0.6 154.4 %copy-start = (s32[1,16]{1,0:T(1,128)S(1)}, s32[1,16]{1,0:T(1,128)}, u32[]{:S(2)}) copy-start(s32[1,16]{1,0:T(1,128)} %param.19) | copy-start | bytes 196
  0.6 8.3 %copy-start.8 = (s32[2048,2]{0,1:T(2,128)S(1)}, s32[2048,2]{0,1:T(2,128)}, u32[]{:S(2)}) copy-start(s32[2048,2]{0,1:T(2,128)} %param.14) | copy-start | bytes 49156
  0.7 9.7 %copy-start.6 = (bf16[8,144,720]{2,1,0:T(8,128)(2,1)S(1)}, bf16[8,144,720]{2,1,0:T(8,128)(2,1)}, u32[]{:S(2)}) copy-start(bf16[8,144,720]{2,1,0:T(8,128)(2,1)} %param.11) | copy-start | bytes 4976644
  2.5 17.3 %all-to-all-start = ((bf16[8,256,144]{1,2,0:T(8,128)(2,1)}), bf16[8,256,144]{1,2,0:T(8,128)(2,1)S(1)}, u32[]{:S(2)}, u32[]{:S(2)}) async-start(bf16[8,256,144]{1,2,0:T(8,128)(2,1)} %broadcast_in_dim.68), calls=%async_computation | async-start | bytes 1179648 | tf_op jit(solution)/shard_map/all_to_all | solution.py:92
  38.5 18.2 %collective-permute-start = (bf16[4,2,2,128,1536]{4,3,2,1,0:T(8,128)(2,1)}, bf16[4,2,2,128,1536]{4,3,2,1,0:T(8,128)(2,1)}, u32[]{:S(2)}, u32[]{:S(2)}) collective-permute-start(bf16[4,2,2,128,1536]{4,3,2,1,0:T(8,128)(2,1)} %bitcast.112), channel_id=1, source_target_pairs={{0,1},{1,0},{2,3},{3,2},{4,5},{5,4},{6,7},{7,6},{8,9},{9,8},{10,11... | collective-permute-start | bytes 18874376 | tf_op jit(solution)/shard_map/ppermute | solution.py:164
  66.5 19.4 %collective-permute-start.4 = (bf16[2,128,1536]{2,1,0:T(8,128)(2,1)S(1)}, bf16[2,128,1536]{2,1,0:T(8,128)(2,1)S(1)}, u32[]{:S(2)}, u32[]{:S(2)}) collective-permute-start(bf16[2,128,1536]{2,1,0:T(8,128)(2,1)S(1)} %slice_bitcast_fusion.3), channel_id=1, source_target_pairs={{0,12},{1,13},{2,14},{3,15},{4,0},{5,1},{6,2},{7,3},{8,4},{9,5},{1... | collective-permute-start | bytes 2359304 | tf_op jit(solution)/shard_map/ppermute | solution.py:141
  69.3 20.4 %collective-permute-start.1 = (bf16[2,128,1536]{2,1,0:T(8,128)(2,1)S(1)}, bf16[2,128,1536]{2,1,0:T(8,128)(2,1)S(1)}, u32[]{:S(2)}, u32[]{:S(2)}) collective-permute-start(bf16[2,128,1536]{2,1,0:T(8,128)(2,1)S(1)} %slice_bitcast_fusion.7), channel_id=1, source_target_pairs={{0,4},{1,5},{2,6},{3,7},{4,8},{5,9},{6,10},{7,11},{8,12},{9,13},{1... | collective-permute-start | bytes 2359304 | tf_op jit(solution)/shard_map/ppermute | solution.py:141
  86.2 4.0 %copy-start.3 = (bf16[1,2,2,128,1536]{4,3,2,1,0:T(8,128)(2,1)S(1)}, bf16[1,2,2,128,1536]{4,3,2,1,0:T(8,128)(2,1)}, u32[]{:S(2)}) copy-start(bf16[1,2,2,128,1536]{4,3,2,1,0:T(8,128)(2,1)} %get-tuple-element.11) | copy-start | bytes 4718596
  86.2 19.5 %collective-permute-start.5 = (bf16[2,128,1536]{2,1,0:T(8,128)(2,1)S(1)}, bf16[2,128,1536]{2,1,0:T(8,128)(2,1)}, u32[]{:S(2)}, u32[]{:S(2)}) collective-permute-start(bf16[2,128,1536]{2,1,0:T(8,128)(2,1)S(1)} %fusion.7), channel_id=1, source_target_pairs={{0,12},{1,13},{2,14},{3,15},{4,0},{5,1},{6,2},{7,3},{8,4},{9,5},{1... | collective-permute-start | bytes 2359304 | tf_op jit(solution)/shard_map/ppermute | solution.py:141
  89.8 20.9 %collective-permute-start.2 = (bf16[2,128,1536]{2,1,0:T(8,128)(2,1)S(1)}, bf16[2,128,1536]{2,1,0:T(8,128)(2,1)}, u32[]{:S(2)}, u32[]{:S(2)}) collective-permute-start(bf16[2,128,1536]{2,1,0:T(8,128)(2,1)S(1)} %fusion.9), channel_id=1, source_target_pairs={{0,4},{1,5},{2,6},{3,7},{4,8},{5,9},{6,10},{7,11},{8,12},{9,13},{1... | collective-permute-start | bytes 2359304 | tf_op jit(solution)/shard_map/ppermute | solution.py:141
  90.2 1.4 copy-start.2
  105.7 6.4 %copy-start.5 = (bf16[1,2,2,128,1536]{4,3,2,1,0:T(8,128)(2,1)S(1)}, bf16[1,2,2,128,1536]{4,3,2,1,0:T(8,128)(2,1)}, u32[]{:S(2)}) copy-start(bf16[1,2,2,128,1536]{4,3,2,1,0:T(8,128)(2,1)} %get-tuple-element.14) | copy-start | bytes 4718596
  107.1 5.0 %copy-start.4 = (bf16[1,2,2,128,1536]{4,3,2,1,0:T(8,128)(2,1)S(1)}, bf16[1,2,2,128,1536]{4,3,2,1,0:T(8,128)(2,1)}, u32[]{:S(2)}) copy-start(bf16[1,2,2,128,1536]{4,3,2,1,0:T(8,128)(2,1)} %get-tuple-element.10) | copy-start | bytes 4718596
  107.1 18.7 %collective-permute-start.6 = (bf16[2,128,1536]{2,1,0:T(8,128)(2,1)S(1)}, bf16[2,128,1536]{2,1,0:T(8,128)(2,1)S(1)}, u32[]{:S(2)}, u32[]{:S(2)}) collective-permute-start(bf16[2,128,1536]{2,1,0:T(8,128)(2,1)S(1)} %fusion.6), channel_id=1, source_target_pairs={{0,12},{1,13},{2,14},{3,15},{4,0},{5,1},{6,2},{7,3},{8,4},{9,5},{1... | collective-permute-start | bytes 2359304 | tf_op jit(solution)/shard_map/ppermute | solution.py:141
  112.0 18.4 %collective-permute-start.3 = (bf16[2,128,1536]{2,1,0:T(8,128)(2,1)S(1)}, bf16[2,128,1536]{2,1,0:T(8,128)(2,1)S(1)}, u32[]{:S(2)}, u32[]{:S(2)}) collective-permute-start(bf16[2,128,1536]{2,1,0:T(8,128)(2,1)S(1)} %fusion.8), channel_id=1, source_target_pairs={{0,4},{1,5},{2,6},{3,7},{4,8},{5,9},{6,10},{7,11},{8,12},{9,13},{1... | collective-permute-start | bytes 2359304 | tf_op jit(solution)/shard_map/ppermute | solution.py:141
  130.6 1.1 copy-start.1
  130.6 4.4 %copy-start.9 = (f32[2048,2]{0,1:T(2,128)S(1)}, f32[2048,2]{0,1:T(2,128)}, u32[]{:S(2)}) copy-start(f32[2048,2]{0,1:T(2,128)} %param.15) | copy-start | bytes 49156
  130.6 4.4 %copy-start.7 = (s32[1,16,16]{2,1,0:T(8,128)S(1)}, s32[1,16,16]{2,1,0:T(8,128)}, u32[]{:S(2)}) copy-start(s32[1,16,16]{2,1,0:T(8,128)} %param.17) | copy-start | bytes 3076
  131.8 18.5 %collective-permute-start.7 = (bf16[256,1536]{1,0:T(8,128)(2,1)S(1)}, bf16[256,1536]{1,0:T(8,128)(2,1)}, u32[]{:S(2)}, u32[]{:S(2)}) collective-permute-start(bf16[256,1536]{1,0:T(8,128)(2,1)S(1)} %fusion.10), channel_id=1, source_target_pairs={{0,2},{1,3},{2,0},{3,1},{4,6},{5,7},{6,4},{7,5},{8,10},{9,11},{10,... | collective-permute-start | bytes 2359304 | tf_op jit(solution)/shard_map/ppermute | solution.py:171
  151.8 3.1 %copy-start.10 = (s32[1,16,16]{2,1,0:T(8,128)S(1)}, s32[1,16,16]{2,1,0:T(8,128)}, u32[]{:S(2)}) copy-start(s32[1,16,16]{2,1,0:T(8,128)} %param.18) | copy-start | bytes 3076
  152.1 8.8 %collective-permute-start.8 = (bf16[256,768]{1,0:T(8,128)(2,1)S(1)}, bf16[256,768]{1,0:T(8,128)(2,1)S(1)}, u32[]{:S(2)}, u32[]{:S(2)}) collective-permute-start(bf16[256,768]{1,0:T(8,128)(2,1)S(1)} %fusion.11), channel_id=1, source_target_pairs={{0,2},{1,3},{2,0},{3,1},{4,6},{5,7},{6,4},{7,5},{8,10},{9,11},{10,... | collective-permute-start | bytes 1179656 | tf_op jit(solution)/shard_map/ppermute | solution.py:180
  161.1 7.9 %collective-permute-start.9 = (bf16[2,128,768]{2,1,0:T(8,128)(2,1)S(1)}, bf16[2,128,768]{2,1,0:T(8,128)(2,1)S(1)}, u32[]{:S(2)}, u32[]{:S(2)}) collective-permute-start(bf16[2,128,768]{2,1,0:T(8,128)(2,1)S(1)} %get-tuple-element.20), channel_id=1, source_target_pairs={{0,4},{1,5},{2,6},{3,7},{4,8},{5,9},{6,10},{7,11},{8,12},{9,13},{1... | collective-permute-start | bytes 1179656 | tf_op jit(solution)/shard_map/ppermute | solution.py:154
  161.2 7.8 %collective-permute-start.12 = (bf16[2,128,768]{2,1,0:T(8,128)(2,1)S(1)}, bf16[2,128,768]{2,1,0:T(8,128)(2,1)S(1)}, u32[]{:S(2)}, u32[]{:S(2)}) collective-permute-start(bf16[2,128,768]{2,1,0:T(8,128)(2,1)S(1)} %get-tuple-element.21), channel_id=1, source_target_pairs={{0,12},{1,13},{2,14},{3,15},{4,0},{5,1},{6,2},{7,3},{8,4},{9,5},{1... | collective-permute-start | bytes 1179656 | tf_op jit(solution)/shard_map/ppermute | solution.py:154
  169.0 9.0 %collective-permute-start.10 = (bf16[2,128,768]{2,1,0:T(8,128)(2,1)S(1)}, bf16[2,128,768]{2,1,0:T(8,128)(2,1)S(1)}, u32[]{:S(2)}, u32[]{:S(2)}) collective-permute-start(bf16[2,128,768]{2,1,0:T(8,128)(2,1)S(1)} %collective-permute-done.9), channel_id=1, source_target_pairs={{0,4},{1,5},{2,6},{3,7},{4,8},{5,9},{6,10},{7,11},{8,12},{9,13},{1... | collective-permute-start | bytes 1179656 | tf_op jit(solution)/shard_map/ppermute | solution.py:154
  169.0 9.0 %collective-permute-start.13 = (bf16[2,128,768]{2,1,0:T(8,128)(2,1)S(1)}, bf16[2,128,768]{2,1,0:T(8,128)(2,1)S(1)}, u32[]{:S(2)}, u32[]{:S(2)}) collective-permute-start(bf16[2,128,768]{2,1,0:T(8,128)(2,1)S(1)} %collective-permute-done.12), channel_id=1, source_target_pairs={{0,12},{1,13},{2,14},{3,15},{4,0},{5,1},{6,2},{7,3},{8,4},{9,5},{1... | collective-permute-start | bytes 1179656 | tf_op jit(solution)/shard_map/ppermute | solution.py:154
  178.0 10.1 %collective-permute-start.11 = (bf16[2,128,768]{2,1,0:T(8,128)(2,1)S(1)}, bf16[2,128,768]{2,1,0:T(8,128)(2,1)S(1)}, u32[]{:S(2)}, u32[]{:S(2)}) collective-permute-start(bf16[2,128,768]{2,1,0:T(8,128)(2,1)S(1)} %collective-permute-done.10), channel_id=1, source_target_pairs={{0,4},{1,5},{2,6},{3,7},{4,8},{5,9},{6,10},{7,11},{8,12},{9,13},{1... | collective-permute-start | bytes 1179656 | tf_op jit(solution)/shard_map/ppermute | solution.py:154
  178.0 10.2 %collective-permute-start.14 = (bf16[2,128,768]{2,1,0:T(8,128)(2,1)S(1)}, bf16[2,128,768]{2,1,0:T(8,128)(2,1)S(1)}, u32[]{:S(2)}, u32[]{:S(2)}) collective-permute-start(bf16[2,128,768]{2,1,0:T(8,128)(2,1)S(1)} %collective-permute-done.13), channel_id=1, source_target_pairs={{0,12},{1,13},{2,14},{3,15},{4,0},{5,1},{6,2},{7,3},{8,4},{9,5},{1... | collective-permute-start | bytes 1179656 | tf_op jit(solution)/shard_map/ppermute | solution.py:154
  190.5 33.9 %collective-permute-start.15 = (bf16[4,2,256,768]{3,2,1,0:T(8,128)(2,1)}, bf16[4,2,256,768]{3,2,1,0:T(8,128)(2,1)}, u32[]{:S(2)}, u32[]{:S(2)}) collective-permute-start(bf16[4,2,256,768]{3,2,1,0:T(8,128)(2,1)} %get-tuple-element.19), channel_id=1, source_target_pairs={{0,1},{1,0},{2,3},{3,2},{4,5},{5,4},{6,7},{7,6},{8,9},{9,8},{10,11... | collective-permute-start | bytes 9437192 | tf_op jit(solution)/shard_map/ppermute | solution.py:186
  208.0 39.3 %all-to-all-start.2 = ((bf16[2,16,16,2304]{3,2,0,1:T(8,128)(2,1)}), bf16[2,16,16,2304]{3,2,0,1:T(8,128)(2,1)}, u32[]{:S(2)}, u32[]{:S(2)}) async-start(bf16[2,16,16,2304]{3,2,0,1:T(8,128)(2,1)} %bitcast.110), calls=%async_computation.2 | async-start | bytes 4718592 | tf_op jit(solution)/shard_map/all_to_all | solution.py:29
  247.3 14.4 %all-to-all-start.1 = ((bf16[8,256,144]{1,2,0:T(8,128)(2,1)}), bf16[8,256,144]{1,2,0:T(8,128)(2,1)S(1)}, u32[]{:S(2)}, u32[]{:S(2)}) async-start(bf16[8,256,144]{1,2,0:T(8,128)(2,1)} %copy.85), calls=%async_computation.1 | async-start | bytes 1179648 | tf_op jit(solution)/shard_map/all_to_all | solution.py:99

commit v10 on v9

--- a/solution.py
+++ b/solution.py
@@ -25,10 +25,8 @@
     is_live = page_index < own_used
     masked_pages = jnp.where(
         is_live[None, :, None, None], prefill_cache, jnp.zeros((), prefill_cache.dtype)
-    )
-    received = lax.all_to_all(
-        masked_pages[:, inverse], "col", split_axis=1, concat_axis=1, tiled=True
-    )
+    )[:, inverse]
+    received = lax.all_to_all(masked_pages, "col", split_axis=1, concat_axis=1, tiled=True)
     senders = jnp.arange(col_devices, dtype=jnp.int32)[:, None]
     arrival = jnp.where(dest_table == own_index, senders * per_peer + dest_rank, slot_count)
     slot_of_arrival = (
@@ -223,7 +221,7 @@
     down_pad = jnp.zeros(
         (experts, padded_width - hidden_width, down_weight.shape[2]), down_weight.dtype
     )
-    per_token = down(route_ids, hidden_all, jnp.concatenate([down_weight, down_pad], axis=1), 256)
+    per_token = down(route_ids, hidden_all, jnp.concatenate([down_weight, down_pad], axis=1), 1024)
     mixed = sum_scatter_rows(per_token, "row").astype(jnp.bfloat16)
     return (mixed, decode_cache)
 

time: 264 us -> 263 us (level)
  transfers between devices with their start and end apart: 19 -> 19, of which waited for: 13 -> 13; matrix products, arithmetic and copies ran while one was open for 19% -> 19% of each run, Pallas kernels for 12% -> 11%
where the time goes in v10:
time: 263 us; the launch traced here: 262 us
  waiting for transfers between devices  93.3 us (35%)
  starting transfers between devices  50.9 us (19%)
  Pallas kernels  47.6 us (18%)
  local copies, waits for them, and re-layouts  42.5 us (16%)
  other arithmetic  27 us (10%)
    ppermute x6, waiting for transfers between devices, ring_reduce(): recv = lax.ppermute(cur, axis_name, perm)  48.2 us
    pallas_call x2, Pallas kernels, gate_up(): pl.pallas_call(gate_up_kernel, grid_spec=pltpu.PrefetchScalarGridSpec(num...  34.8 us
    ppermute x6, waiting for transfers between devices, ring_gather(): cur = lax.ppermute(cur, axis_name, perm)  18.3 us
    ppermute x1, waiting for transfers between devices, col_reduce_scatter(): lax.ppermute(pick(x_sum, 1 - zi).astype(other.dtype), axis_name, col_perm...  14.5 us
    pallas_call x1, Pallas kernels, down(): pl.pallas_call(down_kernel, grid=(token_count // tile,), in_specs=[pl.Blo...  12.8 us
    unnamed x26, local copies, waits for them, and re-layouts  11.3 us
    ppermute x6, starting transfers between devices, ring_reduce(): recv = lax.ppermute(cur, axis_name, perm)  10 us
    ppermute x6, starting transfers between devices, ring_gather(): cur = lax.ppermute(cur, axis_name, perm)  8.37 us
  transfers between devices with their start and end apart: 19, of which 13 were waited for; matrix products, arithmetic and copies ran while one was open for 19% of the time, Pallas kernels for 11%

profile of v10, /device:TPU:1, one launch (start us, length us, event | category | flops | bytes accessed | tf_op | source)
XLA Modules:
  0.0 262.5 jit_solution(33527253217660242)
XLA Ops:
  2.5 6.4 %all-to-all-start = ((bf16[8,256,144]{1,2,0:T(8,128)(2,1)}), bf16[8,256,144]{1,2,0:T(8,128)(2,1)S(1)}, u32[]{:S(2)}, u32[]{:S(2)}) async-start(bf16[8,256,144]{1,2,0:T(8,128)(2,1)} %broadcast_in_dim.68), calls=%async_computation | async-start | bytes 1179648 | tf_op jit(solution)/shard_map/all_to_all | solution.py:90
  10.3 6.3 %concatenate.12.w_ref = bf16[8,144,1536]{2,1,0:T(8,128)(2,1)} concatenate(bf16[8,144,720]{2,1,0:T(8,128)(2,1)S(1)} %copy-done.6, bf16[8,144,48]{2,1,0:T(8,128)(2,1)S(1)} %broadcast_in_dim.69, bf16[8,144,720]{2,1,0:T(8,128)(2,1)} %param.12, bf16[8,144,48]{2,1,0:T(8,128)(2,1)S(1)} %broadcast_in_dim.69), dimensions={2} | concatenate | bytes 7077888 | tf_op jit(solution)/shard_map/concatenate | solution.py:208
  16.6 3.2 %all-to-all-done = bf16[8,256,144]{1,2,0:T(8,128)(2,1)S(1)} async-done(((bf16[8,256,144]{1,2,0:T(8,128)(2,1)}), bf16[8,256,144]{1,2,0:T(8,128)(2,1)S(1)}, u32[]{:S(2)}, u32[]{:S(2)}) %all-to-all-start) | async-done | bytes 589856 | tf_op jit(solution)/shard_map/all_to_all | solution.py:90
  21.1 17.4 %shard_map.114 = bf16[2,1024,1536]{2,1,0:T(8,128)(2,1)} custom-call(s32[1]{0:T(128)} %bitcast.4.sel_ref, s32[2048,2]{1,0:T(8,128)} %copy.84.ids_ref, bf16[2048,144]{1,0:T(8,128)(2,1)} %bitcast.108, bf16[8,144,1536]{2,1,0:T(8,128)(2,1)} %concatenate.12.w_ref), custom_call_target="tpu_custom_call" | custom-call | tf_op jit(solution)/shard_map/pallas_call | solution.py:71
  39.3 17.4 %shard_map.113 = bf16[2,1024,1536]{2,1,0:T(8,128)(2,1)} custom-call(s32[1]{0:T(128)} %bitcast.1.sel_ref, s32[2048,2]{1,0:T(8,128)} %copy.84.ids_ref, bf16[2048,144]{1,0:T(8,128)(2,1)} %bitcast.109, bf16[8,144,1536]{2,1,0:T(8,128)(2,1)} %concatenate.12.w_ref), custom_call_target="tpu_custom_call" | custom-call | tf_op jit(solution)/shard_map/pallas_call | solution.py:71
  56.7 6.8 %fusion = bf16[4,2,2,128,1536]{4,3,2,1,0:T(8,128)(2,1)S(1)} fusion(bf16[4,2,2,128,1536]{4,3,2,1,0:T(8,128)(2,1)} %bitcast.106, bf16[4,2,2,128,1536]{4,3,2,1,0:T(8,128)(2,1)} %collective-permute-done), kind=kLoop, calls=%fused_computation.6 | loop fusion | flops 12582912 | bytes 18874368 | tf_op jit(solution)/shard_map/convert_element_type | solution.py:163
  63.4 2.9 %constant_dynamic-slice_fusion.3 = (bf16[1,2,2,128,1536]{4,3,2,1,0:T(8,128)(2,1)}, bf16[1,2,2,128,1536]{4,3,2,1,0:T(8,128)(2,1)}, bf16[1,2,2,128,1536]{4,3,2,1,0...) fusion(bf16[4,2,2,128,1536]{4,3,2,1,0:T(8,128)(2,1)S(1)} %fusio, ...), kind=kLoop, calls=%fused_computation.64 | loop fusion | bytes 25165856 | tf_op jit(solution)/shard_map/jit(dynamic_index_in_dim)/dynamic_slice | solution.py:127
  69.6 16.4 %collective-permute-done.4 = bf16[2,128,1536]{2,1,0:T(8,128)(2,1)S(1)} collective-permute-done((bf16[2,128,1536]{2,1,0:T(8,128)(2,1)S(1)}, bf16[2,128,1536]{2,1,0:T(8,128)(2,1)S(1)}, u32[]{:S(2)}, u32[]{:S(2)}) %collective-permute-start.4) | collective-permute-done | bytes 786464 | tf_op jit(solution)/shard_map/ppermute | solution.py:139
  86.2 3.5 %collective-permute-start.5 = (bf16[2,128,1536]{2,1,0:T(8,128)(2,1)S(1)}, bf16[2,128,1536]{2,1,0:T(8,128)(2,1)}, u32[]{:S(2)}, u32[]{:S(2)}) collective-permute-start(bf16[2,128,1536]{2,1,0:T(8,128)(2,1)S(1)} %fusion.7), channel_id=1, source_target_pairs={{0,12},{1,13},{2,14},{3,15},{4,0},{5,1},{6,2},{7,3},{8,4},{9,5},{1... | collective-permute-start | bytes 2359304 | tf_op jit(solution)/shard_map/ppermute | solution.py:139
  91.7 14.0 %collective-permute-done.5 = bf16[2,128,1536]{2,1,0:T(8,128)(2,1)} collective-permute-done((bf16[2,128,1536]{2,1,0:T(8,128)(2,1)S(1)}, bf16[2,128,1536]{2,1,0:T(8,128)(2,1)}, u32[]{:S(2)}, u32[]{:S(2)}) %collective-permute-start.5) | collective-permute-done | bytes 786464 | tf_op jit(solution)/shard_map/ppermute | solution.py:139
  107.1 3.6 %collective-permute-start.6 = (bf16[2,128,1536]{2,1,0:T(8,128)(2,1)S(1)}, bf16[2,128,1536]{2,1,0:T(8,128)(2,1)S(1)}, u32[]{:S(2)}, u32[]{:S(2)}) collective-permute-start(bf16[2,128,1536]{2,1,0:T(8,128)(2,1)S(1)} %fusion.6), channel_id=1, source_target_pairs={{0,12},{1,13},{2,14},{3,15},{4,0},{5,1},{6,2},{7,3},{8,4},{9,5},{1... | collective-permute-start | bytes 2359304 | tf_op jit(solution)/shard_map/ppermute | solution.py:139
  112.3 13.5 %collective-permute-done.6 = bf16[2,128,1536]{2,1,0:T(8,128)(2,1)S(1)} collective-permute-done((bf16[2,128,1536]{2,1,0:T(8,128)(2,1)S(1)}, bf16[2,128,1536]{2,1,0:T(8,128)(2,1)S(1)}, u32[]{:S(2)}, u32[]{:S(2)}) %collective-permute-start.6) | collective-permute-done | bytes 786464 | tf_op jit(solution)/shard_map/ppermute | solution.py:139
  126.1 4.3 %collective-permute-done.3 = bf16[2,128,1536]{2,1,0:T(8,128)(2,1)S(1)} collective-permute-done((bf16[2,128,1536]{2,1,0:T(8,128)(2,1)S(1)}, bf16[2,128,1536]{2,1,0:T(8,128)(2,1)S(1)}, u32[]{:S(2)}, u32[]{:S(2)}) %collective-permute-start.3) | collective-permute-done | bytes 786464 | tf_op jit(solution)/shard_map/ppermute | solution.py:139
  131.8 3.3 %collective-permute-start.7 = (bf16[256,1536]{1,0:T(8,128)(2,1)S(1)}, bf16[256,1536]{1,0:T(8,128)(2,1)}, u32[]{:S(2)}, u32[]{:S(2)}) collective-permute-start(bf16[256,1536]{1,0:T(8,128)(2,1)S(1)} %fusion.10), channel_id=1, source_target_pairs={{0,2},{1,3},{2,0},{3,1},{4,6},{5,7},{6,4},{7,5},{8,10},{9,11},{10,... | collective-permute-start | bytes 2359304 | tf_op jit(solution)/shard_map/ppermute | solution.py:169
  135.7 14.5 %collective-permute-done.7 = bf16[256,1536]{1,0:T(8,128)(2,1)} collective-permute-done((bf16[256,1536]{1,0:T(8,128)(2,1)S(1)}, bf16[256,1536]{1,0:T(8,128)(2,1)}, u32[]{:S(2)}, u32[]{:S(2)}) %collective-permute-start.7) | collective-permute-done | bytes 786464 | tf_op jit(solution)/shard_map/ppermute | solution.py:169
  152.1 2.8 %collective-permute-start.8 = (bf16[256,768]{1,0:T(8,128)(2,1)S(1)}, bf16[256,768]{1,0:T(8,128)(2,1)S(1)}, u32[]{:S(2)}, u32[]{:S(2)}) collective-permute-start(bf16[256,768]{1,0:T(8,128)(2,1)S(1)} %fusion.11), channel_id=1, source_target_pairs={{0,2},{1,3},{2,0},{3,1},{4,6},{5,7},{6,4},{7,5},{8,10},{9,11},{10,... | collective-permute-start | bytes 1179656 | tf_op jit(solution)/shard_map/ppermute | solution.py:178
  155.9 5.0 %collective-permute-done.8 = bf16[256,768]{1,0:T(8,128)(2,1)S(1)} collective-permute-done((bf16[256,768]{1,0:T(8,128)(2,1)S(1)}, bf16[256,768]{1,0:T(8,128)(2,1)S(1)}, u32[]{:S(2)}, u32[]{:S(2)}) %collective-permute-start.8) | collective-permute-done | bytes 393248 | tf_op jit(solution)/shard_map/ppermute | solution.py:178
  164.2 4.9 %collective-permute-done.9 = bf16[2,128,768]{2,1,0:T(8,128)(2,1)S(1)} collective-permute-done((bf16[2,128,768]{2,1,0:T(8,128)(2,1)S(1)}, bf16[2,128,768]{2,1,0:T(8,128)(2,1)S(1)}, u32[]{:S(2)}, u32[]{:S(2)}) %collective-permute-start.9) | collective-permute-done | bytes 393248 | tf_op jit(solution)/shard_map/ppermute | solution.py:152
  171.8 6.2 %collective-permute-done.10 = bf16[2,128,768]{2,1,0:T(8,128)(2,1)S(1)} collective-permute-done((bf16[2,128,768]{2,1,0:T(8,128)(2,1)S(1)}, bf16[2,128,768]{2,1,0:T(8,128)(2,1)S(1)}, u32[]{:S(2)}, u32[]{:S(2)}) %collective-permute-start.10) | collective-permute-done | bytes 393248 | tf_op jit(solution)/shard_map/ppermute | solution.py:152
  178.0 3.0 %collective-permute-start.14 = (bf16[2,128,768]{2,1,0:T(8,128)(2,1)S(1)}, bf16[2,128,768]{2,1,0:T(8,128)(2,1)S(1)}, u32[]{:S(2)}, u32[]{:S(2)}) collective-permute-start(bf16[2,128,768]{2,1,0:T(8,128)(2,1)S(1)} %collective-permute-done.13), channel_id=1, source_target_pairs={{0,12},{1,13},{2,14},{3,15},{4,0},{5,1},{6,2},{7,3},{8,4},{9,5},{1... | collective-permute-start | bytes 1179656 | tf_op jit(solution)/shard_map/ppermute | solution.py:152
  181.0 7.1 %collective-permute-done.11 = bf16[2,128,768]{2,1,0:T(8,128)(2,1)S(1)} collective-permute-done((bf16[2,128,768]{2,1,0:T(8,128)(2,1)S(1)}, bf16[2,128,768]{2,1,0:T(8,128)(2,1)S(1)}, u32[]{:S(2)}, u32[]{:S(2)}) %collective-permute-start.11) | collective-permute-done | bytes 393248 | tf_op jit(solution)/shard_map/ppermute | solution.py:152
  190.5 7.7 %collective-permute-start.15 = (bf16[4,2,256,768]{3,2,1,0:T(8,128)(2,1)}, bf16[4,2,256,768]{3,2,1,0:T(8,128)(2,1)}, u32[]{:S(2)}, u32[]{:S(2)}) collective-permute-start(bf16[4,2,256,768]{3,2,1,0:T(8,128)(2,1)} %get-tuple-element.19), channel_id=1, source_target_pairs={{0,1},{1,0},{2,3},{3,2},{4,5},{5,4},{6,7},{7,6},{8,9},{9,8},{10,11... | collective-permute-start | bytes 9437192 | tf_op jit(solution)/shard_map/ppermute | solution.py:184
  201.0 3.3 %broadcast_select_fusion = bf16[2,16,16,2304]{3,2,1,0:T(8,128)(2,1)} fusion(bf16[2,16,16,2304]{3,2,1,0:T(8,128)(2,1)} %param.16, pred[16]{0:T(512)(128)(4,1)S(1)} %iota_compare_fusion.1), kind=kLoop, calls=%fused_computation.13 | loop fusion | flops 1179648 | bytes 4718608 | tf_op jit(solution)/shard_map/jit(_where)/select_n | solution.py:26
  204.3 3.7 %gather_fusion = bf16[16,2,16,2304]{3,2,1,0:T(8,128)(2,1)} fusion(bf16[2,16,16,2304]{3,2,1,0:T(8,128)(2,1)} %broadcast_select_fusion, s32[1024]{0:T(1024)S(1)} %pad_clamp_fusion.1), kind=kCustom, calls=%fused_computation | custom fusion | bytes 4718656 | tf_op jit(solution)/shard_map/gather | solution.py:26
  208.0 8.1 %all-to-all-start.2 = ((bf16[2,16,16,2304]{3,2,0,1:T(8,128)(2,1)}), bf16[2,16,16,2304]{3,2,0,1:T(8,128)(2,1)}, u32[]{:S(2)}, u32[]{:S(2)}) async-start(bf16[2,16,16,2304]{3,2,0,1:T(8,128)(2,1)} %bitcast.110), calls=%async_computation.2 | async-start | bytes 4718592 | tf_op jit(solution)/shard_map/all_to_all | solution.py:29
  216.1 4.3 %copy.83 = bf16[8,720,144]{2,1,0:T(8,128)(2,1)} copy(bf16[8,720,144]{1,2,0:T(8,128)(2,1)} %param.13) | data formatting | bytes 3317760 | tf_op args[3]
  220.5 4.0 %concatenate.15.d_ref = bf16[8,768,144]{2,1,0:T(8,128)(2,1)} pad(bf16[8,720,144]{2,1,0:T(8,128)(2,1)} %copy.83, bf16[]{:T(256)} %constant.178.clone.1), padding=0_0x0_48x0_0 | pad | bytes 3428354 | tf_op jit(solution)/shard_map/concatenate | solution.py:224
  224.4 6.9 %maximum_select_fusion = bf16[4,2,2,256,768]{4,3,2,1,0:T(8,128)(2,1)} fusion(bf16[4,2,1,256,768]{4,3,2,1,0:T(8,128)(2,1)} %bitcast.35, bf16[4,2,1,256,768]{4,3,2,1,0:T(8,128)(2,1)S(1)} %get-tuple-element.18, pred[]{:T(512)S(6)} %eq.55), kind=kLoop, calls=%fused_computation.7 | loop fusion | flops 9437184 | bytes 12582913 | tf_op jit(solution)/shard_map/jit(_where)/select_n | solution.py:185
  231.3 12.8 %shard_map.115 = bf16[2048,144]{1,0:T(8,128)(2,1)} custom-call(s32[2048,2]{1,0:T(8,128)} %copy.84.ids_ref, bf16[2,2048,768]{2,1,0:T(8,128)(2,1)} %bitcast.107, bf16[8,768,144]{2,1,0:T(8,128)(2,1)} %concatenate.15.d_ref), custom_call_target="tpu_custom_call" | custom-call | tf_op jit(solution)/shard_map/pallas_call | solution.py:104
  247.3 3.5 %all-to-all-start.1 = ((bf16[8,256,144]{1,2,0:T(8,128)(2,1)}), bf16[8,256,144]{1,2,0:T(8,128)(2,1)S(1)}, u32[]{:S(2)}, u32[]{:S(2)}) async-start(bf16[8,256,144]{1,2,0:T(8,128)(2,1)} %copy.85), calls=%async_computation.1 | async-start | bytes 1179648 | tf_op jit(solution)/shard_map/all_to_all | solution.py:97
  255.5 3.2 %copy.89 = bf16[2,16,16,2304]{3,2,1,0:T(8,128)(2,1)} copy(bf16[2,16,16,2304]{3,2,0,1:T(8,128)(2,1)} %bitcast.111) | data formatting | bytes 4718592
  258.8 3.0 %all-to-all-done.1 = bf16[8,256,144]{1,2,0:T(8,128)(2,1)S(1)} async-done(((bf16[8,256,144]{1,2,0:T(8,128)(2,1)}), bf16[8,256,144]{1,2,0:T(8,128)(2,1)S(1)}, u32[]{:S(2)}, u32[]{:S(2)}) %all-to-all-start.1) | async-done | bytes 589856 | tf_op jit(solution)/shard_map/all_to_all | solution.py:97
  (102 shorter events, 38.4 us)
Async XLA Ops:
  0.6 154.4 %copy-start = (s32[1,16]{1,0:T(1,128)S(1)}, s32[1,16]{1,0:T(1,128)}, u32[]{:S(2)}) copy-start(s32[1,16]{1,0:T(1,128)} %param.19) | copy-start | bytes 196
  0.6 8.3 %copy-start.8 = (s32[2048,2]{0,1:T(2,128)S(1)}, s32[2048,2]{0,1:T(2,128)}, u32[]{:S(2)}) copy-start(s32[2048,2]{0,1:T(2,128)} %param.14) | copy-start | bytes 49156
  0.7 9.7 %copy-start.6 = (bf16[8,144,720]{2,1,0:T(8,128)(2,1)S(1)}, bf16[8,144,720]{2,1,0:T(8,128)(2,1)}, u32[]{:S(2)}) copy-start(bf16[8,144,720]{2,1,0:T(8,128)(2,1)} %param.11) | copy-start | bytes 4976644
  2.5 17.3 %all-to-all-start = ((bf16[8,256,144]{1,2,0:T(8,128)(2,1)}), bf16[8,256,144]{1,2,0:T(8,128)(2,1)S(1)}, u32[]{:S(2)}, u32[]{:S(2)}) async-start(bf16[8,256,144]{1,2,0:T(8,128)(2,1)} %broadcast_in_dim.68), calls=%async_computation | async-start | bytes 1179648 | tf_op jit(solution)/shard_map/all_to_all | solution.py:90
  38.5 18.2 %collective-permute-start = (bf16[4,2,2,128,1536]{4,3,2,1,0:T(8,128)(2,1)}, bf16[4,2,2,128,1536]{4,3,2,1,0:T(8,128)(2,1)}, u32[]{:S(2)}, u32[]{:S(2)}) collective-permute-start(bf16[4,2,2,128,1536]{4,3,2,1,0:T(8,128)(2,1)} %bitcast.112), channel_id=1, source_target_pairs={{0,1},{1,0},{2,3},{3,2},{4,5},{5,4},{6,7},{7,6},{8,9},{9,8},{10,11... | collective-permute-start | bytes 18874376 | tf_op jit(solution)/shard_map/ppermute | solution.py:162
  66.5 19.4 %collective-permute-start.4 = (bf16[2,128,1536]{2,1,0:T(8,128)(2,1)S(1)}, bf16[2,128,1536]{2,1,0:T(8,128)(2,1)S(1)}, u32[]{:S(2)}, u32[]{:S(2)}) collective-permute-start(bf16[2,128,1536]{2,1,0:T(8,128)(2,1)S(1)} %slice_bitcast_fusion.3), channel_id=1, source_target_pairs={{0,12},{1,13},{2,14},{3,15},{4,0},{5,1},{6,2},{7,3},{8,4},{9,5},{1... | collective-permute-start | bytes 2359304 | tf_op jit(solution)/shard_map/ppermute | solution.py:139
  69.3 20.4 %collective-permute-start.1 = (bf16[2,128,1536]{2,1,0:T(8,128)(2,1)S(1)}, bf16[2,128,1536]{2,1,0:T(8,128)(2,1)S(1)}, u32[]{:S(2)}, u32[]{:S(2)}) collective-permute-start(bf16[2,128,1536]{2,1,0:T(8,128)(2,1)S(1)} %slice_bitcast_fusion.7), channel_id=1, source_target_pairs={{0,4},{1,5},{2,6},{3,7},{4,8},{5,9},{6,10},{7,11},{8,12},{9,13},{1... | collective-permute-start | bytes 2359304 | tf_op jit(solution)/shard_map/ppermute | solution.py:139
  86.2 4.0 %copy-start.3 = (bf16[1,2,2,128,1536]{4,3,2,1,0:T(8,128)(2,1)S(1)}, bf16[1,2,2,128,1536]{4,3,2,1,0:T(8,128)(2,1)}, u32[]{:S(2)}) copy-start(bf16[1,2,2,128,1536]{4,3,2,1,0:T(8,128)(2,1)} %get-tuple-element.11) | copy-start | bytes 4718596
  86.2 19.5 %collective-permute-start.5 = (bf16[2,128,1536]{2,1,0:T(8,128)(2,1)S(1)}, bf16[2,128,1536]{2,1,0:T(8,128)(2,1)}, u32[]{:S(2)}, u32[]{:S(2)}) collective-permute-start(bf16[2,128,1536]{2,1,0:T(8,128)(2,1)S(1)} %fusion.7), channel_id=1, source_target_pairs={{0,12},{1,13},{2,14},{3,15},{4,0},{5,1},{6,2},{7,3},{8,4},{9,5},{1... | collective-permute-start | bytes 2359304 | tf_op jit(solution)/shard_map/ppermute | solution.py:139
  89.8 20.9 %collective-permute-start.2 = (bf16[2,128,1536]{2,1,0:T(8,128)(2,1)S(1)}, bf16[2,128,1536]{2,1,0:T(8,128)(2,1)}, u32[]{:S(2)}, u32[]{:S(2)}) collective-permute-start(bf16[2,128,1536]{2,1,0:T(8,128)(2,1)S(1)} %fusion.9), channel_id=1, source_target_pairs={{0,4},{1,5},{2,6},{3,7},{4,8},{5,9},{6,10},{7,11},{8,12},{9,13},{1... | collective-permute-start | bytes 2359304 | tf_op jit(solution)/shard_map/ppermute | solution.py:139
  90.2 1.4 copy-start.2
  105.7 6.4 %copy-start.5 = (bf16[1,2,2,128,1536]{4,3,2,1,0:T(8,128)(2,1)S(1)}, bf16[1,2,2,128,1536]{4,3,2,1,0:T(8,128)(2,1)}, u32[]{:S(2)}) copy-start(bf16[1,2,2,128,1536]{4,3,2,1,0:T(8,128)(2,1)} %get-tuple-element.14) | copy-start | bytes 4718596
  107.1 5.0 %copy-start.4 = (bf16[1,2,2,128,1536]{4,3,2,1,0:T(8,128)(2,1)S(1)}, bf16[1,2,2,128,1536]{4,3,2,1,0:T(8,128)(2,1)}, u32[]{:S(2)}) copy-start(bf16[1,2,2,128,1536]{4,3,2,1,0:T(8,128)(2,1)} %get-tuple-element.10) | copy-start | bytes 4718596
  107.1 18.7 %collective-permute-start.6 = (bf16[2,128,1536]{2,1,0:T(8,128)(2,1)S(1)}, bf16[2,128,1536]{2,1,0:T(8,128)(2,1)S(1)}, u32[]{:S(2)}, u32[]{:S(2)}) collective-permute-start(bf16[2,128,1536]{2,1,0:T(8,128)(2,1)S(1)} %fusion.6), channel_id=1, source_target_pairs={{0,12},{1,13},{2,14},{3,15},{4,0},{5,1},{6,2},{7,3},{8,4},{9,5},{1... | collective-permute-start | bytes 2359304 | tf_op jit(solution)/shard_map/ppermute | solution.py:139
  112.0 18.4 %collective-permute-start.3 = (bf16[2,128,1536]{2,1,0:T(8,128)(2,1)S(1)}, bf16[2,128,1536]{2,1,0:T(8,128)(2,1)S(1)}, u32[]{:S(2)}, u32[]{:S(2)}) collective-permute-start(bf16[2,128,1536]{2,1,0:T(8,128)(2,1)S(1)} %fusion.8), channel_id=1, source_target_pairs={{0,4},{1,5},{2,6},{3,7},{4,8},{5,9},{6,10},{7,11},{8,12},{9,13},{1... | collective-permute-start | bytes 2359304 | tf_op jit(solution)/shard_map/ppermute | solution.py:139
  130.6 1.1 copy-start.1
  130.6 4.4 %copy-start.9 = (f32[2048,2]{0,1:T(2,128)S(1)}, f32[2048,2]{0,1:T(2,128)}, u32[]{:S(2)}) copy-start(f32[2048,2]{0,1:T(2,128)} %param.15) | copy-start | bytes 49156
  130.6 4.4 %copy-start.7 = (s32[1,16,16]{2,1,0:T(8,128)S(1)}, s32[1,16,16]{2,1,0:T(8,128)}, u32[]{:S(2)}) copy-start(s32[1,16,16]{2,1,0:T(8,128)} %param.17) | copy-start | bytes 3076
  131.8 18.5 %collective-permute-start.7 = (bf16[256,1536]{1,0:T(8,128)(2,1)S(1)}, bf16[256,1536]{1,0:T(8,128)(2,1)}, u32[]{:S(2)}, u32[]{:S(2)}) collective-permute-start(bf16[256,1536]{1,0:T(8,128)(2,1)S(1)} %fusion.10), channel_id=1, source_target_pairs={{0,2},{1,3},{2,0},{3,1},{4,6},{5,7},{6,4},{7,5},{8,10},{9,11},{10,... | collective-permute-start | bytes 2359304 | tf_op jit(solution)/shard_map/ppermute | solution.py:169
  151.8 3.1 %copy-start.10 = (s32[1,16,16]{2,1,0:T(8,128)S(1)}, s32[1,16,16]{2,1,0:T(8,128)}, u32[]{:S(2)}) copy-start(s32[1,16,16]{2,1,0:T(8,128)} %param.18) | copy-start | bytes 3076
  152.1 8.8 %collective-permute-start.8 = (bf16[256,768]{1,0:T(8,128)(2,1)S(1)}, bf16[256,768]{1,0:T(8,128)(2,1)S(1)}, u32[]{:S(2)}, u32[]{:S(2)}) collective-permute-start(bf16[256,768]{1,0:T(8,128)(2,1)S(1)} %fusion.11), channel_id=1, source_target_pairs={{0,2},{1,3},{2,0},{3,1},{4,6},{5,7},{6,4},{7,5},{8,10},{9,11},{10,... | collective-permute-start | bytes 1179656 | tf_op jit(solution)/shard_map/ppermute | solution.py:178
  161.1 7.9 %collective-permute-start.9 = (bf16[2,128,768]{2,1,0:T(8,128)(2,1)S(1)}, bf16[2,128,768]{2,1,0:T(8,128)(2,1)S(1)}, u32[]{:S(2)}, u32[]{:S(2)}) collective-permute-start(bf16[2,128,768]{2,1,0:T(8,128)(2,1)S(1)} %get-tuple-element.20), channel_id=1, source_target_pairs={{0,4},{1,5},{2,6},{3,7},{4,8},{5,9},{6,10},{7,11},{8,12},{9,13},{1... | collective-permute-start | bytes 1179656 | tf_op jit(solution)/shard_map/ppermute | solution.py:152
  161.2 7.8 %collective-permute-start.12 = (bf16[2,128,768]{2,1,0:T(8,128)(2,1)S(1)}, bf16[2,128,768]{2,1,0:T(8,128)(2,1)S(1)}, u32[]{:S(2)}, u32[]{:S(2)}) collective-permute-start(bf16[2,128,768]{2,1,0:T(8,128)(2,1)S(1)} %get-tuple-element.21), channel_id=1, source_target_pairs={{0,12},{1,13},{2,14},{3,15},{4,0},{5,1},{6,2},{7,3},{8,4},{9,5},{1... | collective-permute-start | bytes 1179656 | tf_op jit(solution)/shard_map/ppermute | solution.py:152
  169.0 9.0 %collective-permute-start.10 = (bf16[2,128,768]{2,1,0:T(8,128)(2,1)S(1)}, bf16[2,128,768]{2,1,0:T(8,128)(2,1)S(1)}, u32[]{:S(2)}, u32[]{:S(2)}) collective-permute-start(bf16[2,128,768]{2,1,0:T(8,128)(2,1)S(1)} %collective-permute-done.9), channel_id=1, source_target_pairs={{0,4},{1,5},{2,6},{3,7},{4,8},{5,9},{6,10},{7,11},{8,12},{9,13},{1... | collective-permute-start | bytes 1179656 | tf_op jit(solution)/shard_map/ppermute | solution.py:152
  169.0 9.0 %collective-permute-start.13 = (bf16[2,128,768]{2,1,0:T(8,128)(2,1)S(1)}, bf16[2,128,768]{2,1,0:T(8,128)(2,1)S(1)}, u32[]{:S(2)}, u32[]{:S(2)}) collective-permute-start(bf16[2,128,768]{2,1,0:T(8,128)(2,1)S(1)} %collective-permute-done.12), channel_id=1, source_target_pairs={{0,12},{1,13},{2,14},{3,15},{4,0},{5,1},{6,2},{7,3},{8,4},{9,5},{1... | collective-permute-start | bytes 1179656 | tf_op jit(solution)/shard_map/ppermute | solution.py:152
  178.0 10.1 %collective-permute-start.11 = (bf16[2,128,768]{2,1,0:T(8,128)(2,1)S(1)}, bf16[2,128,768]{2,1,0:T(8,128)(2,1)S(1)}, u32[]{:S(2)}, u32[]{:S(2)}) collective-permute-start(bf16[2,128,768]{2,1,0:T(8,128)(2,1)S(1)} %collective-permute-done.10), channel_id=1, source_target_pairs={{0,4},{1,5},{2,6},{3,7},{4,8},{5,9},{6,10},{7,11},{8,12},{9,13},{1... | collective-permute-start | bytes 1179656 | tf_op jit(solution)/shard_map/ppermute | solution.py:152
  178.0 10.2 %collective-permute-start.14 = (bf16[2,128,768]{2,1,0:T(8,128)(2,1)S(1)}, bf16[2,128,768]{2,1,0:T(8,128)(2,1)S(1)}, u32[]{:S(2)}, u32[]{:S(2)}) collective-permute-start(bf16[2,128,768]{2,1,0:T(8,128)(2,1)S(1)} %collective-permute-done.13), channel_id=1, source_target_pairs={{0,12},{1,13},{2,14},{3,15},{4,0},{5,1},{6,2},{7,3},{8,4},{9,5},{1... | collective-permute-start | bytes 1179656 | tf_op jit(solution)/shard_map/ppermute | solution.py:152
  190.5 33.9 %collective-permute-start.15 = (bf16[4,2,256,768]{3,2,1,0:T(8,128)(2,1)}, bf16[4,2,256,768]{3,2,1,0:T(8,128)(2,1)}, u32[]{:S(2)}, u32[]{:S(2)}) collective-permute-start(bf16[4,2,256,768]{3,2,1,0:T(8,128)(2,1)} %get-tuple-element.19), channel_id=1, source_target_pairs={{0,1},{1,0},{2,3},{3,2},{4,5},{5,4},{6,7},{7,6},{8,9},{9,8},{10,11... | collective-permute-start | bytes 9437192 | tf_op jit(solution)/shard_map/ppermute | solution.py:184
  208.0 39.3 %all-to-all-start.2 = ((bf16[2,16,16,2304]{3,2,0,1:T(8,128)(2,1)}), bf16[2,16,16,2304]{3,2,0,1:T(8,128)(2,1)}, u32[]{:S(2)}, u32[]{:S(2)}) async-start(bf16[2,16,16,2304]{3,2,0,1:T(8,128)(2,1)} %bitcast.110), calls=%async_computation.2 | async-start | bytes 4718592 | tf_op jit(solution)/shard_map/all_to_all | solution.py:29
  247.3 14.4 %all-to-all-start.1 = ((bf16[8,256,144]{1,2,0:T(8,128)(2,1)}), bf16[8,256,144]{1,2,0:T(8,128)(2,1)S(1)}, u32[]{:S(2)}, u32[]{:S(2)}) async-start(bf16[8,256,144]{1,2,0:T(8,128)(2,1)} %copy.85), calls=%async_computation.1 | async-start | bytes 1179648 | tf_op jit(solution)/shard_map/all_to_all | solution.py:97
